TPU v7x, 128 devices: a whole 4x4x4 slice. The times are simulated.
128 devices in a mesh: ep: 64 (over z, y, x), dp: 2 (over core).
Axes of the slice: x: 4, y: 4, z: 4, core: 2. Of those that a mesh axis runs over, the one named last changes fastest.
Arguments:
- attention_out: bfloat16 [8192, 2560], P(('ep', 'dp')), may hold values from -6 to 6
- residual: bfloat16 [8192, 2560], P(('ep', 'dp')), may hold values from -30 to 30
- out_weight: bfloat16 [2560, 2560], P(None, 'dp'), may hold values from -0.125 to 0.125
- pre_gain: float32 [2560], replicated, may hold values from 0.5 to 1.5
- routes: int32 [8192, 6], P(('ep', 'dp')), may hold values from 0 to 63, all different within a row; in each aligned block of 64 rows (0 to 63, 64 to 127, ...) at most 9 rows name the same one
- gate_prob: float32 [8192, 6], P(('ep', 'dp')), may hold values from 0.05 to 1
- gate_weight: bfloat16 [64, 2560, 1536], P('ep', None, 'dp'), may hold values from -0.125 to 0.125
- up_weight: bfloat16 [64, 2560, 1536], P('ep', None, 'dp'), may hold values from -0.125 to 0.125
- down_weight: bfloat16 [64, 1536, 2560], P('ep', None, 'dp'), may hold values from -0.15625 to 0.15625
- post_gain: float32 [2560], replicated, may hold values from 0.5 to 1.5
Outputs:
- new_state: bfloat16 [8192, 2560], P(('ep', 'dp'))
- normed_state: bfloat16 [8192, 2560], P(('ep', 'dp'))
Inputs may be any that keep to these rules, and one draw needn't show every extreme that they name: `routes`: each row names 6 different experts; within the 64 rows of one device no expert is named more than 9 times, a bound that some block reaches.
All inputs are finite; a program needn't handle non-finite values.
Results may differ from a plain program's by a relative error of at most 0.015.
Values may be sent and summed in bfloat16 or wider, within the bound.
No kernel may reach another device: no remote copies, remote signals or barrier semaphores. Data moves between devices by JAX's collectives and lax.ppermute only.
A program may use at most 128 MiB of HBM per device.

v0:
```python
import jax
import jax.numpy as jnp
from jax import lax
from jax.sharding import PartitionSpec as P


def rms_scale(values, gain):
    widened = values.astype(jnp.float32)
    meansq = jnp.mean(widened * widened, axis=-1, keepdims=True)
    return widened * lax.rsqrt(meansq + 1e-06) * gain


def slot_table(route_block, experts, capacity):
    flat_ids = route_block.reshape(-1)
    onehot = (flat_ids[:, None] == jnp.arange(experts, dtype=jnp.int32)[None, :]).astype(jnp.int32)
    before = jnp.cumsum(onehot, axis=0) - onehot
    rank_in = jnp.sum(before * onehot, axis=1)
    return (flat_ids * capacity + rank_in).reshape(route_block.shape)


def per_device(
    attention_out,
    residual,
    out_weight,
    pre_gain,
    routes,
    gate_prob,
    gate_weight,
    up_weight,
    down_weight,
    post_gain,
):
    groups = lax.axis_size("dp")
    experts = lax.axis_size("ep")
    tok_rows, top_picks = routes.shape
    row_width = residual.shape[1]
    part_cols = out_weight.shape[1]
    capacity = max(2, 3 * tok_rows * top_picks // (2 * experts))
    columns = jnp.dot(
        lax.all_gather(attention_out, "dp", axis=0, tiled=True),
        out_weight,
        preferred_element_type=jnp.float32,
    )
    home_cols = lax.all_to_all(
        columns.reshape(groups, tok_rows, part_cols).astype(jnp.bfloat16),
        "dp",
        split_axis=0,
        concat_axis=2,
        tiled=True,
    ).astype(jnp.float32)
    summed = (residual.astype(jnp.float32) + home_cols.reshape(tok_rows, row_width)).astype(
        jnp.bfloat16
    )
    normed_in = rms_scale(summed, pre_gain).astype(jnp.bfloat16)
    slot_ids = slot_table(routes, experts, capacity)
    matches = (
        slot_ids[:, :, None] == jnp.arange(experts * capacity, dtype=jnp.int32)[None, None, :]
    ).astype(jnp.float32)
    placing = jnp.sum(matches, axis=1).astype(jnp.bfloat16)
    weights = gate_prob / jnp.sum(gate_prob, axis=1, keepdims=True)
    mixing = jnp.sum(weights[:, :, None] * matches, axis=1)
    outgoing = lax.dot_general(
        placing, normed_in, (((0,), (0,)), ((), ())), preferred_element_type=jnp.float32
    ).astype(jnp.bfloat16)
    gate_local = gate_weight[0]
    up_local = up_weight[0]
    down_local = down_weight[0]
    arrived = lax.all_to_all(
        outgoing.reshape(experts, capacity, row_width),
        "ep",
        split_axis=0,
        concat_axis=0,
        tiled=True,
    )
    segment = lax.all_gather(arrived.reshape(-1, row_width), "dp", axis=0, tiled=True)
    gate_part = jnp.dot(segment, gate_local, preferred_element_type=jnp.float32)
    up_part = jnp.dot(segment, up_local, preferred_element_type=jnp.float32)
    hidden = (jax.nn.silu(gate_part) * up_part).astype(jnp.bfloat16)
    results = jnp.dot(
        lax.all_gather(hidden, "dp", axis=1, tiled=True),
        down_local,
        preferred_element_type=jnp.float32,
    ).astype(jnp.bfloat16)
    joined = lax.all_to_all(
        results.reshape(groups, experts * capacity, part_cols),
        "dp",
        split_axis=0,
        concat_axis=2,
        tiled=True,
    )
    returned_rows = lax.all_to_all(
        joined.reshape(experts, capacity, row_width), "ep", split_axis=0, concat_axis=0, tiled=True
    )
    returned = returned_rows.reshape(experts * capacity, row_width).astype(jnp.float32)
    expert_sum = jnp.dot(
        mixing, returned, precision=lax.Precision.HIGHEST, preferred_element_type=jnp.float32
    )
    new_state = (summed.astype(jnp.float32) + expert_sum).astype(jnp.bfloat16)
    normed_state = rms_scale(new_state, post_gain).astype(jnp.bfloat16)
    return (new_state, normed_state)


def solution(mesh):
    return jax.shard_map(
        per_device,
        mesh=mesh,
        in_specs=(
            P(("ep", "dp"), None),
            P(("ep", "dp"), None),
            P(None, "dp"),
            P(),
            P(("ep", "dp"), None),
            P(("ep", "dp"), None),
            P("ep", None, "dp"),
            P("ep", None, "dp"),
            P("ep", None, "dp"),
            P(),
        ),
        out_specs=(P(("ep", "dp"), None), P(("ep", "dp"), None)),
        check_vma=False,
    )
```

profile of v0, /device:TPU:0, one launch (start us, length us, event | category | flops | bytes accessed | tf_op | source)
XLA Modules:
  0.0 261.9 jit_solution(15246952357685593123)
XLA Ops:
  7.2 2.5 all_gather.9
  9.7 4.6 %convolution_convert_fusion.2 = bf16[128,1280]{1,0:T(8,128)(2,1)} fusion(bf16[128,2560]{1,0:T(8,128)(2,1)S(1)} %all_gather.9, bf16[2560,1280]{1,0:T(8,128)(2,1)} %param.12), kind=kOutput, calls=%fused_computation.10 | convolution fusion | flops 839024640 | bytes 7536640 | tf_op jit(solution)/shard_map/dot_general | solution.py:39
  14.3 3.6 %all-to-all-start = ((bf16[2,64,1280]{2,1,0:T(8,128)(2,1)}), bf16[2,64,1280]{2,1,0:T(8,128)(2,1)S(1)}, u32[]{:S(2)}, u32[]{:S(2)}) async-start(bf16[2,64,1280]{2,1,0:T(8,128)(2,1)} %bitcast), calls=%async_computation | async-start | bytes 655360 | tf_op jit(solution)/shard_map/all_to_all | solution.py:44
  17.9 0.1 copy.40
  18.0 0.1 eq.42
  18.2 0.1 eq.38
  18.4 0.9 reduce-window.6
  19.3 0.2 slice_reduce_fusion
  19.6 0.1 fusion.19
  19.7 0.1 reduce_sum.57
  19.8 0.1 copy.43
  19.9 0.1 convert_bitcast_fusion
  20.0 0.5 copy.39
  20.5 0.2 fusion.11
  20.8 0.3 convert_reduce_fusion
  21.0 1.0 convolution_convert_fusion.1
  22.0 3.3 %reshape.76 = bf16[64,9,2560]{2,1,0:T(8,128)(2,1)} reshape(bf16[576,2560]{1,0:T(8,128)(2,1)S(1)} %convolution_convert_fusion.1) | data formatting | bytes 5898240 | tf_op jit(solution)/shard_map/reshape | solution.py:69
  25.3 76.1 %all_to_all.34 = bf16[64,9,2560]{2,1,0:T(8,128)(2,1)} all-to-all(bf16[64,9,2560]{2,1,0:T(8,128)(2,1)} %reshape.76), channel_id=1, replica_groups=mesh['ep'=64,'dp'=2] {'ep'}, dimensions={0} | all-to-all | bytes 5898240 | tf_op jit(solution)/shard_map/all_to_all | solution.py:68
  101.4 5.2 %reshape.77 = bf16[576,2560]{1,0:T(8,128)(2,1)} reshape(bf16[64,9,2560]{2,1,0:T(8,128)(2,1)} %all_to_all.34) | data formatting | bytes 5898240 | tf_op jit(solution)/shard_map/reshape | solution.py:75
  106.7 0.2 all-gather.5.cloned.1.call-start
  106.9 14.9 %all-gather.3.cloned.1.call-done = bf16[1152,2560]{1,0:T(8,128)(2,1)} async-done(((bf16[576,2560]{1,0:T(8,128)(2,1)}), bf16[1152,2560]{1,0:T(8,128)(2,1)}) %all-gather.3.cloned.1.call-update) | async-done | bytes 5898256 | tf_op jit(solution)/shard_map/all_gather | solution.py:75
  121.8 8.1 %fusion.2 = f32[1152,768]{1,0:T(8,128)S(1)} fusion(bf16[1152,2560]{1,0:T(8,128)(2,1)} %all-gather.3.cloned.1.call-done, bf16[1,2560,768]{2,1,0:T(8,128)(2,1)} %param.16), kind=kOutput, calls=%fused_computation.5 | convolution fusion | flops 4529848320 | bytes 13369344 | tf_op jit(solution)/shard_map/dot_general | solution.py:76
  129.9 6.1 %fusion.5 = bf16[1152,768]{1,0:T(8,128)(2,1)} fusion(bf16[1152,2560]{1,0:T(8,128)(2,1)S(1)} %copy-done.6, bf16[1,2560,768]{2,1,0:T(8,128)(2,1)S(1)} %copy-done.7, f32[1152,768]{1,0:T(8,128)S(1)} %fusion.2), kind=kOutput, calls=%fused_computation.9 | convolution fusion | flops 4535156736 | bytes 15138816 | tf_op jit(solution)/shard_map/dot_general | solution.py:77
  136.0 16.9 %all-gather.5.cloned.1.call-done = bf16[1152,1536]{1,0:T(8,128)(2,1)} async-done(((bf16[1152,768]{1,0:T(8,128)(2,1)}), bf16[1152,1536]{1,0:T(8,128)(2,1)}) %all-gather.5.cloned.1.call-update) | async-done | bytes 3538960 | tf_op jit(solution)/shard_map/all_gather | solution.py:80
  152.9 7.9 %convolution_convert_fusion = bf16[1152,1280]{1,0:T(8,128)(2,1)S(1)} fusion(bf16[1152,1536]{1,0:T(8,128)(2,1)} %all-gather.5.cloned.1.call-done, bf16[1,1536,1280]{2,1,0:T(8,128)(2,1)} %param.18), kind=kOutput, calls=%fused_computation | convolution fusion | flops 4531322880 | bytes 10420224 | tf_op jit(solution)/shard_map/dot_general | solution.py:79
  160.9 6.1 %all_to_all.35 = bf16[2,576,1280]{2,1,0:T(8,128)(2,1)S(1)} all-to-all(bf16[2,576,1280]{2,1,0:T(8,128)(2,1)S(1)} %bitcast.53), channel_id=1, replica_groups=mesh['ep'=64,'dp'=2] {'dp'}, dimensions={0} | all-to-all | bytes 5898240 | tf_op jit(solution)/shard_map/all_to_all | solution.py:84
  167.0 3.0 %copy.44 = bf16[1,576,2,1280]{3,2,1,0:T(2,128)(2,1)S(1)} copy(bf16[1,576,2,1280]{3,1,2,0:T(8,128)(2,1)S(1)} %bitcast.52) | data formatting | bytes 5898240 | tf_op jit(solution)/shard_map/all_to_all | solution.py:84
  170.0 3.8 %reshape.79 = bf16[64,9,2560]{2,1,0:T(8,128)(2,1)} reshape(bf16[1,576,2,1280]{3,2,1,0:T(2,128)(2,1)S(1)} %copy.44) | data formatting | bytes 5898240 | tf_op jit(solution)/shard_map/reshape | solution.py:92
  173.8 74.7 %all_to_all.36 = bf16[64,9,2560]{2,1,0:T(8,128)(2,1)} all-to-all(bf16[64,9,2560]{2,1,0:T(8,128)(2,1)} %reshape.79), channel_id=1, replica_groups=mesh['ep'=64,'dp'=2] {'ep'}, dimensions={0} | all-to-all | bytes 5898240 | tf_op jit(solution)/shard_map/all_to_all | solution.py:91
  248.5 3.8 %reshape.80 = bf16[576,2560]{1,0:T(8,128)(2,1)S(1)} reshape(bf16[64,9,2560]{2,1,0:T(8,128)(2,1)} %all_to_all.36) | data formatting | bytes 5898240 | tf_op jit(solution)/shard_map/reshape | solution.py:94
  252.3 1.8 fusion.8
  254.1 0.9 fusion.10
  (28 shorter events, 0.3 us)
Async XLA Ops:
  9.7 8.3 %copy-start.2 = (s32[64,6]{0,1:T(8,128)S(1)}, s32[64,6]{0,1:T(8,128)}, u32[]{:S(2)}) copy-start(s32[64,6]{0,1:T(8,128)} %param.14) | copy-start | bytes 4612
  9.7 8.7 %copy-start.3 = (f32[64,6]{0,1:T(8,128)S(1)}, f32[64,6]{0,1:T(8,128)}, u32[]{:S(2)}) copy-start(f32[64,6]{0,1:T(8,128)} %param.15) | copy-start | bytes 4612
  14.3 6.2 %copy-start.1 = (bf16[64,2560]{1,0:T(8,128)(2,1)S(1)}, bf16[64,2560]{1,0:T(8,128)(2,1)}, u32[]{:S(2)}) copy-start(bf16[64,2560]{1,0:T(8,128)(2,1)} %param.11) | copy-start | bytes 983044
  14.3 6.7 %copy-start.4 = (f32[2560]{0:T(1024)S(1)}, f32[2560]{0:T(1024)}, u32[]{:S(2)}) copy-start(f32[2560]{0:T(1024)} %param.13) | copy-start | bytes 30724
  14.3 5.6 %all-to-all-start = ((bf16[2,64,1280]{2,1,0:T(8,128)(2,1)}), bf16[2,64,1280]{2,1,0:T(8,128)(2,1)S(1)}, u32[]{:S(2)}, u32[]{:S(2)}) async-start(bf16[2,64,1280]{2,1,0:T(8,128)(2,1)} %bitcast), calls=%async_computation | async-start | bytes 655360 | tf_op jit(solution)/shard_map/all_to_all | solution.py:44
  17.9 103.9 %all-gather.3.cloned.1.call-start = ((), (), s32[]{:S(2)}) async-start(), calls=%async_computation.4 | async-start | bytes 8847360 | tf_op jit(solution)/shard_map/all_gather | solution.py:75
  106.7 46.2 %all-gather.5.cloned.1.call-start = ((), (), s32[]{:S(2)}) async-start(), calls=%async_computation.5 | async-start | bytes 5308416 | tf_op jit(solution)/shard_map/all_gather | solution.py:80
  121.8 8.1 %copy-start.6 = (bf16[1152,2560]{1,0:T(8,128)(2,1)S(1)}, bf16[1152,2560]{1,0:T(8,128)(2,1)}, u32[]{:S(2)}) copy-start(bf16[1152,2560]{1,0:T(8,128)(2,1)} %all-gather.3.cloned.1.call-done) | copy-start | bytes 17694724
  121.8 8.1 %copy-start.7 = (bf16[1,2560,768]{2,1,0:T(8,128)(2,1)S(1)}, bf16[1,2560,768]{2,1,0:T(8,128)(2,1)}, u32[]{:S(2)}) copy-start(bf16[1,2560,768]{2,1,0:T(8,128)(2,1)} %param.17) | copy-start | bytes 11796484
  248.5 5.7 %copy-start.5 = (f32[2560]{0:T(1024)S(1)}, f32[2560]{0:T(1024)}, u32[]{:S(2)}) copy-start(f32[2560]{0:T(1024)} %param.19) | copy-start | bytes 30724
  254.1 0.9 copy-start
Sparse Core Ops, SparseCore 0:
  106.8 14.9 all-gather.2
  136.1 16.7 all-gather.4
where the time goes:
time: 262 us
  blocking collectives  159 us (61%)
  waiting for transfers between devices  31.8 us (12%)
  matrix products  29.6 us (11%)
  local copies, waits for them, and re-layouts  20.5 us (8%)
  between operations  14.2 us (5%)
  starting transfers between devices  3.85 us (1%)
    all_to_all x1, blocking collectives, per_device(): lax.all_to_all(outgoing.reshape(experts, capacity, row_width), 'ep', spli...  76.1 us
    all_to_all x1, blocking collectives, per_device(): lax.all_to_all(joined.reshape(experts, capacity, row_width), 'ep', split_...  74.7 us
    all_gather x1, waiting for transfers between devices, per_device(): lax.all_gather(hidden, 'dp', axis=1, tiled=True)  16.9 us
    all_gather x1, waiting for transfers between devices, per_device(): lax.all_gather(arrived.reshape(-1, row_width), 'dp', axis=0, tiled=True)  14.9 us
    dot_general x1, matrix products, per_device(): gate_part = jnp.dot(segment, gate_local, preferred_element_type=jnp.float32)  8.07 us
    dot_general x1, matrix products, per_device(): jnp.dot(lax.all_gather(hidden, 'dp', axis=1, tiled=True), down_local, pre...  7.94 us
    all_to_all x1, blocking collectives, per_device(): lax.all_to_all(results.reshape(groups, experts * capacity, part_cols), 'd...  6.1 us
    dot_general x1, matrix products, per_device(): up_part = jnp.dot(segment, up_local, preferred_element_type=jnp.float32)  6.08 us
  transfers between devices with their start and end apart: 3, of which 2 were waited for; matrix products, arithmetic and copies ran while one was open for 1% of the time, Pallas kernels for 0%

commit v1 on v0

--- a/solution.py
+++ b/solution.py
@@ -16,6 +16,14 @@
     before = jnp.cumsum(onehot, axis=0) - onehot
     rank_in = jnp.sum(before * onehot, axis=1)
     return (flat_ids * capacity + rank_in).reshape(route_block.shape)
+
+
+def exchange_rows(rows, experts):
+    total, width = rows.shape
+    lanes = 128
+    wire = rows.reshape(experts, total * width // (experts * lanes), lanes)
+    moved = lax.all_to_all(wire, "ep", split_axis=0, concat_axis=0, tiled=True)
+    return moved.reshape(total, width)
 
 
 def per_device(
@@ -65,14 +73,8 @@
     gate_local = gate_weight[0]
     up_local = up_weight[0]
     down_local = down_weight[0]
-    arrived = lax.all_to_all(
-        outgoing.reshape(experts, capacity, row_width),
-        "ep",
-        split_axis=0,
-        concat_axis=0,
-        tiled=True,
-    )
-    segment = lax.all_gather(arrived.reshape(-1, row_width), "dp", axis=0, tiled=True)
+    arrived = exchange_rows(outgoing, experts)
+    segment = lax.all_gather(arrived, "dp", axis=0, tiled=True)
     gate_part = jnp.dot(segment, gate_local, preferred_element_type=jnp.float32)
     up_part = jnp.dot(segment, up_local, preferred_element_type=jnp.float32)
     hidden = (jax.nn.silu(gate_part) * up_part).astype(jnp.bfloat16)
@@ -88,10 +90,9 @@
         concat_axis=2,
         tiled=True,
     )
-    returned_rows = lax.all_to_all(
-        joined.reshape(experts, capacity, row_width), "ep", split_axis=0, concat_axis=0, tiled=True
+    returned = exchange_rows(joined.reshape(experts * capacity, row_width), experts).astype(
+        jnp.float32
     )
-    returned = returned_rows.reshape(experts * capacity, row_width).astype(jnp.float32)
     expert_sum = jnp.dot(
         mixing, returned, precision=lax.Precision.HIGHEST, preferred_element_type=jnp.float32
     )

time: 262 us -> 223 us (0.85)
  blocking collectives: 159 us -> 111 us
  local copies, waits for them, and re-layouts: 20.5 us -> 28.2 us
    all_to_all x2, blocking collectives: 151 us -> 103 us  [exchange_rows(): moved = lax.all_to_all(wire, 'ep', split_axis=0, concat_axis=0, tiled=True)]
    another operation x0 -> x1, local copies, waits for them, and re-layouts: none -> 6.4 us  [exchange_rows(): wire = rows.reshape(experts, total * width // (experts * lanes), lanes)]
    reshape x4 -> x3, local copies, waits for them, and re-layouts: 16 us -> 15.8 us  [the longest x2 10.8 us: exchange_rows(): return moved.reshape(total, width)]
where the time goes in v1:
time: 223 us
  blocking collectives  111 us (50%)
  waiting for transfers between devices  31.6 us (14%)
  matrix products  31.2 us (14%)
  local copies, waits for them, and re-layouts  28.2 us (13%)
  between operations  14.2 us (6%)
  starting transfers between devices  3.85 us (2%)
  other arithmetic  2.51 us (1%)
    all_to_all x2, blocking collectives, exchange_rows(): moved = lax.all_to_all(wire, 'ep', split_axis=0, concat_axis=0, tiled=True)  103 us
    all_gather x1, waiting for transfers between devices, per_device(): lax.all_gather(hidden, 'dp', axis=1, tiled=True)  16.9 us
    all_gather x1, waiting for transfers between devices, per_device(): segment = lax.all_gather(arrived, 'dp', axis=0, tiled=True)  14.6 us
    reshape x2, local copies, waits for them, and re-layouts, exchange_rows(): return moved.reshape(total, width)  10.8 us
    dot_general x1, matrix products, per_device(): gate_part = jnp.dot(segment, gate_local, preferred_element_type=jnp.float32)  8.07 us
    dot_general x1, matrix products, per_device(): jnp.dot(lax.all_gather(hidden, 'dp', axis=1, tiled=True), down_local, pre...  7.94 us
    another operation x1, local copies, waits for them, and re-layouts, exchange_rows(): wire = rows.reshape(experts, total * width // (experts * lanes), lanes)  6.4 us
    all_to_all x1, blocking collectives, per_device(): lax.all_to_all(results.reshape(groups, experts * capacity, part_cols), 'd...  6.1 us
  transfers between devices with their start and end apart: 3, of which 2 were waited for; matrix products, arithmetic and copies ran while one was open for 1% of the time, Pallas kernels for 0%

profile of v1, /device:TPU:0, one launch (start us, length us, event | category | flops | bytes accessed | tf_op | source)
XLA Modules:
  0.0 222.7 jit_solution(9077040411435942727)
XLA Ops:
  7.2 2.5 %all_gather.9 = bf16[128,2560]{1,0:T(8,128)(2,1)S(1)} all-gather(bf16[64,2560]{1,0:T(8,128)(2,1)} %param.10), channel_id=1, replica_groups=mesh['ep'=64,'dp'=2] {'dp'}, dimensions={0}, use_global_device_ids=true | all-gather | bytes 983040 | tf_op jit(solution)/shard_map/all_gather | solution.py:48
  9.7 4.6 %convolution_convert_fusion.2 = bf16[128,1280]{1,0:T(8,128)(2,1)} fusion(bf16[128,2560]{1,0:T(8,128)(2,1)S(1)} %all_gather.9, bf16[2560,1280]{1,0:T(8,128)(2,1)} %param.12), kind=kOutput, calls=%fused_computation.10 | convolution fusion | flops 839024640 | bytes 7536640 | tf_op jit(solution)/shard_map/dot_general | solution.py:47
  14.3 3.6 %all-to-all-start = ((bf16[2,64,1280]{2,1,0:T(8,128)(2,1)}), bf16[2,64,1280]{2,1,0:T(8,128)(2,1)S(1)}, u32[]{:S(2)}, u32[]{:S(2)}) async-start(bf16[2,64,1280]{2,1,0:T(8,128)(2,1)} %bitcast), calls=%async_computation | async-start | bytes 655360 | tf_op jit(solution)/shard_map/all_to_all | solution.py:52
  17.9 0.1 copy.40
  18.0 0.1 eq.42
  18.2 0.1 eq.38
  18.4 0.9 reduce-window.6
  19.3 0.2 slice_reduce_fusion
  19.6 0.1 fusion.19
  19.7 0.1 reduce_sum.57
  19.8 0.1 copy.43
  19.9 0.1 convert_bitcast_fusion
  20.0 0.5 copy.39
  20.5 0.2 fusion.11
  20.8 0.3 convert_reduce_fusion
  21.0 2.6 %convolution_convert_fusion.1 = bf16[576,2560]{1,0:T(8,128)(2,1)} fusion(bf16[64,2560]{1,0:T(8,128)(2,1)S(1)} %get-tuple-element.5, f32[2560]{0:T(1024)S(1)} %copy-done.4, f32[64]{0:T(128)S(1)} %add_rsqrt_fusion.1, bf16[64,576]{1,0:T(8,128)(2,1)S(1)} %get-tuple-element.2), kind=kOutput, calls=%fused_computation.1 | convolution fusion | flops 190873600 | bytes 3361024 | tf_op jit(solution)/shard_map/dot_general | solution.py:70
  23.6 5.1 %reshape.73 = bf16[64,180,128]{2,1,0:T(8,128)(2,1)S(1)} reshape(bf16[576,2560]{1,0:T(8,128)(2,1)} %convolution_convert_fusion.1) | data formatting | bytes 5898240 | tf_op jit(solution)/shard_map/reshape | solution.py:24
  28.7 52.0 %all_to_all.34 = bf16[64,180,128]{2,1,0:T(8,128)(2,1)} all-to-all(bf16[64,180,128]{2,1,0:T(8,128)(2,1)S(1)} %reshape.73), channel_id=1, replica_groups=mesh['ep'=64,'dp'=2] {'ep'}, dimensions={0} | all-to-all | bytes 5898240 | tf_op jit(solution)/shard_map/all_to_all | solution.py:25
  80.7 6.0 %reshape.74 = bf16[576,2560]{1,0:T(8,128)(2,1)} reshape(bf16[64,180,128]{2,1,0:T(8,128)(2,1)} %all_to_all.34) | data formatting | bytes 5898240 | tf_op jit(solution)/shard_map/reshape | solution.py:26
  86.7 0.2 all-gather.5.cloned.1.call-start
  86.9 14.6 %all-gather.3.cloned.1.call-done = bf16[1152,2560]{1,0:T(8,128)(2,1)} async-done(((bf16[576,2560]{1,0:T(8,128)(2,1)}), bf16[1152,2560]{1,0:T(8,128)(2,1)}) %all-gather.3.cloned.1.call-update) | async-done | bytes 5898256 | tf_op jit(solution)/shard_map/all_gather | solution.py:77
  101.5 8.1 %fusion.2 = f32[1152,768]{1,0:T(8,128)S(1)} fusion(bf16[1152,2560]{1,0:T(8,128)(2,1)} %all-gather.3.cloned.1.call-done, bf16[1,2560,768]{2,1,0:T(8,128)(2,1)} %param.16), kind=kOutput, calls=%fused_computation.5 | convolution fusion | flops 4529848320 | bytes 13369344 | tf_op jit(solution)/shard_map/dot_general | solution.py:78
  109.6 6.1 %fusion.5 = bf16[1152,768]{1,0:T(8,128)(2,1)} fusion(bf16[1152,2560]{1,0:T(8,128)(2,1)S(1)} %copy-done.6, bf16[1,2560,768]{2,1,0:T(8,128)(2,1)S(1)} %copy-done.7, f32[1152,768]{1,0:T(8,128)S(1)} %fusion.2), kind=kOutput, calls=%fused_computation.9 | convolution fusion | flops 4535156736 | bytes 15138816 | tf_op jit(solution)/shard_map/dot_general | solution.py:79
  115.7 16.9 %all-gather.5.cloned.1.call-done = bf16[1152,1536]{1,0:T(8,128)(2,1)} async-done(((bf16[1152,768]{1,0:T(8,128)(2,1)}), bf16[1152,1536]{1,0:T(8,128)(2,1)}) %all-gather.5.cloned.1.call-update) | async-done | bytes 3538960 | tf_op jit(solution)/shard_map/all_gather | solution.py:82
  132.6 7.9 %convolution_convert_fusion = bf16[1152,1280]{1,0:T(8,128)(2,1)S(1)} fusion(bf16[1152,1536]{1,0:T(8,128)(2,1)} %all-gather.5.cloned.1.call-done, bf16[1,1536,1280]{2,1,0:T(8,128)(2,1)} %param.18), kind=kOutput, calls=%fused_computation | convolution fusion | flops 4531322880 | bytes 10420224 | tf_op jit(solution)/shard_map/dot_general | solution.py:81
  140.6 6.1 %all_to_all.35 = bf16[2,576,1280]{2,1,0:T(8,128)(2,1)S(1)} all-to-all(bf16[2,576,1280]{2,1,0:T(8,128)(2,1)S(1)} %bitcast.53), channel_id=1, replica_groups=mesh['ep'=64,'dp'=2] {'dp'}, dimensions={0} | all-to-all | bytes 5898240 | tf_op jit(solution)/shard_map/all_to_all | solution.py:86
  146.7 4.6 %copy.44 = bf16[1,576,2,1280]{3,2,1,0:T(2,128)(2,1)} copy(bf16[1,576,2,1280]{3,1,2,0:T(8,128)(2,1)S(1)} %bitcast.52) | data formatting | bytes 5898240 | tf_op jit(solution)/shard_map/all_to_all | solution.py:86
  151.3 6.4 %reshape_reshape.3 = bf16[64,180,128]{2,1,0:T(8,128)(2,1)S(1)} reshape(bf16[1,576,2,1280]{3,2,1,0:T(2,128)(2,1)} %copy.44) | data formatting | bytes 5898240 | tf_op jit(solution)/shard_map/reshape;reshape | solution.py:24
  157.7 50.6 %all_to_all.36 = bf16[64,180,128]{2,1,0:T(8,128)(2,1)} all-to-all(bf16[64,180,128]{2,1,0:T(8,128)(2,1)S(1)} %reshape_reshape.3), channel_id=1, replica_groups=mesh['ep'=64,'dp'=2] {'ep'}, dimensions={0} | all-to-all | bytes 5898240 | tf_op jit(solution)/shard_map/all_to_all | solution.py:25
  208.3 4.8 %reshape.76 = bf16[576,2560]{1,0:T(8,128)(2,1)S(1)} reshape(bf16[64,180,128]{2,1,0:T(8,128)(2,1)} %all_to_all.36) | data formatting | bytes 5898240 | tf_op jit(solution)/shard_map/reshape | solution.py:26
  213.1 1.8 fusion.8
  215.0 0.9 fusion.10
  (28 shorter events, 0.3 us)
Async XLA Ops:
  9.7 8.3 %copy-start.2 = (s32[64,6]{0,1:T(8,128)S(1)}, s32[64,6]{0,1:T(8,128)}, u32[]{:S(2)}) copy-start(s32[64,6]{0,1:T(8,128)} %param.14) | copy-start | bytes 4612
  9.7 8.7 %copy-start.3 = (f32[64,6]{0,1:T(8,128)S(1)}, f32[64,6]{0,1:T(8,128)}, u32[]{:S(2)}) copy-start(f32[64,6]{0,1:T(8,128)} %param.15) | copy-start | bytes 4612
  14.3 6.2 %copy-start.1 = (bf16[64,2560]{1,0:T(8,128)(2,1)S(1)}, bf16[64,2560]{1,0:T(8,128)(2,1)}, u32[]{:S(2)}) copy-start(bf16[64,2560]{1,0:T(8,128)(2,1)} %param.11) | copy-start | bytes 983044
  14.3 6.7 %copy-start.4 = (f32[2560]{0:T(1024)S(1)}, f32[2560]{0:T(1024)}, u32[]{:S(2)}) copy-start(f32[2560]{0:T(1024)} %param.13) | copy-start | bytes 30724
  14.3 5.6 %all-to-all-start = ((bf16[2,64,1280]{2,1,0:T(8,128)(2,1)}), bf16[2,64,1280]{2,1,0:T(8,128)(2,1)S(1)}, u32[]{:S(2)}, u32[]{:S(2)}) async-start(bf16[2,64,1280]{2,1,0:T(8,128)(2,1)} %bitcast), calls=%async_computation | async-start | bytes 655360 | tf_op jit(solution)/shard_map/all_to_all | solution.py:52
  17.9 83.6 %all-gather.3.cloned.1.call-start = ((), (), s32[]{:S(2)}) async-start(), calls=%async_computation.4 | async-start | bytes 8847360 | tf_op jit(solution)/shard_map/all_gather | solution.py:77
  86.7 46.0 %all-gather.5.cloned.1.call-start = ((), (), s32[]{:S(2)}) async-start(), calls=%async_computation.5 | async-start | bytes 5308416 | tf_op jit(solution)/shard_map/all_gather | solution.py:82
  101.5 8.1 %copy-start.6 = (bf16[1152,2560]{1,0:T(8,128)(2,1)S(1)}, bf16[1152,2560]{1,0:T(8,128)(2,1)}, u32[]{:S(2)}) copy-start(bf16[1152,2560]{1,0:T(8,128)(2,1)} %all-gather.3.cloned.1.call-done) | copy-start | bytes 17694724
  101.5 8.1 %copy-start.7 = (bf16[1,2560,768]{2,1,0:T(8,128)(2,1)S(1)}, bf16[1,2560,768]{2,1,0:T(8,128)(2,1)}, u32[]{:S(2)}) copy-start(bf16[1,2560,768]{2,1,0:T(8,128)(2,1)} %param.17) | copy-start | bytes 11796484
  208.3 6.7 %copy-start.5 = (f32[2560]{0:T(1024)S(1)}, f32[2560]{0:T(1024)}, u32[]{:S(2)}) copy-start(f32[2560]{0:T(1024)} %param.19) | copy-start | bytes 30724
  215.0 0.9 copy-start
Sparse Core Ops, SparseCore 0:
  86.8 14.7 all-gather.2
  115.9 16.7 all-gather.4

commit v2 on v1

--- a/solution.py
+++ b/solution.py
@@ -73,29 +73,39 @@
     gate_local = gate_weight[0]
     up_local = up_weight[0]
     down_local = down_weight[0]
-    arrived = exchange_rows(outgoing, experts)
-    segment = lax.all_gather(arrived, "dp", axis=0, tiled=True)
-    gate_part = jnp.dot(segment, gate_local, preferred_element_type=jnp.float32)
-    up_part = jnp.dot(segment, up_local, preferred_element_type=jnp.float32)
-    hidden = (jax.nn.silu(gate_part) * up_part).astype(jnp.bfloat16)
-    results = jnp.dot(
-        lax.all_gather(hidden, "dp", axis=1, tiled=True),
-        down_local,
-        preferred_element_type=jnp.float32,
-    ).astype(jnp.bfloat16)
-    joined = lax.all_to_all(
-        results.reshape(groups, experts * capacity, part_cols),
-        "dp",
-        split_axis=0,
-        concat_axis=2,
-        tiled=True,
-    )
-    returned = exchange_rows(joined.reshape(experts * capacity, row_width), experts).astype(
-        jnp.float32
-    )
+    swap = [(0, 1), (1, 0)]
+    own_rows = exchange_rows(outgoing, experts)
+    other_rows = lax.ppermute(own_rows, "dp", swap)
+
+    def hidden_of(rows):
+        gate_part = jnp.dot(rows, gate_local, preferred_element_type=jnp.float32)
+        up_part = jnp.dot(rows, up_local, preferred_element_type=jnp.float32)
+        return (jax.nn.silu(gate_part) * up_part).astype(jnp.bfloat16)
+
+    hidden_own = hidden_of(own_rows)
+    hidden_own_in = lax.ppermute(hidden_own, "dp", swap)
+    hidden_other = hidden_of(other_rows)
+    hidden_other_in = lax.ppermute(hidden_other, "dp", swap)
+    me = lax.axis_index("dp")
+
+    ff_half = hidden_own.shape[1]
+    down_mine = lax.dynamic_slice_in_dim(down_local, me * ff_half, ff_half, axis=0)
+    down_theirs = lax.dynamic_slice_in_dim(down_local, (1 - me) * ff_half, ff_half, axis=0)
+
+    def project(mine, theirs):
+        total = jnp.dot(mine, down_mine, preferred_element_type=jnp.float32)
+        total = total + jnp.dot(theirs, down_theirs, preferred_element_type=jnp.float32)
+        return total.astype(jnp.bfloat16)
+
+    out_other = project(hidden_other, hidden_own_in)
+    out_other_in = lax.ppermute(out_other, "dp", swap)
+    out_own = project(hidden_own, hidden_other_in)
+    joined = jnp.concatenate([out_own, out_other_in], axis=1)
+    returned = exchange_rows(joined, experts).astype(jnp.float32)
     expert_sum = jnp.dot(
         mixing, returned, precision=lax.Precision.HIGHEST, preferred_element_type=jnp.float32
     )
+    expert_sum = jnp.where(me == 0, expert_sum, jnp.roll(expert_sum, part_cols, axis=1))
     new_state = (summed.astype(jnp.float32) + expert_sum).astype(jnp.bfloat16)
     normed_state = rms_scale(new_state, post_gain).astype(jnp.bfloat16)
     return (new_state, normed_state)

time: 223 us -> 164 us (0.74)
  blocking collectives: 111 us -> 54.5 us
  between operations: 14.2 us -> 0.95 us
  waiting for transfers between devices: 31.6 us -> 43.3 us
  local copies, waits for them, and re-layouts: 28.2 us -> 20 us
  starting transfers between devices: 3.85 us -> 9.89 us
    all_to_all x2 -> x1, blocking collectives: 103 us -> 52 us  [exchange_rows(): moved = lax.all_to_all(wire, 'ep', split_axis=0, concat_axis=0, tiled=True)]
    all_to_all x0 -> x1, waiting for transfers between devices: none -> 40.6 us  [exchange_rows(): moved = lax.all_to_all(wire, 'ep', split_axis=0, concat_axis=0, tiled=True)]
    all_gather x2 -> x0, waiting for transfers between devices: 31.5 us -> none  [the longest x1 16.9 us: per_device(): lax.all_gather(hidden, 'dp', axis=1, tiled=True)]
    another operation x1, local copies, waits for them, and re-layouts: 6.4 us -> 0.22 us  [exchange_rows(): wire = rows.reshape(experts, total * width // (experts * lanes), lanes)]
    all_to_all x1 -> x0, blocking collectives: 6.1 us -> none  [per_device(): lax.all_to_all(results.reshape(groups, experts * capacity, part_cols), 'd...]
    all_to_all x0 -> x1, starting transfers between devices: none -> 4.89 us  [exchange_rows(): moved = lax.all_to_all(wire, 'ep', split_axis=0, concat_axis=0, tiled=True)]
    all_to_all x1 -> x0, local copies, waits for them, and re-layouts: 4.63 us -> none  [per_device(): lax.all_to_all(results.reshape(groups, experts * capacity, part_cols), 'd...]
    reshape x1 -> x2, local copies, waits for them, and re-layouts: 5.06 us -> 9.63 us  [exchange_rows(): wire = rows.reshape(experts, total * width // (experts * lanes), lanes)]
  transfers between devices with their start and end apart: 3 -> 6, of which waited for: 2 -> 2; matrix products, arithmetic and copies ran while one was open for 1% -> 13% of each run, Pallas kernels for 0% -> 0%
where the time goes in v2:
time: 164 us
  blocking collectives  54.5 us (33%)
  waiting for transfers between devices  43.3 us (26%)
  matrix products  32.3 us (20%)
  local copies, waits for them, and re-layouts  20 us (12%)
  starting transfers between devices  9.89 us (6%)
  other arithmetic  2.93 us (2%)
    all_to_all x1, blocking collectives, exchange_rows(): moved = lax.all_to_all(wire, 'ep', split_axis=0, concat_axis=0, tiled=True)  52 us
    all_to_all x1, waiting for transfers between devices, exchange_rows(): moved = lax.all_to_all(wire, 'ep', split_axis=0, concat_axis=0, tiled=True)  40.6 us
    reshape x2, local copies, waits for them, and re-layouts, exchange_rows(): wire = rows.reshape(experts, total * width // (experts * lanes), lanes)  9.63 us
    dot_general x2, matrix products, hidden_of(): gate_part = jnp.dot(rows, gate_local, preferred_element_type=jnp.float32)  8.99 us
    reshape x2, local copies, waits for them, and re-layouts, exchange_rows(): return moved.reshape(total, width)  8.98 us
    dot_general x2, matrix products, hidden_of(): up_part = jnp.dot(rows, up_local, preferred_element_type=jnp.float32)  7.17 us
    all_to_all x1, starting transfers between devices, exchange_rows(): moved = lax.all_to_all(wire, 'ep', split_axis=0, concat_axis=0, tiled=True)  4.89 us
    dot_general x1, matrix products, per_device(): jnp.dot(lax.all_gather(attention_out, 'dp', axis=0, tiled=True), out_weig...  4.64 us
  transfers between devices with their start and end apart: 6, of which 2 were waited for; matrix products, arithmetic and copies ran while one was open for 13% of the time, Pallas kernels for 0%

profile of v2, /device:TPU:0, one launch (start us, length us, event | category | flops | bytes accessed | tf_op | source)
XLA Modules:
  0.0 163.9 jit_solution(9931211148720386825)
XLA Ops:
  0.6 2.5 %all_gather.3 = bf16[128,2560]{1,0:T(8,128)(2,1)S(1)} all-gather(bf16[64,2560]{1,0:T(8,128)(2,1)} %param.10), channel_id=1, replica_groups=mesh['ep'=64,'dp'=2] {'dp'}, dimensions={0}, use_global_device_ids=true | all-gather | bytes 983040 | tf_op jit(solution)/shard_map/all_gather | solution.py:48
  3.1 4.6 %convolution_convert_fusion.1 = bf16[128,1280]{1,0:T(8,128)(2,1)} fusion(bf16[128,2560]{1,0:T(8,128)(2,1)S(1)} %all_gather.3, bf16[2560,1280]{1,0:T(8,128)(2,1)} %param.12), kind=kOutput, calls=%fused_computation.14 | convolution fusion | flops 839024640 | bytes 7536640 | tf_op jit(solution)/shard_map/dot_general | solution.py:47
  7.8 3.6 %all-to-all-start = ((bf16[2,64,1280]{2,1,0:T(8,128)(2,1)}), bf16[2,64,1280]{2,1,0:T(8,128)(2,1)S(1)}, u32[]{:S(2)}, u32[]{:S(2)}) async-start(bf16[2,64,1280]{2,1,0:T(8,128)(2,1)} %bitcast), calls=%async_computation | async-start | bytes 655360 | tf_op jit(solution)/shard_map/all_to_all | solution.py:52
  11.6 0.1 eq.46
  11.8 0.9 reduce-window.6
  12.7 0.2 slice_reduce_fusion
  13.4 0.5 copy.29
  14.0 0.2 fusion.25
  14.2 0.3 convert_reduce_fusion
  14.4 2.6 %convolution_convert_fusion = bf16[576,2560]{1,0:T(8,128)(2,1)} fusion(bf16[64,2560]{1,0:T(8,128)(2,1)S(1)} %get-tuple-element.7, f32[2560]{0:T(1024)S(1)} %copy-done.4, f32[64]{0:T(128)S(1)} %add_rsqrt_fusion.1, bf16[64,576]{1,0:T(8,128)(2,1)S(1)} %get-tuple-element.2), kind=kOutput, calls=%fused_computation | convolution fusion | flops 190873600 | bytes 3361024 | tf_op jit(solution)/shard_map/dot_general | solution.py:70
  17.0 5.1 %reshape.74 = bf16[64,180,128]{2,1,0:T(8,128)(2,1)S(1)} reshape(bf16[576,2560]{1,0:T(8,128)(2,1)} %convolution_convert_fusion) | data formatting | bytes 5898240 | tf_op jit(solution)/shard_map/reshape | solution.py:24
  22.1 52.0 %all_to_all.19 = bf16[64,180,128]{2,1,0:T(8,128)(2,1)} all-to-all(bf16[64,180,128]{2,1,0:T(8,128)(2,1)S(1)} %reshape.74), channel_id=1, replica_groups=mesh['ep'=64,'dp'=2] {'ep'}, dimensions={0} | all-to-all | bytes 5898240 | tf_op jit(solution)/shard_map/all_to_all | solution.py:25
  74.1 4.8 %reshape.75 = bf16[576,2560]{1,0:T(8,128)(2,1)S(1)} reshape(bf16[64,180,128]{2,1,0:T(8,128)(2,1)} %all_to_all.19) | data formatting | bytes 5898240 | tf_op jit(solution)/shard_map/reshape | solution.py:26
  79.0 4.7 %fusion.6 = f32[576,768]{1,0:T(8,128)S(1)} fusion(bf16[576,2560]{1,0:T(8,128)(2,1)S(1)} %reshape.75, bf16[1,2560,768]{2,1,0:T(8,128)(2,1)} %param.16), kind=kOutput, calls=%fused_computation.7 | convolution fusion | flops 2264924160 | bytes 8650752 | tf_op jit(solution)/shard_map/dot_general | solution.py:81
  83.7 2.6 %multiply_convert_fusion.1 = bf16[576,768]{1,0:T(8,128)(2,1)S(1)} fusion(f32[576,768]{1,0:T(8,128)S(1)} %fusion.6, bf16[576,2560]{1,0:T(8,128)(2,1)S(1)} %reshape.75, bf16[1,2560,768]{2,1,0:T(8,128)(2,1)S(1)} %copy-done.7), kind=kOutput, calls=%fused_computation.22 | convolution fusion | flops 2267578368 | bytes 9535488 | tf_op jit(solution)/shard_map/dot_general | solution.py:82
  86.4 0.7 collective-permute-start.2
  87.1 4.3 %fusion.4 = f32[576,768]{1,0:T(8,128)S(1)} fusion(bf16[576,2560]{1,0:T(8,128)(2,1)} %collective-permute-done, bf16[1,2560,768]{2,1,0:T(8,128)(2,1)S(1)} %copy-done.6), kind=kOutput, calls=%fused_computation.5 | convolution fusion | flops 2264924160 | bytes 8650752 | tf_op jit(solution)/shard_map/dot_general | solution.py:81
  91.4 4.6 %multiply_convert_fusion = bf16[576,768]{1,0:T(8,128)(2,1)S(1)} fusion(f32[576,768]{1,0:T(8,128)S(1)} %fusion.4, bf16[576,2560]{1,0:T(8,128)(2,1)} %collective-permute-done, bf16[1,2560,768]{2,1,0:T(8,128)(2,1)S(1)} %copy-done.7), kind=kOutput, calls=%fused_computation.21 | convolution fusion | flops 2267578368 | bytes 9535488 | tf_op jit(solution)/shard_map/dot_general | solution.py:82
  96.0 1.3 fusion.12
  97.3 1.3 fusion.9
  98.8 0.5 collective-permute-start.1
  99.2 1.3 fusion.14
  100.6 2.7 %collective-permute-done.1 = bf16[576,768]{1,0:T(8,128)(2,1)S(1)} collective-permute-done((bf16[576,768]{1,0:T(8,128)(2,1)S(1)}, bf16[576,768]{1,0:T(8,128)(2,1)S(1)}, u32[]{:S(2)}, u32[]{:S(2)}) %collective-permute-start.1) | collective-permute-done | bytes 884768 | tf_op jit(solution)/shard_map/ppermute | solution.py:88
  103.3 1.3 fusion.8
  104.6 0.2 pad_maximum_fusion
  104.8 4.6 %reshape.76 = bf16[64,180,128]{2,1,0:T(8,128)(2,1)} reshape(bf16[576,2560]{1,0:T(8,128)(2,1)S(1)} %pad_maximum_fusion) | data formatting | bytes 5898240 | tf_op jit(solution)/shard_map/reshape | solution.py:24
  109.4 4.9 %all-to-all-start.2 = ((bf16[64,180,128]{2,1,0:T(8,128)(2,1)}), bf16[64,180,128]{2,1,0:T(8,128)(2,1)S(1)}, u32[]{:S(2)}, u32[]{:S(2)}) async-start(bf16[64,180,128]{2,1,0:T(8,128)(2,1)} %reshape.76), calls=%async_computation.2 | async-start | bytes 6029312 | tf_op jit(solution)/shard_map/all_to_all | solution.py:25
  114.3 40.6 %all-to-all-done.2 = bf16[64,180,128]{2,1,0:T(8,128)(2,1)S(1)} async-done(((bf16[64,180,128]{2,1,0:T(8,128)(2,1)}), bf16[64,180,128]{2,1,0:T(8,128)(2,1)S(1)}, u32[]{:S(2)}, u32[]{:S(2)}) %all-to-all-start.2) | async-done | bytes 2949152 | tf_op jit(solution)/shard_map/all_to_all | solution.py:25
  154.9 4.2 %reshape.77 = bf16[576,2560]{1,0:T(8,128)(2,1)} reshape(bf16[64,180,128]{2,1,0:T(8,128)(2,1)S(1)} %all-to-all-done.2) | data formatting | bytes 5898240 | tf_op jit(solution)/shard_map/reshape | solution.py:26
  159.2 3.6 %fusion.43 = f32[64,2560]{1,0:T(8,128)S(1)} fusion(f32[64,576]{1,0:T(8,128)S(1)} %get-tuple-element.3, bf16[576,2560]{1,0:T(8,128)(2,1)} %reshape.77), kind=kOutput, calls=%fused_computation.66 | convolution fusion | flops 1132462080 | bytes 3751936 | tf_op jit(solution)/shard_map/dot_general | solution.py:105
  162.8 0.2 fusion.22
  163.1 0.9 fusion.24
  (39 shorter events, 1.0 us)
Async XLA Ops:
  3.1 8.2 %copy-start.2 = (s32[64,6]{0,1:T(8,128)S(1)}, s32[64,6]{0,1:T(8,128)}, u32[]{:S(2)}) copy-start(s32[64,6]{0,1:T(8,128)} %param.14) | copy-start | bytes 4612
  3.1 10.2 %copy-start.3 = (f32[64,6]{0,1:T(8,128)S(1)}, f32[64,6]{0,1:T(8,128)}, u32[]{:S(2)}) copy-start(f32[64,6]{0,1:T(8,128)} %param.15) | copy-start | bytes 4612
  7.8 6.2 %copy-start.1 = (bf16[64,2560]{1,0:T(8,128)(2,1)S(1)}, bf16[64,2560]{1,0:T(8,128)(2,1)}, u32[]{:S(2)}) copy-start(bf16[64,2560]{1,0:T(8,128)(2,1)} %param.11) | copy-start | bytes 983044
  7.8 5.6 %all-to-all-start = ((bf16[2,64,1280]{2,1,0:T(8,128)(2,1)}), bf16[2,64,1280]{2,1,0:T(8,128)(2,1)S(1)}, u32[]{:S(2)}, u32[]{:S(2)}) async-start(bf16[2,64,1280]{2,1,0:T(8,128)(2,1)} %bitcast), calls=%async_computation | async-start | bytes 655360 | tf_op jit(solution)/shard_map/all_to_all | solution.py:52
  11.4 3.1 %copy-start.4 = (f32[2560]{0:T(1024)S(1)}, f32[2560]{0:T(1024)}, u32[]{:S(2)}) copy-start(f32[2560]{0:T(1024)} %param.13) | copy-start | bytes 30724
  78.9 8.2 %collective-permute-start = (bf16[576,2560]{1,0:T(8,128)(2,1)S(1)}, bf16[576,2560]{1,0:T(8,128)(2,1)}, u32[]{:S(2)}, u32[]{:S(2)}) collective-permute-start(bf16[576,2560]{1,0:T(8,128)(2,1)S(1)} %reshape.75), channel_id=1, source_target_pairs={{0,1},{1,0},{2,3},{3,2},{4,5},{5,4},{6,7},{7,6},{8,9},{9,8},{10,11... | collective-permute-start | bytes 8847368 | tf_op jit(solution)/shard_map/ppermute | solution.py:78
  79.0 4.7 %copy-start.7 = (bf16[1,2560,768]{2,1,0:T(8,128)(2,1)S(1)}, bf16[1,2560,768]{2,1,0:T(8,128)(2,1)}, u32[]{:S(2)}) copy-start(bf16[1,2560,768]{2,1,0:T(8,128)(2,1)} %param.17) | copy-start | bytes 11796484
  83.7 3.4 %copy-start.6 = (bf16[1,2560,768]{2,1,0:T(8,128)(2,1)S(1)}, bf16[1,2560,768]{2,1,0:T(8,128)(2,1)}, u32[]{:S(2)}) copy-start(bf16[1,2560,768]{2,1,0:T(8,128)(2,1)} %param.16) | copy-start | bytes 11796484
  86.4 11.0 %collective-permute-start.2 = (bf16[576,768]{1,0:T(8,128)(2,1)S(1)}, bf16[576,768]{1,0:T(8,128)(2,1)S(1)}, u32[]{:S(2)}, u32[]{:S(2)}) collective-permute-start(bf16[576,768]{1,0:T(8,128)(2,1)S(1)} %multiply_convert_fusion.1), channel_id=1, source_target_pairs={{0,1},{1,0},{2,3},{3,2},{4,5},{5,4},{6,7},{7,6},{8,9},{9,8},{10,11... | collective-permute-start | bytes 2654216 | tf_op jit(solution)/shard_map/ppermute | solution.py:86
  91.4 4.6 %copy-start.8 = (bf16[1,1536,1280]{2,1,0:T(8,128)(2,1)S(1)}, bf16[1,1536,1280]{2,1,0:T(8,128)(2,1)}, u32[]{:S(2)}) copy-start(bf16[1,1536,1280]{2,1,0:T(8,128)(2,1)} %param.18) | copy-start | bytes 11796484
  98.7 5.9 %collective-permute-start.3 = (bf16[576,1280]{1,0:T(8,128)(2,1)S(1)}, bf16[576,1280]{1,0:T(8,128)(2,1)S(1)}, u32[]{:S(2)}, u32[]{:S(2)}) collective-permute-start(bf16[576,1280]{1,0:T(8,128)(2,1)S(1)} %fusion.9), channel_id=1, source_target_pairs={{0,1},{1,0},{2,3},{3,2},{4,5},{5,4},{6,7},{7,6},{8,9},{9,8},{10,11... | collective-permute-start | bytes 4423688 | tf_op jit(solution)/shard_map/ppermute | solution.py:101
  98.8 4.5 %collective-permute-start.1 = (bf16[576,768]{1,0:T(8,128)(2,1)S(1)}, bf16[576,768]{1,0:T(8,128)(2,1)S(1)}, u32[]{:S(2)}, u32[]{:S(2)}) collective-permute-start(bf16[576,768]{1,0:T(8,128)(2,1)S(1)} %multiply_convert_fusion), channel_id=1, source_target_pairs={{0,1},{1,0},{2,3},{3,2},{4,5},{5,4},{6,7},{7,6},{8,9},{9,8},{10,11... | collective-permute-start | bytes 2654216 | tf_op jit(solution)/shard_map/ppermute | solution.py:88
  109.4 45.5 %all-to-all-start.2 = ((bf16[64,180,128]{2,1,0:T(8,128)(2,1)}), bf16[64,180,128]{2,1,0:T(8,128)(2,1)S(1)}, u32[]{:S(2)}, u32[]{:S(2)}) async-start(bf16[64,180,128]{2,1,0:T(8,128)(2,1)} %reshape.76), calls=%async_computation.2 | async-start | bytes 6029312 | tf_op jit(solution)/shard_map/all_to_all | solution.py:25
  159.2 3.9 %copy-start.5 = (f32[2560]{0:T(1024)S(1)}, f32[2560]{0:T(1024)}, u32[]{:S(2)}) copy-start(f32[2560]{0:T(1024)} %param.19) | copy-start | bytes 30724
  163.0 0.9 copy-start

commit v3 on v2

--- a/solution.py
+++ b/solution.py
@@ -67,44 +67,54 @@
     placing = jnp.sum(matches, axis=1).astype(jnp.bfloat16)
     weights = gate_prob / jnp.sum(gate_prob, axis=1, keepdims=True)
     mixing = jnp.sum(weights[:, :, None] * matches, axis=1)
-    outgoing = lax.dot_general(
-        placing, normed_in, (((0,), (0,)), ((), ())), preferred_element_type=jnp.float32
-    ).astype(jnp.bfloat16)
     gate_local = gate_weight[0]
     up_local = up_weight[0]
     down_local = down_weight[0]
     swap = [(0, 1), (1, 0)]
-    own_rows = exchange_rows(outgoing, experts)
-    other_rows = lax.ppermute(own_rows, "dp", swap)
+    me = lax.axis_index("dp")
+    ff_half = gate_local.shape[1]
+    down_mine = lax.dynamic_slice_in_dim(down_local, me * ff_half, ff_half, axis=0)
+    down_theirs = lax.dynamic_slice_in_dim(down_local, (1 - me) * ff_half, ff_half, axis=0)
 
     def hidden_of(rows):
         gate_part = jnp.dot(rows, gate_local, preferred_element_type=jnp.float32)
         up_part = jnp.dot(rows, up_local, preferred_element_type=jnp.float32)
         return (jax.nn.silu(gate_part) * up_part).astype(jnp.bfloat16)
 
-    hidden_own = hidden_of(own_rows)
-    hidden_own_in = lax.ppermute(hidden_own, "dp", swap)
-    hidden_other = hidden_of(other_rows)
-    hidden_other_in = lax.ppermute(hidden_other, "dp", swap)
-    me = lax.axis_index("dp")
-
-    ff_half = hidden_own.shape[1]
-    down_mine = lax.dynamic_slice_in_dim(down_local, me * ff_half, ff_half, axis=0)
-    down_theirs = lax.dynamic_slice_in_dim(down_local, (1 - me) * ff_half, ff_half, axis=0)
-
     def project(mine, theirs):
         total = jnp.dot(mine, down_mine, preferred_element_type=jnp.float32)
         total = total + jnp.dot(theirs, down_theirs, preferred_element_type=jnp.float32)
         return total.astype(jnp.bfloat16)
 
-    out_other = project(hidden_other, hidden_own_in)
-    out_other_in = lax.ppermute(out_other, "dp", swap)
-    out_own = project(hidden_own, hidden_other_in)
-    joined = jnp.concatenate([out_own, out_other_in], axis=1)
-    returned = exchange_rows(joined, experts).astype(jnp.float32)
-    expert_sum = jnp.dot(
-        mixing, returned, precision=lax.Precision.HIGHEST, preferred_element_type=jnp.float32
-    )
+    def expert_rows(own_rows):
+        other_rows = lax.ppermute(own_rows, "dp", swap)
+        hidden_own = hidden_of(own_rows)
+        hidden_own_in = lax.ppermute(hidden_own, "dp", swap)
+        hidden_other = hidden_of(other_rows)
+        hidden_other_in = lax.ppermute(hidden_other, "dp", swap)
+        out_other = project(hidden_other, hidden_own_in)
+        out_other_in = lax.ppermute(out_other, "dp", swap)
+        out_own = project(hidden_own, hidden_other_in)
+        return jnp.concatenate([out_own, out_other_in], axis=1)
+
+    placing3 = placing.reshape(tok_rows, experts, capacity)
+    mixing3 = mixing.reshape(tok_rows, experts, capacity)
+    cut = (capacity + 1) // 2
+    expert_sum = None
+    for lo, hi in ((0, cut), (cut, capacity)):
+        chunk_place = placing3[:, :, lo:hi].reshape(tok_rows, -1)
+        outgoing = lax.dot_general(
+            chunk_place, normed_in, (((0,), (0,)), ((), ())), preferred_element_type=jnp.float32
+        ).astype(jnp.bfloat16)
+        joined = expert_rows(exchange_rows(outgoing, experts))
+        returned = exchange_rows(joined, experts).astype(jnp.float32)
+        part = jnp.dot(
+            mixing3[:, :, lo:hi].reshape(tok_rows, -1),
+            returned,
+            precision=lax.Precision.HIGHEST,
+            preferred_element_type=jnp.float32,
+        )
+        expert_sum = part if expert_sum is None else expert_sum + part
     expert_sum = jnp.where(me == 0, expert_sum, jnp.roll(expert_sum, part_cols, axis=1))
     new_state = (summed.astype(jnp.float32) + expert_sum).astype(jnp.bfloat16)
     normed_state = rms_scale(new_state, post_gain).astype(jnp.bfloat16)

time: 164 us -> 173 us (1.055)
  blocking collectives: 54.5 us -> 2.49 us
  starting transfers between devices: 9.89 us -> 33.1 us
  waiting for transfers between devices: 43.3 us -> 63.2 us
  matrix products: 32.3 us -> 41.1 us
  local copies, waits for them, and re-layouts: 20 us -> 28.1 us
    all_to_all x1 -> x0, blocking collectives: 52 us -> none  [exchange_rows(): moved = lax.all_to_all(wire, 'ep', split_axis=0, concat_axis=0, tiled=True)]
    all_to_all x1 -> x4, starting transfers between devices: 4.89 us -> 27.3 us  [exchange_rows(): moved = lax.all_to_all(wire, 'ep', split_axis=0, concat_axis=0, tiled=True)]
    all_to_all x1 -> x4, waiting for transfers between devices: 40.6 us -> 62.5 us  [exchange_rows(): moved = lax.all_to_all(wire, 'ep', split_axis=0, concat_axis=0, tiled=True)]
    dot_general x2 -> x4, matrix products: 2.65 us -> 6.21 us  [project(): total = jnp.dot(mine, down_mine, preferred_element_type=jnp.float32)]
    dot_general x2 -> x4, matrix products: 2.64 us -> 5.86 us  [project(): jnp.dot(theirs, down_theirs, preferred_element_type=jnp.float32)]
    dot_general x2 -> x4, matrix products: 8.99 us -> 11.9 us  [hidden_of(): gate_part = jnp.dot(rows, gate_local, preferred_element_type=jnp.float32)]
    reshape x0 -> x3, local copies, waits for them, and re-layouts: none -> 2.66 us  [the longest x1 1 us: per_device(): mixing3 = mixing.reshape(tok_rows, experts, capacity)]
    dot_general x2 -> x4, matrix products: 6.17 us -> 4.08 us  [the longest x2 2.08 us: per_device(): lax.dot_general(chunk_place, normed_in, (((0,), (0,)), ((), ())), preferr...]
  transfers between devices with their start and end apart: 6 -> 13, of which waited for: 2 -> 5; matrix products, arithmetic and copies ran while one was open for 13% -> 33% of each run, Pallas kernels for 0% -> 0%
where the time goes in v3:
time: 173 us; the launch traced here: 172 us
  waiting for transfers between devices  63.2 us (37%)
  matrix products  41.1 us (24%)
  starting transfers between devices  33.1 us (19%)
  local copies, waits for them, and re-layouts  28.1 us (16%)
  other arithmetic  2.91 us (2%)
  blocking collectives  2.49 us (1%)
    all_to_all x4, waiting for transfers between devices, exchange_rows(): moved = lax.all_to_all(wire, 'ep', split_axis=0, concat_axis=0, tiled=True)  62.5 us
    all_to_all x4, starting transfers between devices, exchange_rows(): moved = lax.all_to_all(wire, 'ep', split_axis=0, concat_axis=0, tiled=True)  27.3 us
    dot_general x4, matrix products, hidden_of(): gate_part = jnp.dot(rows, gate_local, preferred_element_type=jnp.float32)  11.9 us
    reshape x4, local copies, waits for them, and re-layouts, exchange_rows(): wire = rows.reshape(experts, total * width // (experts * lanes), lanes)  11 us
    reshape x4, local copies, waits for them, and re-layouts, exchange_rows(): return moved.reshape(total, width)  9.21 us
    dot_general x4, matrix products, hidden_of(): up_part = jnp.dot(rows, up_local, preferred_element_type=jnp.float32)  8.37 us
    dot_general x4, matrix products, project(): total = jnp.dot(mine, down_mine, preferred_element_type=jnp.float32)  6.21 us
    dot_general x4, matrix products, project(): jnp.dot(theirs, down_theirs, preferred_element_type=jnp.float32)  5.86 us
  transfers between devices with their start and end apart: 13, of which 5 were waited for; matrix products, arithmetic and copies ran while one was open for 33% of the time, Pallas kernels for 0%

profile of v3, /device:TPU:0, one launch (start us, length us, event | category | flops | bytes accessed | tf_op | source)
XLA Modules:
  0.0 172.0 jit_solution(1652725697353831564)
XLA Ops:
  0.6 2.5 %all_gather.3 = bf16[128,2560]{1,0:T(8,128)(2,1)S(1)} all-gather(bf16[64,2560]{1,0:T(8,128)(2,1)} %param.10), channel_id=1, replica_groups=mesh['ep'=64,'dp'=2] {'dp'}, dimensions={0}, use_global_device_ids=true | all-gather | bytes 983040 | tf_op jit(solution)/shard_map/all_gather | solution.py:48
  3.1 4.6 %convolution_convert_fusion.2 = bf16[128,1280]{1,0:T(8,128)(2,1)} fusion(bf16[128,2560]{1,0:T(8,128)(2,1)S(1)} %all_gather.3, bf16[2560,1280]{1,0:T(8,128)(2,1)} %param.12), kind=kOutput, calls=%fused_computation.27 | convolution fusion | flops 839024640 | bytes 7536640 | tf_op jit(solution)/shard_map/dot_general | solution.py:47
  7.8 3.5 %all-to-all-start = ((bf16[2,64,1280]{2,1,0:T(8,128)(2,1)}), bf16[2,64,1280]{2,1,0:T(8,128)(2,1)S(1)}, u32[]{:S(2)}, u32[]{:S(2)}) async-start(bf16[2,64,1280]{2,1,0:T(8,128)(2,1)} %bitcast), calls=%async_computation | async-start | bytes 655360 | tf_op jit(solution)/shard_map/all_to_all | solution.py:52
  15.6 2.4 %reshape.113 = bf16[64,80,128]{2,1,0:T(8,128)(2,1)} reshape(bf16[256,2560]{1,0:T(8,128)(2,1)S(1)} %convolution_convert_fusion.1) | data formatting | bytes 2621440 | tf_op jit(solution)/shard_map/reshape | solution.py:24
  18.0 11.5 %all-to-all-start.3 = ((bf16[64,80,128]{2,1,0:T(8,128)(2,1)}), bf16[64,80,128]{2,1,0:T(8,128)(2,1)S(1)}, u32[]{:S(2)}, u32[]{:S(2)}) async-start(bf16[64,80,128]{2,1,0:T(8,128)(2,1)} %reshape.113), calls=%async_computation.3 | async-start | bytes 2621440 | tf_op jit(solution)/shard_map/all_to_all | solution.py:25
  30.2 1.5 convolution_convert_fusion
  31.8 3.0 %reshape.107 = bf16[64,100,128]{2,1,0:T(8,128)(2,1)} reshape(bf16[320,2560]{1,0:T(8,128)(2,1)S(1)} %convolution_convert_fusion) | data formatting | bytes 3276800 | tf_op jit(solution)/shard_map/reshape | solution.py:24
  34.8 17.0 %all-to-all-done.3 = bf16[64,80,128]{2,1,0:T(8,128)(2,1)S(1)} async-done(((bf16[64,80,128]{2,1,0:T(8,128)(2,1)}), bf16[64,80,128]{2,1,0:T(8,128)(2,1)S(1)}, u32[]{:S(2)}, u32[]{:S(2)}) %all-to-all-start.3) | async-done | bytes 1310752 | tf_op jit(solution)/shard_map/all_to_all | solution.py:25
  51.8 5.1 %all-to-all-start.1 = ((bf16[64,100,128]{2,1,0:T(8,128)(2,1)}), bf16[64,100,128]{2,1,0:T(8,128)(2,1)S(1)}, u32[]{:S(2)}, u32[]{:S(2)}) async-start(bf16[64,100,128]{2,1,0:T(8,128)(2,1)} %reshape.107), calls=%async_computation.1 | async-start | bytes 3407872 | tf_op jit(solution)/shard_map/all_to_all | solution.py:25
  56.9 2.3 %reshape.114 = bf16[256,2560]{1,0:T(8,128)(2,1)} reshape(bf16[64,80,128]{2,1,0:T(8,128)(2,1)S(1)} %all-to-all-done.3) | data formatting | bytes 2621440 | tf_op jit(solution)/shard_map/reshape | solution.py:26
  59.2 3.8 %fusion.10 = f32[256,768]{1,0:T(8,128)S(1)} fusion(bf16[256,2560]{1,0:T(8,128)(2,1)} %reshape.114, bf16[1,2560,768]{2,1,0:T(8,128)(2,1)} %param.16), kind=kOutput, calls=%fused_computation.11 | convolution fusion | flops 1006632960 | bytes 6029312 | tf_op jit(solution)/shard_map/dot_general | solution.py:80
  63.3 2.0 %fusion.49 = bf16[256,768]{1,0:T(8,128)(2,1)} fusion(bf16[256,2560]{1,0:T(8,128)(2,1)S(1)} %copy-done.9, bf16[1,2560,768]{2,1,0:T(8,128)(2,1)S(1)} %copy-done.19, f32[256,768]{1,0:T(8,128)S(1)} %fusion.10), kind=kOutput, calls=%fused_computation.53 | convolution fusion | flops 1007812608 | bytes 6422528 | tf_op jit(solution)/shard_map/dot_general | solution.py:81
  65.9 1.7 fusion.26
  67.6 15.0 %all-to-all-done.1 = bf16[64,100,128]{2,1,0:T(8,128)(2,1)S(1)} async-done(((bf16[64,100,128]{2,1,0:T(8,128)(2,1)}), bf16[64,100,128]{2,1,0:T(8,128)(2,1)S(1)}, u32[]{:S(2)}, u32[]{:S(2)}) %all-to-all-start.1) | async-done | bytes 1638432 | tf_op jit(solution)/shard_map/all_to_all | solution.py:25
  82.5 2.7 %reshape.108 = bf16[320,2560]{1,0:T(8,128)(2,1)} reshape(bf16[64,100,128]{2,1,0:T(8,128)(2,1)S(1)} %all-to-all-done.1) | data formatting | bytes 3276800 | tf_op jit(solution)/shard_map/reshape | solution.py:26
  85.3 4.2 %fusion.14 = f32[320,768]{1,0:T(8,128)S(1)} fusion(bf16[320,2560]{1,0:T(8,128)(2,1)} %reshape.108, bf16[1,2560,768]{2,1,0:T(8,128)(2,1)} %param.16), kind=kOutput, calls=%fused_computation.15 | convolution fusion | flops 1258291200 | bytes 6553600 | tf_op jit(solution)/shard_map/dot_general | solution.py:80
  89.5 2.3 %fusion.38 = bf16[320,768]{1,0:T(8,128)(2,1)} fusion(bf16[320,2560]{1,0:T(8,128)(2,1)S(1)} %copy-done.6, bf16[1,2560,768]{2,1,0:T(8,128)(2,1)S(1)} %copy-done.20, f32[320,768]{1,0:T(8,128)S(1)} %fusion.14), kind=kOutput, calls=%fused_computation.44 | convolution fusion | flops 1259765760 | bytes 7045120 | tf_op jit(solution)/shard_map/dot_general | solution.py:81
  92.1 2.5 %fusion.8 = f32[256,768]{1,0:T(8,128)S(1)} fusion(bf16[256,2560]{1,0:T(8,128)(2,1)} %collective-permute-done.4, bf16[1,2560,768]{2,1,0:T(8,128)(2,1)S(1)} %copy-done.18), kind=kOutput, calls=%fused_computation.9 | convolution fusion | flops 1006632960 | bytes 6029312 | tf_op jit(solution)/shard_map/dot_general | solution.py:80
  94.6 2.7 %multiply_convert_fusion.1 = bf16[256,768]{1,0:T(8,128)(2,1)S(1)} fusion(f32[256,768]{1,0:T(8,128)S(1)} %fusion.8, bf16[256,2560]{1,0:T(8,128)(2,1)} %collective-permute-done.4, bf16[1,2560,768]{2,1,0:T(8,128)(2,1)S(1)} %copy-done.20), kind=kOutput, calls=%fused_computation.63 | convolution fusion | flops 1007812608 | bytes 6422528 | tf_op jit(solution)/shard_map/dot_general | solution.py:81
  98.3 1.7 fusion.19
  102.7 1.5 multiply_convert_fusion
  104.2 2.0 %fusion.28 = f32[320,1280]{1,0:T(8,128)} fusion(bf16[320,768]{1,0:T(8,128)(2,1)S(1)} %multiply_convert_fusion, bf16[1,1536,1280]{2,1,0:T(8,128)(2,1)S(1)} %copy-done.1, s32[]{:T(128)S(6)} %select_n.15), kind=kOutput, calls=%fused_computation.36 | convolution fusion | flops 629145600 | bytes 4096004 | tf_op jit(solution)/shard_map/dot_general | solution.py:85
  106.3 2.4 %reshape.115 = bf16[64,80,128]{2,1,0:T(8,128)(2,1)} reshape(bf16[256,2560]{1,0:T(8,128)(2,1)S(1)} %pad_maximum_fusion.1) | data formatting | bytes 2621440 | tf_op jit(solution)/shard_map/reshape | solution.py:24
  108.8 5.4 %all-to-all-start.4 = ((bf16[64,80,128]{2,1,0:T(8,128)(2,1)}), bf16[64,80,128]{2,1,0:T(8,128)(2,1)S(1)}, u32[]{:S(2)}, u32[]{:S(2)}) async-start(bf16[64,80,128]{2,1,0:T(8,128)(2,1)} %reshape.115), calls=%async_computation.4 | async-start | bytes 2621440 | tf_op jit(solution)/shard_map/all_to_all | solution.py:25
  114.3 2.7 %fusion.17 = bf16[320,1280]{1,0:T(8,128)(2,1)S(1)} fusion(f32[320,1280]{1,0:T(8,128)S(1)} %copy-done.7, bf16[320,768]{1,0:T(8,128)(2,1)} %collective-permute-done.2, bf16[1,1536,1280]{2,1,0:T(8,128)(2,1)} %param.18, s32[]{:T(128)S(6)} %select_n.16), kind=kOutput, calls=%fused_computation.24 | convolution fusion | flops 629964800 | bytes 4915204 | tf_op jit(solution)/shard_map/dot_general | solution.py:86
  117.5 1.8 %fusion.30 = f32[320,1280]{1,0:T(8,128)S(1)} fusion(bf16[320,768]{1,0:T(8,128)(2,1)} %fusion.38, bf16[1,1536,1280]{2,1,0:T(8,128)(2,1)S(1)} %copy-done.2, s32[]{:T(128)S(6)} %select_n.15), kind=kOutput, calls=%fused_computation.38 | convolution fusion | flops 629145600 | bytes 4096004 | tf_op jit(solution)/shard_map/dot_general | solution.py:85
  121.0 3.0 %reshape.109 = bf16[64,100,128]{2,1,0:T(8,128)(2,1)} reshape(bf16[320,2560]{1,0:T(8,128)(2,1)S(1)} %pad_maximum_fusion) | data formatting | bytes 3276800 | tf_op jit(solution)/shard_map/reshape | solution.py:24
  124.0 12.2 %all-to-all-done.4 = bf16[64,80,128]{2,1,0:T(8,128)(2,1)S(1)} async-done(((bf16[64,80,128]{2,1,0:T(8,128)(2,1)}), bf16[64,80,128]{2,1,0:T(8,128)(2,1)S(1)}, u32[]{:S(2)}, u32[]{:S(2)}) %all-to-all-start.4) | async-done | bytes 1310752 | tf_op jit(solution)/shard_map/all_to_all | solution.py:25
  136.2 5.3 %all-to-all-start.2 = ((bf16[64,100,128]{2,1,0:T(8,128)(2,1)}), bf16[64,100,128]{2,1,0:T(8,128)(2,1)S(1)}, u32[]{:S(2)}, u32[]{:S(2)}) async-start(bf16[64,100,128]{2,1,0:T(8,128)(2,1)} %reshape.109), calls=%async_computation.2 | async-start | bytes 3407872 | tf_op jit(solution)/shard_map/all_to_all | solution.py:25
  145.7 2.3 %reshape.116 = bf16[256,2560]{1,0:T(8,128)(2,1)} reshape(bf16[64,80,128]{2,1,0:T(8,128)(2,1)S(1)} %all-to-all-done.4) | data formatting | bytes 2621440 | tf_op jit(solution)/shard_map/reshape | solution.py:26
  148.1 18.3 %all-to-all-done.2 = bf16[64,100,128]{2,1,0:T(8,128)(2,1)S(1)} async-done(((bf16[64,100,128]{2,1,0:T(8,128)(2,1)}), bf16[64,100,128]{2,1,0:T(8,128)(2,1)S(1)}, u32[]{:S(2)}, u32[]{:S(2)}) %all-to-all-start.2) | async-done | bytes 1638432 | tf_op jit(solution)/shard_map/all_to_all | solution.py:25
  166.4 1.8 %reshape.110 = bf16[320,2560]{1,0:T(8,128)(2,1)S(1)} reshape(bf16[64,100,128]{2,1,0:T(8,128)(2,1)S(1)} %all-to-all-done.2) | data formatting | bytes 3276800 | tf_op jit(solution)/shard_map/reshape | solution.py:26
  (101 shorter events, 20.1 us)
Async XLA Ops:
  3.1 8.1 %copy-start.15 = (s32[64,6]{0,1:T(8,128)S(1)}, s32[64,6]{0,1:T(8,128)}, u32[]{:S(2)}) copy-start(s32[64,6]{0,1:T(8,128)} %param.14) | copy-start | bytes 4612
  3.1 10.0 %copy-start.16 = (f32[64,6]{0,1:T(8,128)S(1)}, f32[64,6]{0,1:T(8,128)}, u32[]{:S(2)}) copy-start(f32[64,6]{0,1:T(8,128)} %param.15) | copy-start | bytes 4612
  7.8 5.9 %all-to-all-start = ((bf16[2,64,1280]{2,1,0:T(8,128)(2,1)}), bf16[2,64,1280]{2,1,0:T(8,128)(2,1)S(1)}, u32[]{:S(2)}, u32[]{:S(2)}) async-start(bf16[2,64,1280]{2,1,0:T(8,128)(2,1)} %bitcast), calls=%async_computation | async-start | bytes 655360 | tf_op jit(solution)/shard_map/all_to_all | solution.py:52
  13.7 1.0 copy-start.13
  14.9 15.4 %copy-start.4 = (bf16[64,2560]{1,0:T(8,128)(2,1)}, bf16[64,2560]{1,0:T(8,128)(2,1)S(1)}, u32[]{:S(2)}) copy-start(bf16[64,2560]{1,0:T(8,128)(2,1)S(1)} %get-tuple-element.7) | copy-start | bytes 983044
  18.0 33.8 %all-to-all-start.3 = ((bf16[64,80,128]{2,1,0:T(8,128)(2,1)}), bf16[64,80,128]{2,1,0:T(8,128)(2,1)S(1)}, u32[]{:S(2)}, u32[]{:S(2)}) async-start(bf16[64,80,128]{2,1,0:T(8,128)(2,1)} %reshape.113), calls=%async_computation.3 | async-start | bytes 2621440 | tf_op jit(solution)/shard_map/all_to_all | solution.py:25
  51.8 30.7 %all-to-all-start.1 = ((bf16[64,100,128]{2,1,0:T(8,128)(2,1)}), bf16[64,100,128]{2,1,0:T(8,128)(2,1)S(1)}, u32[]{:S(2)}, u32[]{:S(2)}) async-start(bf16[64,100,128]{2,1,0:T(8,128)(2,1)} %reshape.107), calls=%async_computation.1 | async-start | bytes 3407872 | tf_op jit(solution)/shard_map/all_to_all | solution.py:25
  59.2 3.9 %copy-start.9 = (bf16[256,2560]{1,0:T(8,128)(2,1)S(1)}, bf16[256,2560]{1,0:T(8,128)(2,1)}, u32[]{:S(2)}) copy-start(bf16[256,2560]{1,0:T(8,128)(2,1)} %reshape.114) | copy-start | bytes 3932164
  59.2 4.1 %copy-start.19 = (bf16[1,2560,768]{2,1,0:T(8,128)(2,1)S(1)}, bf16[1,2560,768]{2,1,0:T(8,128)(2,1)}, u32[]{:S(2)}) copy-start(bf16[1,2560,768]{2,1,0:T(8,128)(2,1)} %param.17) | copy-start | bytes 11796484
  59.2 32.9 %collective-permute-start.4 = (bf16[256,2560]{1,0:T(8,128)(2,1)}, bf16[256,2560]{1,0:T(8,128)(2,1)}, u32[]{:S(2)}, u32[]{:S(2)}) collective-permute-start(bf16[256,2560]{1,0:T(8,128)(2,1)} %reshape.114), channel_id=1, source_target_pairs={{0,1},{1,0},{2,3},{3,2},{4,5},{5,4},{6,7},{7,6},{8,9},{9,8},{10,11... | collective-permute-start | bytes 3932168 | tf_op jit(solution)/shard_map/ppermute | solution.py:90
  63.3 2.6 %copy-start = (bf16[1,1536,1280]{2,1,0:T(8,128)(2,1)S(1)}, bf16[1,1536,1280]{2,1,0:T(8,128)(2,1)}, u32[]{:S(2)}) copy-start(bf16[1,1536,1280]{2,1,0:T(8,128)(2,1)} %param.18) | copy-start | bytes 11796484
  65.3 33.0 %collective-permute-start.6 = (bf16[256,768]{1,0:T(8,128)(2,1)}, bf16[256,768]{1,0:T(8,128)(2,1)}, u32[]{:S(2)}, u32[]{:S(2)}) collective-permute-start(bf16[256,768]{1,0:T(8,128)(2,1)} %fusion.49), channel_id=1, source_target_pairs={{0,1},{1,0},{2,3},{3,2},{4,5},{5,4},{6,7},{7,6},{8,9},{9,8},{10,11... | collective-permute-start | bytes 1179656 | tf_op jit(solution)/shard_map/ppermute | solution.py:92
  85.2 4.2 %copy-start.6 = (bf16[320,2560]{1,0:T(8,128)(2,1)S(1)}, bf16[320,2560]{1,0:T(8,128)(2,1)}, u32[]{:S(2)}) copy-start(bf16[320,2560]{1,0:T(8,128)(2,1)} %reshape.108) | copy-start | bytes 4915204
  85.2 4.3 %copy-start.20 = (bf16[1,2560,768]{2,1,0:T(8,128)(2,1)S(1)}, bf16[1,2560,768]{2,1,0:T(8,128)(2,1)}, u32[]{:S(2)}) copy-start(bf16[1,2560,768]{2,1,0:T(8,128)(2,1)} %param.17) | copy-start | bytes 11796484
  85.3 16.1 %collective-permute-start = (bf16[320,2560]{1,0:T(8,128)(2,1)}, bf16[320,2560]{1,0:T(8,128)(2,1)S(1)}, u32[]{:S(2)}, u32[]{:S(2)}) collective-permute-start(bf16[320,2560]{1,0:T(8,128)(2,1)} %reshape.108), channel_id=1, source_target_pairs={{0,1},{1,0},{2,3},{3,2},{4,5},{5,4},{6,7},{7,6},{8,9},{9,8},{10,11... | collective-permute-start | bytes 4915208 | tf_op jit(solution)/shard_map/ppermute | solution.py:90
  89.5 2.6 %copy-start.18 = (bf16[1,2560,768]{2,1,0:T(8,128)(2,1)S(1)}, bf16[1,2560,768]{2,1,0:T(8,128)(2,1)}, u32[]{:S(2)}) copy-start(bf16[1,2560,768]{2,1,0:T(8,128)(2,1)} %param.16) | copy-start | bytes 11796484
  91.8 22.5 %collective-permute-start.2 = (bf16[320,768]{1,0:T(8,128)(2,1)}, bf16[320,768]{1,0:T(8,128)(2,1)}, u32[]{:S(2)}, u32[]{:S(2)}) collective-permute-start(bf16[320,768]{1,0:T(8,128)(2,1)} %fusion.38), channel_id=1, source_target_pairs={{0,1},{1,0},{2,3},{3,2},{4,5},{5,4},{6,7},{7,6},{8,9},{9,8},{10,11... | collective-permute-start | bytes 1474568 | tf_op jit(solution)/shard_map/ppermute | solution.py:92
  94.6 2.9 %copy-start.1 = (bf16[1,1536,1280]{2,1,0:T(8,128)(2,1)S(1)}, bf16[1,1536,1280]{2,1,0:T(8,128)(2,1)}, u32[]{:S(2)}) copy-start(bf16[1,1536,1280]{2,1,0:T(8,128)(2,1)} %param.18) | copy-start | bytes 11796484
  97.3 3.3 %collective-permute-start.5 = (bf16[256,768]{1,0:T(8,128)(2,1)S(1)}, bf16[256,768]{1,0:T(8,128)(2,1)S(1)}, u32[]{:S(2)}, u32[]{:S(2)}) collective-permute-start(bf16[256,768]{1,0:T(8,128)(2,1)S(1)} %multiply_convert_fusion.1), channel_id=1, source_target_pairs={{0,1},{1,0},{2,3},{3,2},{4,5},{5,4},{6,7},{7,6},{8,9},{9,8},{10,11... | collective-permute-start | bytes 1179656 | tf_op jit(solution)/shard_map/ppermute | solution.py:94
  100.0 6.3 %collective-permute-start.7 = (bf16[256,1280]{1,0:T(8,128)(2,1)S(1)}, bf16[256,1280]{1,0:T(8,128)(2,1)S(1)}, u32[]{:S(2)}, u32[]{:S(2)}) collective-permute-start(bf16[256,1280]{1,0:T(8,128)(2,1)S(1)} %fusion.19), channel_id=1, source_target_pairs={{0,1},{1,0},{2,3},{3,2},{4,5},{5,4},{6,7},{7,6},{8,9},{9,8},{10,11... | collective-permute-start | bytes 1966088 | tf_op jit(solution)/shard_map/ppermute | solution.py:96
  104.2 2.0 %copy-start.11 = (bf16[320,768]{1,0:T(8,128)(2,1)}, bf16[320,768]{1,0:T(8,128)(2,1)S(1)}, u32[]{:S(2)}) copy-start(bf16[320,768]{1,0:T(8,128)(2,1)S(1)} %multiply_convert_fusion) | copy-start | bytes 1474564
  108.8 5.5 %copy-start.7 = (f32[320,1280]{1,0:T(8,128)S(1)}, f32[320,1280]{1,0:T(8,128)}, u32[]{:S(2)}) copy-start(f32[320,1280]{1,0:T(8,128)} %fusion.28) | copy-start | bytes 4915204
  108.8 27.4 %all-to-all-start.4 = ((bf16[64,80,128]{2,1,0:T(8,128)(2,1)}), bf16[64,80,128]{2,1,0:T(8,128)(2,1)S(1)}, u32[]{:S(2)}, u32[]{:S(2)}) async-start(bf16[64,80,128]{2,1,0:T(8,128)(2,1)} %reshape.115), calls=%async_computation.4 | async-start | bytes 2621440 | tf_op jit(solution)/shard_map/all_to_all | solution.py:25
  114.2 2.8 %copy-start.12 = (bf16[320,768]{1,0:T(8,128)(2,1)S(1)}, bf16[320,768]{1,0:T(8,128)(2,1)}, u32[]{:S(2)}) copy-start(bf16[320,768]{1,0:T(8,128)(2,1)} %copy-done.11) | copy-start | bytes 1474564
  114.2 3.3 %copy-start.2 = (bf16[1,1536,1280]{2,1,0:T(8,128)(2,1)S(1)}, bf16[1,1536,1280]{2,1,0:T(8,128)(2,1)}, u32[]{:S(2)}) copy-start(bf16[1,1536,1280]{2,1,0:T(8,128)(2,1)} %param.18) | copy-start | bytes 11796484
  116.9 3.9 %collective-permute-start.3 = (bf16[320,1280]{1,0:T(8,128)(2,1)S(1)}, bf16[320,1280]{1,0:T(8,128)(2,1)S(1)}, u32[]{:S(2)}, u32[]{:S(2)}) collective-permute-start(bf16[320,1280]{1,0:T(8,128)(2,1)S(1)} %fusion.17), channel_id=1, source_target_pairs={{0,1},{1,0},{2,3},{3,2},{4,5},{5,4},{6,7},{7,6},{8,9},{9,8},{10,11... | collective-permute-start | bytes 2457608 | tf_op jit(solution)/shard_map/ppermute | solution.py:96
  117.0 3.0 %collective-permute-start.1 = (bf16[320,768]{1,0:T(8,128)(2,1)S(1)}, bf16[320,768]{1,0:T(8,128)(2,1)S(1)}, u32[]{:S(2)}, u32[]{:S(2)}) collective-permute-start(bf16[320,768]{1,0:T(8,128)(2,1)S(1)} %copy-done.12), channel_id=1, source_target_pairs={{0,1},{1,0},{2,3},{3,2},{4,5},{5,4},{6,7},{7,6},{8,9},{9,8},{10,11... | collective-permute-start | bytes 1474568 | tf_op jit(solution)/shard_map/ppermute | solution.py:94
  136.2 30.2 %all-to-all-start.2 = ((bf16[64,100,128]{2,1,0:T(8,128)(2,1)}), bf16[64,100,128]{2,1,0:T(8,128)(2,1)S(1)}, u32[]{:S(2)}, u32[]{:S(2)}) async-start(bf16[64,100,128]{2,1,0:T(8,128)(2,1)} %reshape.109), calls=%async_computation.2 | async-start | bytes 3407872 | tf_op jit(solution)/shard_map/all_to_all | solution.py:25
  168.2 1.3 copy-start.3
  168.2 1.3 copy-start.10
  169.5 1.0 copy-start.5
  170.7 1.3 copy-start.8
  (2 other events, 1.5 us)

commit v4 on v2

--- a/solution.py
+++ b/solution.py
@@ -44,21 +44,18 @@
     row_width = residual.shape[1]
     part_cols = out_weight.shape[1]
     capacity = max(2, 3 * tok_rows * top_picks // (2 * experts))
-    columns = jnp.dot(
-        lax.all_gather(attention_out, "dp", axis=0, tiled=True),
-        out_weight,
-        preferred_element_type=jnp.float32,
+    swap = [(0, 1), (1, 0)]
+    me = lax.axis_index("dp")
+    partner_att = lax.ppermute(attention_out, "dp", swap)
+    cols_own = jnp.dot(attention_out, out_weight, preferred_element_type=jnp.float32)
+    cols_partner = jnp.dot(partner_att, out_weight, preferred_element_type=jnp.float32)
+    cols_in = lax.ppermute(cols_partner.astype(jnp.bfloat16), "dp", swap).astype(jnp.float32)
+    home_cols = jnp.where(
+        me == 0,
+        jnp.concatenate([cols_own, cols_in], axis=1),
+        jnp.concatenate([cols_in, cols_own], axis=1),
     )
-    home_cols = lax.all_to_all(
-        columns.reshape(groups, tok_rows, part_cols).astype(jnp.bfloat16),
-        "dp",
-        split_axis=0,
-        concat_axis=2,
-        tiled=True,
-    ).astype(jnp.float32)
-    summed = (residual.astype(jnp.float32) + home_cols.reshape(tok_rows, row_width)).astype(
-        jnp.bfloat16
-    )
+    summed = (residual.astype(jnp.float32) + home_cols).astype(jnp.bfloat16)
     normed_in = rms_scale(summed, pre_gain).astype(jnp.bfloat16)
     slot_ids = slot_table(routes, experts, capacity)
     matches = (
@@ -73,7 +70,6 @@
     gate_local = gate_weight[0]
     up_local = up_weight[0]
     down_local = down_weight[0]
-    swap = [(0, 1), (1, 0)]
     own_rows = exchange_rows(outgoing, experts)
     other_rows = lax.ppermute(own_rows, "dp", swap)
 
@@ -101,10 +97,11 @@
     out_other_in = lax.ppermute(out_other, "dp", swap)
     out_own = project(hidden_own, hidden_other_in)
     joined = jnp.concatenate([out_own, out_other_in], axis=1)
-    returned = exchange_rows(joined, experts).astype(jnp.float32)
-    expert_sum = jnp.dot(
-        mixing, returned, precision=lax.Precision.HIGHEST, preferred_element_type=jnp.float32
-    )
+    returned = exchange_rows(joined, experts)
+    mixing_hi = mixing.astype(jnp.bfloat16)
+    mixing_lo = (mixing - mixing_hi.astype(jnp.float32)).astype(jnp.bfloat16)
+    expert_sum = jnp.dot(mixing_hi, returned, preferred_element_type=jnp.float32)
+    expert_sum = expert_sum + jnp.dot(mixing_lo, returned, preferred_element_type=jnp.float32)
     expert_sum = jnp.where(me == 0, expert_sum, jnp.roll(expert_sum, part_cols, axis=1))
     new_state = (summed.astype(jnp.float32) + expert_sum).astype(jnp.bfloat16)
     normed_state = rms_scale(new_state, post_gain).astype(jnp.bfloat16)

time: 164 us -> 164 us (level)
  blocking collectives: 54.5 us -> 97 us
  waiting for transfers between devices: 43.3 us -> 3.47 us
  starting transfers between devices: 9.89 us -> 2.07 us
    all_to_all x1 -> x2, blocking collectives: 52 us -> 97 us  [exchange_rows(): moved = lax.all_to_all(wire, 'ep', split_axis=0, concat_axis=0, tiled=True)]
    all_to_all x2 -> x0, waiting for transfers between devices: 40.6 us -> none  [the longest x1 40.6 us: exchange_rows(): moved = lax.all_to_all(wire, 'ep', split_axis=0, concat_axis=0, tiled=True)]
    all_to_all x2 -> x0, starting transfers between devices: 8.48 us -> none  [the longest x1 4.89 us: exchange_rows(): moved = lax.all_to_all(wire, 'ep', split_axis=0, concat_axis=0, tiled=True)]
    all_gather x1 -> x0, blocking collectives: 2.49 us -> none  [per_device(): lax.all_gather(attention_out, 'dp', axis=0, tiled=True)]
    dot_general x2 -> x4, matrix products: 8.22 us -> 9.73 us  [the longest x1 4.24 us: per_device(): jnp.dot(attention_out, out_weight, preferred_element_type=jnp.float32)]
  transfers between devices with their start and end apart: 6 -> 6, of which waited for: 2 -> 2; matrix products, arithmetic and copies ran while one was open for 13% -> 17% of each run, Pallas kernels for 0% -> 0%
where the time goes in v4:
time: 164 us; the launch traced here: 163 us
  blocking collectives  97 us (59%)
  matrix products  33.8 us (21%)
  local copies, waits for them, and re-layouts  21.2 us (13%)
  other arithmetic  4.54 us (3%)
  waiting for transfers between devices  3.47 us (2%)
  starting transfers between devices  2.07 us (1%)
    all_to_all x2, blocking collectives, exchange_rows(): moved = lax.all_to_all(wire, 'ep', split_axis=0, concat_axis=0, tiled=True)  97 us
    reshape x2, local copies, waits for them, and re-layouts, exchange_rows(): wire = rows.reshape(experts, total * width // (experts * lanes), lanes)  10.1 us
    reshape x2, local copies, waits for them, and re-layouts, exchange_rows(): return moved.reshape(total, width)  9.54 us
    dot_general x2, matrix products, hidden_of(): gate_part = jnp.dot(rows, gate_local, preferred_element_type=jnp.float32)  8.99 us
    dot_general x2, matrix products, hidden_of(): up_part = jnp.dot(rows, up_local, preferred_element_type=jnp.float32)  7.17 us
    dot_general x1, matrix products, per_device(): jnp.dot(attention_out, out_weight, preferred_element_type=jnp.float32)  4.24 us
    dot_general x1, matrix products, per_device(): jnp.dot(partner_att, out_weight, preferred_element_type=jnp.float32)  4.15 us
  transfers between devices with their start and end apart: 6, of which 2 were waited for; matrix products, arithmetic and copies ran while one was open for 17% of the time, Pallas kernels for 0%

profile of v4, /device:TPU:0, one launch (start us, length us, event | category | flops | bytes accessed | tf_op | source)
XLA Modules:
  0.0 163.0 jit_solution(8737102779515670186)
XLA Ops:
  0.7 0.8 copy.26
  1.8 4.2 %fusion.49 = f32[64,1280]{1,0:T(8,128)S(1)} fusion(bf16[64,2560]{1,0:T(8,128)(2,1)} %param.10, bf16[2560,1280]{1,0:T(8,128)(2,1)} %param.12), kind=kOutput, calls=%fused_computation.72 | convolution fusion | flops 419430400 | bytes 7208960 | tf_op jit(solution)/shard_map/dot_general | solution.py:50
  6.1 0.9 reduce-window.6
  7.0 0.2 slice_reduce_fusion
  7.7 4.2 %convolution_convert_fusion.1 = bf16[64,1280]{1,0:T(8,128)(2,1)S(1)} fusion(bf16[64,2560]{1,0:T(8,128)(2,1)S(1)} %collective-permute-done, bf16[2560,1280]{1,0:T(8,128)(2,1)} %param.12), kind=kOutput, calls=%fused_computation.15 | convolution fusion | flops 419512320 | bytes 7045120 | tf_op jit(solution)/shard_map/dot_general | solution.py:51
  11.8 0.6 collective-permute-start.1
  12.4 0.3 select_reduce_fusion
  12.7 0.8 collective-permute-done.1
  13.5 0.2 fusion.25
  13.7 2.6 %convolution_convert_fusion = bf16[576,2560]{1,0:T(8,128)(2,1)} fusion(bf16[64,2560]{1,0:T(8,128)(2,1)S(1)} %get-tuple-element.7, f32[2560]{0:T(1024)S(1)} %copy-done.4, f32[64]{0:T(128)S(1)} %add_rsqrt_fusion.1, bf16[64,576]{1,0:T(8,128)(2,1)S(1)} %get-tuple-element.3), kind=kOutput, calls=%fused_computation | convolution fusion | flops 190873600 | bytes 3361024 | tf_op jit(solution)/shard_map/dot_general | solution.py:67
  16.3 5.1 %reshape.63 = bf16[64,180,128]{2,1,0:T(8,128)(2,1)S(1)} reshape(bf16[576,2560]{1,0:T(8,128)(2,1)} %convolution_convert_fusion) | data formatting | bytes 5898240 | tf_op jit(solution)/shard_map/reshape | solution.py:24
  21.3 51.9 %all_to_all.10 = bf16[64,180,128]{2,1,0:T(8,128)(2,1)} all-to-all(bf16[64,180,128]{2,1,0:T(8,128)(2,1)S(1)} %reshape.63), channel_id=1, replica_groups=mesh['ep'=64,'dp'=2] {'ep'}, dimensions={0} | all-to-all | bytes 5898240 | tf_op jit(solution)/shard_map/all_to_all | solution.py:25
  73.3 4.8 %reshape.64 = bf16[576,2560]{1,0:T(8,128)(2,1)S(1)} reshape(bf16[64,180,128]{2,1,0:T(8,128)(2,1)} %all_to_all.10) | data formatting | bytes 5898240 | tf_op jit(solution)/shard_map/reshape | solution.py:26
  78.2 4.7 %fusion.6 = f32[576,768]{1,0:T(8,128)S(1)} fusion(bf16[576,2560]{1,0:T(8,128)(2,1)S(1)} %reshape.64, bf16[1,2560,768]{2,1,0:T(8,128)(2,1)} %param.16), kind=kOutput, calls=%fused_computation.7 | convolution fusion | flops 2264924160 | bytes 8650752 | tf_op jit(solution)/shard_map/dot_general | solution.py:77
  82.9 2.6 %multiply_convert_fusion.1 = bf16[576,768]{1,0:T(8,128)(2,1)S(1)} fusion(f32[576,768]{1,0:T(8,128)S(1)} %fusion.6, bf16[576,2560]{1,0:T(8,128)(2,1)S(1)} %reshape.64, bf16[1,2560,768]{2,1,0:T(8,128)(2,1)S(1)} %copy-done.7), kind=kOutput, calls=%fused_computation.23 | convolution fusion | flops 2267578368 | bytes 9535488 | tf_op jit(solution)/shard_map/dot_general | solution.py:78
  85.5 0.7 collective-permute-start.4
  86.2 4.3 %fusion.4 = f32[576,768]{1,0:T(8,128)S(1)} fusion(bf16[576,2560]{1,0:T(8,128)(2,1)} %collective-permute-done.2, bf16[1,2560,768]{2,1,0:T(8,128)(2,1)S(1)} %copy-done.6), kind=kOutput, calls=%fused_computation.5 | convolution fusion | flops 2264924160 | bytes 8650752 | tf_op jit(solution)/shard_map/dot_general | solution.py:77
  90.5 4.6 %multiply_convert_fusion = bf16[576,768]{1,0:T(8,128)(2,1)S(1)} fusion(f32[576,768]{1,0:T(8,128)S(1)} %fusion.4, bf16[576,2560]{1,0:T(8,128)(2,1)} %collective-permute-done.2, bf16[1,2560,768]{2,1,0:T(8,128)(2,1)S(1)} %copy-done.7), kind=kOutput, calls=%fused_computation.22 | convolution fusion | flops 2267578368 | bytes 9535488 | tf_op jit(solution)/shard_map/dot_general | solution.py:78
  95.1 1.3 fusion.12
  96.5 1.3 fusion.9
  97.9 0.5 collective-permute-start.3
  98.4 1.3 fusion.14
  99.7 2.7 %collective-permute-done.3 = bf16[576,768]{1,0:T(8,128)(2,1)S(1)} collective-permute-done((bf16[576,768]{1,0:T(8,128)(2,1)S(1)}, bf16[576,768]{1,0:T(8,128)(2,1)S(1)}, u32[]{:S(2)}, u32[]{:S(2)}) %collective-permute-start.3) | collective-permute-done | bytes 884768 | tf_op jit(solution)/shard_map/ppermute | solution.py:84
  102.4 1.3 fusion.8
  103.8 1.8 %pad_maximum_fusion = bf16[576,2560]{1,0:T(8,128)(2,1)} fusion(bf16[576,1280]{1,0:T(8,128)(2,1)S(1)} %collective-permute-done.5, bf16[576,1280]{1,0:T(8,128)(2,1)S(1)} %fusion.8), kind=kLoop, calls=%fused_computation.14 | loop fusion | flops 5898240 | bytes 5898240 | tf_op jit(solution)/shard_map/concatenate | solution.py:99
  105.6 5.1 %reshape.65 = bf16[64,180,128]{2,1,0:T(8,128)(2,1)S(1)} reshape(bf16[576,2560]{1,0:T(8,128)(2,1)} %pad_maximum_fusion) | data formatting | bytes 5898240 | tf_op jit(solution)/shard_map/reshape | solution.py:24
  110.6 45.1 %all_to_all.11 = bf16[64,180,128]{2,1,0:T(8,128)(2,1)} all-to-all(bf16[64,180,128]{2,1,0:T(8,128)(2,1)S(1)} %reshape.65), channel_id=1, replica_groups=mesh['ep'=64,'dp'=2] {'ep'}, dimensions={0} | all-to-all | bytes 5898240 | tf_op jit(solution)/shard_map/all_to_all | solution.py:25
  155.7 4.8 %reshape.66 = bf16[576,2560]{1,0:T(8,128)(2,1)S(1)} reshape(bf16[64,180,128]{2,1,0:T(8,128)(2,1)} %all_to_all.11) | data formatting | bytes 5898240 | tf_op jit(solution)/shard_map/reshape | solution.py:26
  160.5 0.7 fusion.40
  161.2 0.7 convolution_add_fusion
  161.9 0.2 fusion.22
  162.2 0.9 fusion.24
  (39 shorter events, 1.1 us)
Async XLA Ops:
  0.6 7.0 %collective-permute-start = (bf16[64,2560]{1,0:T(8,128)(2,1)}, bf16[64,2560]{1,0:T(8,128)(2,1)S(1)}, u32[]{:S(2)}, u32[]{:S(2)}) collective-permute-start(bf16[64,2560]{1,0:T(8,128)(2,1)} %param.10), channel_id=1, source_target_pairs={{0,1},{1,0},{2,3},{3,2},{4,5},{5,4},{6,7},{7,6},{8,9},{9,8},{10,11... | collective-permute-start | bytes 983048 | tf_op jit(solution)/shard_map/ppermute | solution.py:49
  1.8 5.8 %copy-start.3 = (f32[64,6]{0,1:T(8,128)S(1)}, f32[64,6]{0,1:T(8,128)}, u32[]{:S(2)}) copy-start(f32[64,6]{0,1:T(8,128)} %param.15) | copy-start | bytes 4612
  1.8 5.8 %copy-start.2 = (s32[64,6]{0,1:T(8,128)S(1)}, s32[64,6]{0,1:T(8,128)}, u32[]{:S(2)}) copy-start(s32[64,6]{0,1:T(8,128)} %param.14) | copy-start | bytes 4612
  7.6 5.8 %copy-start.1 = (bf16[64,2560]{1,0:T(8,128)(2,1)S(1)}, bf16[64,2560]{1,0:T(8,128)(2,1)}, u32[]{:S(2)}) copy-start(bf16[64,2560]{1,0:T(8,128)(2,1)} %param.11) | copy-start | bytes 983044
  7.6 6.0 %copy-start.4 = (f32[2560]{0:T(1024)S(1)}, f32[2560]{0:T(1024)}, u32[]{:S(2)}) copy-start(f32[2560]{0:T(1024)} %param.13) | copy-start | bytes 30724
  11.8 1.6 collective-permute-start.1
  78.0 8.2 %collective-permute-start.2 = (bf16[576,2560]{1,0:T(8,128)(2,1)S(1)}, bf16[576,2560]{1,0:T(8,128)(2,1)}, u32[]{:S(2)}, u32[]{:S(2)}) collective-permute-start(bf16[576,2560]{1,0:T(8,128)(2,1)S(1)} %reshape.64), channel_id=1, source_target_pairs={{0,1},{1,0},{2,3},{3,2},{4,5},{5,4},{6,7},{7,6},{8,9},{9,8},{10,11... | collective-permute-start | bytes 8847368 | tf_op jit(solution)/shard_map/ppermute | solution.py:74
  78.1 4.7 %copy-start.7 = (bf16[1,2560,768]{2,1,0:T(8,128)(2,1)S(1)}, bf16[1,2560,768]{2,1,0:T(8,128)(2,1)}, u32[]{:S(2)}) copy-start(bf16[1,2560,768]{2,1,0:T(8,128)(2,1)} %param.17) | copy-start | bytes 11796484
  82.9 3.4 %copy-start.6 = (bf16[1,2560,768]{2,1,0:T(8,128)(2,1)S(1)}, bf16[1,2560,768]{2,1,0:T(8,128)(2,1)}, u32[]{:S(2)}) copy-start(bf16[1,2560,768]{2,1,0:T(8,128)(2,1)} %param.16) | copy-start | bytes 11796484
  85.5 11.0 %collective-permute-start.4 = (bf16[576,768]{1,0:T(8,128)(2,1)S(1)}, bf16[576,768]{1,0:T(8,128)(2,1)S(1)}, u32[]{:S(2)}, u32[]{:S(2)}) collective-permute-start(bf16[576,768]{1,0:T(8,128)(2,1)S(1)} %multiply_convert_fusion.1), channel_id=1, source_target_pairs={{0,1},{1,0},{2,3},{3,2},{4,5},{5,4},{6,7},{7,6},{8,9},{9,8},{10,11... | collective-permute-start | bytes 2654216 | tf_op jit(solution)/shard_map/ppermute | solution.py:82
  90.5 4.6 %copy-start.8 = (bf16[1,1536,1280]{2,1,0:T(8,128)(2,1)S(1)}, bf16[1,1536,1280]{2,1,0:T(8,128)(2,1)}, u32[]{:S(2)}) copy-start(bf16[1,1536,1280]{2,1,0:T(8,128)(2,1)} %param.18) | copy-start | bytes 11796484
  97.8 5.9 %collective-permute-start.5 = (bf16[576,1280]{1,0:T(8,128)(2,1)S(1)}, bf16[576,1280]{1,0:T(8,128)(2,1)S(1)}, u32[]{:S(2)}, u32[]{:S(2)}) collective-permute-start(bf16[576,1280]{1,0:T(8,128)(2,1)S(1)} %fusion.9), channel_id=1, source_target_pairs={{0,1},{1,0},{2,3},{3,2},{4,5},{5,4},{6,7},{7,6},{8,9},{9,8},{10,11... | collective-permute-start | bytes 4423688 | tf_op jit(solution)/shard_map/ppermute | solution.py:97
  97.9 4.5 %collective-permute-start.3 = (bf16[576,768]{1,0:T(8,128)(2,1)S(1)}, bf16[576,768]{1,0:T(8,128)(2,1)S(1)}, u32[]{:S(2)}, u32[]{:S(2)}) collective-permute-start(bf16[576,768]{1,0:T(8,128)(2,1)S(1)} %multiply_convert_fusion), channel_id=1, source_target_pairs={{0,1},{1,0},{2,3},{3,2},{4,5},{5,4},{6,7},{7,6},{8,9},{9,8},{10,11... | collective-permute-start | bytes 2654216 | tf_op jit(solution)/shard_map/ppermute | solution.py:84
  161.2 1.0 copy-start.5
  162.1 0.9 copy-start

commit v5 on v4

--- a/solution.py
+++ b/solution.py
@@ -24,6 +24,17 @@
     wire = rows.reshape(experts, total * width // (experts * lanes), lanes)
     moved = lax.all_to_all(wire, "ep", split_axis=0, concat_axis=0, tiled=True)
     return moved.reshape(total, width)
+
+
+def return_rows(first, second, experts):
+    total, width = first.shape
+    lanes = 128
+    cut = total * width // (experts * lanes)
+    wire = jnp.zeros((experts, 2 * cut, lanes), first.dtype)
+    wire = wire.at[:, :cut].set(first.reshape(experts, cut, lanes))
+    wire = wire.at[:, cut:].set(second.reshape(experts, cut, lanes))
+    moved = lax.all_to_all(wire, "ep", split_axis=0, concat_axis=0, tiled=True)
+    return [moved[:, :cut].reshape(total, width), moved[:, cut:].reshape(total, width)]
 
 
 def per_device(
@@ -96,12 +107,14 @@
     out_other = project(hidden_other, hidden_own_in)
     out_other_in = lax.ppermute(out_other, "dp", swap)
     out_own = project(hidden_own, hidden_other_in)
-    joined = jnp.concatenate([out_own, out_other_in], axis=1)
-    returned = exchange_rows(joined, experts)
+    returned = return_rows(out_own, out_other_in, experts)
     mixing_hi = mixing.astype(jnp.bfloat16)
     mixing_lo = (mixing - mixing_hi.astype(jnp.float32)).astype(jnp.bfloat16)
-    expert_sum = jnp.dot(mixing_hi, returned, preferred_element_type=jnp.float32)
-    expert_sum = expert_sum + jnp.dot(mixing_lo, returned, preferred_element_type=jnp.float32)
+    sums = []
+    for half in returned:
+        total = jnp.dot(mixing_hi, half, preferred_element_type=jnp.float32)
+        sums.append(total + jnp.dot(mixing_lo, half, preferred_element_type=jnp.float32))
+    expert_sum = jnp.concatenate(sums, axis=1)
     expert_sum = jnp.where(me == 0, expert_sum, jnp.roll(expert_sum, part_cols, axis=1))
     new_state = (summed.astype(jnp.float32) + expert_sum).astype(jnp.bfloat16)
     normed_state = rms_scale(new_state, post_gain).astype(jnp.bfloat16)

time: 164 us -> 167 us (1.018)
  local copies, waits for them, and re-layouts: 21.2 us -> 23.9 us
  matrix products: 33.8 us -> 35.7 us
    all_to_all x0 -> x1, blocking collectives: none -> 45.2 us  [return_rows(): moved = lax.all_to_all(wire, 'ep', split_axis=0, concat_axis=0, tiled=True)]
    all_to_all x2 -> x1, blocking collectives: 97 us -> 51.9 us  [exchange_rows(): moved = lax.all_to_all(wire, 'ep', split_axis=0, concat_axis=0, tiled=True)]
    reshape x2 -> x1, local copies, waits for them, and re-layouts: 10.1 us -> 5.06 us  [exchange_rows(): wire = rows.reshape(experts, total * width // (experts * lanes), lanes)]
    another operation x1 -> x3, local copies, waits for them, and re-layouts: 0.22 us -> 5.13 us
    reshape x0 -> x2, local copies, waits for them, and re-layouts: none -> 4.87 us  [the longest x1 3.16 us: return_rows(): moved[:, :cut].reshape(total, width)]
    reshape x2 -> x1, local copies, waits for them, and re-layouts: 9.54 us -> 4.77 us  [exchange_rows(): return moved.reshape(total, width)]
    concatenate x1 -> x0, other arithmetic: 1.82 us -> none  [per_device(): joined = jnp.concatenate([out_own, out_other_in], axis=1)]
where the time goes in v5:
time: 167 us; the launch traced here: 166 us
  blocking collectives  97.1 us (58%)
  matrix products  35.7 us (21%)
  local copies, waits for them, and re-layouts  23.9 us (14%)
  other arithmetic  3.45 us (2%)
  waiting for transfers between devices  3.15 us (2%)
  starting transfers between devices  1.99 us (1%)
    all_to_all x1, blocking collectives, exchange_rows(): moved = lax.all_to_all(wire, 'ep', split_axis=0, concat_axis=0, tiled=True)  51.9 us
    all_to_all x1, blocking collectives, return_rows(): moved = lax.all_to_all(wire, 'ep', split_axis=0, concat_axis=0, tiled=True)  45.2 us
    dot_general x2, matrix products, hidden_of(): gate_part = jnp.dot(rows, gate_local, preferred_element_type=jnp.float32)  8.99 us
    dot_general x2, matrix products, hidden_of(): up_part = jnp.dot(rows, up_local, preferred_element_type=jnp.float32)  7.14 us
    another operation x3, local copies, waits for them, and re-layouts  5.13 us
    reshape x1, local copies, waits for them, and re-layouts, exchange_rows(): wire = rows.reshape(experts, total * width // (experts * lanes), lanes)  5.06 us
    reshape x1, local copies, waits for them, and re-layouts, exchange_rows(): return moved.reshape(total, width)  4.77 us
    dot_general x1, matrix products, per_device(): jnp.dot(attention_out, out_weight, preferred_element_type=jnp.float32)  4.24 us
  transfers between devices with their start and end apart: 6, of which 2 were waited for; matrix products, arithmetic and copies ran while one was open for 17% of the time, Pallas kernels for 0%

profile of v5, /device:TPU:0, one launch (start us, length us, event | category | flops | bytes accessed | tf_op | source)
XLA Modules:
  0.0 166.3 jit_solution(3538367877320226952)
XLA Ops:
  0.7 0.8 copy.26
  1.8 4.2 %fusion.50 = f32[64,1280]{1,0:T(8,128)S(1)} fusion(bf16[64,2560]{1,0:T(8,128)(2,1)} %param.14, bf16[2560,1280]{1,0:T(8,128)(2,1)} %param.16), kind=kOutput, calls=%fused_computation.74 | convolution fusion | flops 419430400 | bytes 7208960 | tf_op jit(solution)/shard_map/dot_general | solution.py:61
  6.1 0.9 reduce-window.6
  7.7 4.2 %convolution_convert_fusion.1 = bf16[64,1280]{1,0:T(8,128)(2,1)S(1)} fusion(bf16[64,2560]{1,0:T(8,128)(2,1)S(1)} %collective-permute-done, bf16[2560,1280]{1,0:T(8,128)(2,1)} %param.16), kind=kOutput, calls=%fused_computation.16 | convolution fusion | flops 419512320 | bytes 7045120 | tf_op jit(solution)/shard_map/dot_general | solution.py:62
  11.8 0.6 collective-permute-start.1
  12.7 0.8 collective-permute-done.1
  13.7 0.7 copy-done
  14.4 2.6 %convolution_convert_fusion = bf16[576,2560]{1,0:T(8,128)(2,1)} fusion(bf16[64,2560]{1,0:T(8,128)(2,1)S(1)} %get-tuple-element.31, f32[2560]{0:T(1024)S(1)} %copy-done.7, f32[64]{0:T(128)S(1)} %add_rsqrt_fusion.1, bf16[64,576]{1,0:T(8,128)(2,1)S(1)} %get-tuple-element.27), kind=kOutput, calls=%fused_computation | convolution fusion | flops 190873600 | bytes 3361024 | tf_op jit(solution)/shard_map/dot_general | solution.py:78
  17.0 5.1 %reshape.129 = bf16[64,180,128]{2,1,0:T(8,128)(2,1)S(1)} reshape(bf16[576,2560]{1,0:T(8,128)(2,1)} %convolution_convert_fusion) | data formatting | bytes 5898240 | tf_op jit(solution)/shard_map/reshape | solution.py:24
  22.1 51.9 %all_to_all.10 = bf16[64,180,128]{2,1,0:T(8,128)(2,1)} all-to-all(bf16[64,180,128]{2,1,0:T(8,128)(2,1)S(1)} %reshape.129), channel_id=1, replica_groups=mesh['ep'=64,'dp'=2] {'ep'}, dimensions={0} | all-to-all | bytes 5898240 | tf_op jit(solution)/shard_map/all_to_all | solution.py:25
  74.0 4.8 %reshape.130 = bf16[576,2560]{1,0:T(8,128)(2,1)S(1)} reshape(bf16[64,180,128]{2,1,0:T(8,128)(2,1)} %all_to_all.10) | data formatting | bytes 5898240 | tf_op jit(solution)/shard_map/reshape | solution.py:26
  78.9 4.7 %fusion.6 = f32[576,768]{1,0:T(8,128)S(1)} fusion(bf16[576,2560]{1,0:T(8,128)(2,1)S(1)} %reshape.130, bf16[1,2560,768]{2,1,0:T(8,128)(2,1)} %param.20), kind=kOutput, calls=%fused_computation.7 | convolution fusion | flops 2264924160 | bytes 8650752 | tf_op jit(solution)/shard_map/dot_general | solution.py:88
  83.6 2.6 %multiply_convert_fusion.1 = bf16[576,768]{1,0:T(8,128)(2,1)S(1)} fusion(f32[576,768]{1,0:T(8,128)S(1)} %fusion.6, bf16[576,2560]{1,0:T(8,128)(2,1)S(1)} %reshape.130, bf16[1,2560,768]{2,1,0:T(8,128)(2,1)S(1)} %copy-done.10), kind=kOutput, calls=%fused_computation.24 | convolution fusion | flops 2267578368 | bytes 9535488 | tf_op jit(solution)/shard_map/dot_general | solution.py:89
  86.2 0.7 collective-permute-start.4
  86.9 4.3 %fusion.4 = f32[576,768]{1,0:T(8,128)S(1)} fusion(bf16[576,2560]{1,0:T(8,128)(2,1)} %collective-permute-done.2, bf16[1,2560,768]{2,1,0:T(8,128)(2,1)S(1)} %copy-done.9), kind=kOutput, calls=%fused_computation.5 | convolution fusion | flops 2264924160 | bytes 8650752 | tf_op jit(solution)/shard_map/dot_general | solution.py:88
  91.2 4.6 %multiply_convert_fusion = bf16[576,768]{1,0:T(8,128)(2,1)S(1)} fusion(f32[576,768]{1,0:T(8,128)S(1)} %fusion.4, bf16[576,2560]{1,0:T(8,128)(2,1)} %collective-permute-done.2, bf16[1,2560,768]{2,1,0:T(8,128)(2,1)S(1)} %copy-done.10), kind=kOutput, calls=%fused_computation.23 | convolution fusion | flops 2267578368 | bytes 9535488 | tf_op jit(solution)/shard_map/dot_general | solution.py:89
  95.8 1.3 fusion.12
  97.1 2.5 %fusion.9 = bf16[576,1280]{1,0:T(8,128)(2,1)} fusion(f32[576,1280]{1,0:T(8,128)S(1)} %fusion.12, bf16[576,768]{1,0:T(8,128)(2,1)S(1)} %collective-permute-done.4, bf16[1,1536,1280]{2,1,0:T(8,128)(2,1)S(1)} %copy-done.11, s32[]{:T(128)S(6)} %select_n.21), kind=kOutput, calls=%fused_computation.12 | convolution fusion | flops 1133936640 | bytes 7274500 | tf_op jit(solution)/shard_map/dot_general | solution.py:104
  99.6 0.5 collective-permute-start.3
  100.1 1.3 fusion.14
  101.4 2.4 %collective-permute-done.3 = bf16[576,768]{1,0:T(8,128)(2,1)S(1)} collective-permute-done((bf16[576,768]{1,0:T(8,128)(2,1)S(1)}, bf16[576,768]{1,0:T(8,128)(2,1)S(1)}, u32[]{:S(2)}, u32[]{:S(2)}) %collective-permute-start.3) | collective-permute-done | bytes 884768 | tf_op jit(solution)/shard_map/ppermute | solution.py:95
  103.8 1.3 fusion.8
  105.1 1.7 %reshape.131 = bf16[64,90,128]{2,1,0:T(8,128)(2,1)S(1)} reshape(bf16[576,1280]{1,0:T(8,128)(2,1)S(1)} %fusion.8) | data formatting | bytes 2949120 | tf_op jit(solution)/shard_map/reshape.47
  106.9 3.2 %reshape.132 = bf16[64,90,128]{2,1,0:T(8,128)(2,1)S(1)} reshape(bf16[576,1280]{1,0:T(8,128)(2,1)} %collective-permute-done.5) | data formatting | bytes 2949120 | tf_op jit(solution)/shard_map/reshape.57
  110.1 0.7 pad_maximum_fusion
  110.8 45.2 %all_to_all.11 = bf16[64,180,128]{2,1,0:T(8,128)(2,1)S(1)} all-to-all(bf16[64,180,128]{2,1,0:T(8,128)(2,1)S(1)} %pad_maximum_fusion), channel_id=1, replica_groups=mesh['ep'=64,'dp'=2] {'ep'}, dimensions={0} | all-to-all | bytes 5898240 | tf_op jit(solution)/shard_map/all_to_all | solution.py:36
  156.0 1.7 %fusion.49 = (bf16[64,90,128]{2,1,0:T(8,128)(2,1)S(1)}, bf16[64,90,128]{2,1,0:T(8,128)(2,1)}) fusion(bf16[64,180,128]{2,1,0:T(8,128)(2,1)S(1)} %all_to_all.11), kind=kLoop, calls=%fused_computation.73 | loop fusion | bytes 5898240 | tf_op jit(solution)/shard_map/slice | solution.py:37
  157.7 3.2 %reshape.133 = bf16[576,1280]{1,0:T(8,128)(2,1)S(1)} reshape(bf16[64,90,128]{2,1,0:T(8,128)(2,1)} %get-tuple-element.33) | data formatting | bytes 2949120 | tf_op jit(solution)/shard_map/reshape | solution.py:37
  161.3 1.1 convolution_add_fusion.3
  162.4 1.7 %reshape.134 = bf16[576,1280]{1,0:T(8,128)(2,1)S(1)} reshape(bf16[64,90,128]{2,1,0:T(8,128)(2,1)S(1)} %get-tuple-element.32) | data formatting | bytes 2949120 | tf_op jit(solution)/shard_map/reshape | solution.py:37
  164.5 0.4 convolution_add_fusion.2
  165.4 0.9 fusion.24
  (49 shorter events, 2.9 us)
Async XLA Ops:
  0.6 7.0 %collective-permute-start = (bf16[64,2560]{1,0:T(8,128)(2,1)}, bf16[64,2560]{1,0:T(8,128)(2,1)S(1)}, u32[]{:S(2)}, u32[]{:S(2)}) collective-permute-start(bf16[64,2560]{1,0:T(8,128)(2,1)} %param.14), channel_id=1, source_target_pairs={{0,1},{1,0},{2,3},{3,2},{4,5},{5,4},{6,7},{7,6},{8,9},{9,8},{10,11... | collective-permute-start | bytes 983048 | tf_op jit(solution)/shard_map/ppermute | solution.py:60
  1.8 5.8 %copy-start.6 = (f32[64,6]{0,1:T(8,128)S(1)}, f32[64,6]{0,1:T(8,128)}, u32[]{:S(2)}) copy-start(f32[64,6]{0,1:T(8,128)} %param.19) | copy-start | bytes 4612
  1.8 5.8 %copy-start.5 = (s32[64,6]{0,1:T(8,128)S(1)}, s32[64,6]{0,1:T(8,128)}, u32[]{:S(2)}) copy-start(s32[64,6]{0,1:T(8,128)} %param.18) | copy-start | bytes 4612
  7.6 5.8 %copy-start.4 = (bf16[64,2560]{1,0:T(8,128)(2,1)S(1)}, bf16[64,2560]{1,0:T(8,128)(2,1)}, u32[]{:S(2)}) copy-start(bf16[64,2560]{1,0:T(8,128)(2,1)} %param.15) | copy-start | bytes 983044
  7.6 6.8 %copy-start.7 = (f32[2560]{0:T(1024)S(1)}, f32[2560]{0:T(1024)}, u32[]{:S(2)}) copy-start(f32[2560]{0:T(1024)} %param.17) | copy-start | bytes 30724
  11.8 1.6 collective-permute-start.1
  13.7 0.7 copy-start
  78.8 8.2 %collective-permute-start.2 = (bf16[576,2560]{1,0:T(8,128)(2,1)S(1)}, bf16[576,2560]{1,0:T(8,128)(2,1)}, u32[]{:S(2)}, u32[]{:S(2)}) collective-permute-start(bf16[576,2560]{1,0:T(8,128)(2,1)S(1)} %reshape.130), channel_id=1, source_target_pairs={{0,1},{1,0},{2,3},{3,2},{4,5},{5,4},{6,7},{7,6},{8,9},{9,8},{10,11... | collective-permute-start | bytes 8847368 | tf_op jit(solution)/shard_map/ppermute | solution.py:85
  78.9 4.7 %copy-start.10 = (bf16[1,2560,768]{2,1,0:T(8,128)(2,1)S(1)}, bf16[1,2560,768]{2,1,0:T(8,128)(2,1)}, u32[]{:S(2)}) copy-start(bf16[1,2560,768]{2,1,0:T(8,128)(2,1)} %param.21) | copy-start | bytes 11796484
  83.6 3.3 %copy-start.9 = (bf16[1,2560,768]{2,1,0:T(8,128)(2,1)S(1)}, bf16[1,2560,768]{2,1,0:T(8,128)(2,1)}, u32[]{:S(2)}) copy-start(bf16[1,2560,768]{2,1,0:T(8,128)(2,1)} %param.20) | copy-start | bytes 11796484
  86.2 10.9 %collective-permute-start.4 = (bf16[576,768]{1,0:T(8,128)(2,1)S(1)}, bf16[576,768]{1,0:T(8,128)(2,1)S(1)}, u32[]{:S(2)}, u32[]{:S(2)}) collective-permute-start(bf16[576,768]{1,0:T(8,128)(2,1)S(1)} %multiply_convert_fusion.1), channel_id=1, source_target_pairs={{0,1},{1,0},{2,3},{3,2},{4,5},{5,4},{6,7},{7,6},{8,9},{9,8},{10,11... | collective-permute-start | bytes 2654216 | tf_op jit(solution)/shard_map/ppermute | solution.py:93
  91.2 4.6 %copy-start.11 = (bf16[1,1536,1280]{2,1,0:T(8,128)(2,1)S(1)}, bf16[1,1536,1280]{2,1,0:T(8,128)(2,1)}, u32[]{:S(2)}) copy-start(bf16[1,1536,1280]{2,1,0:T(8,128)(2,1)} %param.22) | copy-start | bytes 11796484
  99.6 7.3 %collective-permute-start.5 = (bf16[576,1280]{1,0:T(8,128)(2,1)}, bf16[576,1280]{1,0:T(8,128)(2,1)}, u32[]{:S(2)}, u32[]{:S(2)}) collective-permute-start(bf16[576,1280]{1,0:T(8,128)(2,1)} %fusion.9), channel_id=1, source_target_pairs={{0,1},{1,0},{2,3},{3,2},{4,5},{5,4},{6,7},{7,6},{8,9},{9,8},{10,11... | collective-permute-start | bytes 4423688 | tf_op jit(solution)/shard_map/ppermute | solution.py:108
  99.6 4.2 %collective-permute-start.3 = (bf16[576,768]{1,0:T(8,128)(2,1)S(1)}, bf16[576,768]{1,0:T(8,128)(2,1)S(1)}, u32[]{:S(2)}, u32[]{:S(2)}) collective-permute-start(bf16[576,768]{1,0:T(8,128)(2,1)S(1)} %multiply_convert_fusion), channel_id=1, source_target_pairs={{0,1},{1,0},{2,3},{3,2},{4,5},{5,4},{6,7},{7,6},{8,9},{9,8},{10,11... | collective-permute-start | bytes 2654216 | tf_op jit(solution)/shard_map/ppermute | solution.py:95
  164.1 1.0 copy-start.1
  164.1 1.1 copy-start.2
  164.1 1.3 copy-start.8
  165.4 0.9 copy-start.3

commit v6 on v4

--- a/solution.py
+++ b/solution.py
@@ -47,8 +47,12 @@
     swap = [(0, 1), (1, 0)]
     me = lax.axis_index("dp")
     partner_att = lax.ppermute(attention_out, "dp", swap)
-    cols_own = jnp.dot(attention_out, out_weight, preferred_element_type=jnp.float32)
-    cols_partner = jnp.dot(partner_att, out_weight, preferred_element_type=jnp.float32)
+    cols = jnp.dot(
+        jnp.concatenate([attention_out, partner_att], axis=0),
+        out_weight,
+        preferred_element_type=jnp.float32,
+    )
+    cols_own, cols_partner = cols[:tok_rows], cols[tok_rows:]
     cols_in = lax.ppermute(cols_partner.astype(jnp.bfloat16), "dp", swap).astype(jnp.float32)
     home_cols = jnp.where(
         me == 0,

time: 164 us -> 161 us (0.982)
  matrix products: 33.8 us -> 29.4 us
    dot_general x2 -> x1, matrix products: 8.39 us -> 4.04 us  [per_device(): jnp.dot(jnp.concatenate([attention_out, partner_att], axis=0), out_weight...]
  transfers between devices with their start and end apart: 6 -> 6, of which waited for: 2 -> 2; matrix products, arithmetic and copies ran while one was open for 17% -> 15% of each run, Pallas kernels for 0% -> 0%
where the time goes in v6:
time: 161 us; the launch traced here: 160 us
  blocking collectives  97 us (60%)
  matrix products  29.4 us (18%)
  local copies, waits for them, and re-layouts  21.3 us (13%)
  other arithmetic  5.91 us (4%)
  waiting for transfers between devices  3.44 us (2%)
  starting transfers between devices  2.07 us (1%)
    all_to_all x2, blocking collectives, exchange_rows(): moved = lax.all_to_all(wire, 'ep', split_axis=0, concat_axis=0, tiled=True)  97 us
    reshape x2, local copies, waits for them, and re-layouts, exchange_rows(): wire = rows.reshape(experts, total * width // (experts * lanes), lanes)  10.1 us
    reshape x2, local copies, waits for them, and re-layouts, exchange_rows(): return moved.reshape(total, width)  9.54 us
    dot_general x2, matrix products, hidden_of(): gate_part = jnp.dot(rows, gate_local, preferred_element_type=jnp.float32)  8.99 us
    dot_general x2, matrix products, hidden_of(): up_part = jnp.dot(rows, up_local, preferred_element_type=jnp.float32)  7.17 us
    dot_general x1, matrix products, per_device(): jnp.dot(jnp.concatenate([attention_out, partner_att], axis=0), out_weight...  4.04 us
  transfers between devices with their start and end apart: 6, of which 2 were waited for; matrix products, arithmetic and copies ran while one was open for 15% of the time, Pallas kernels for 0%

profile of v6, /device:TPU:0, one launch (start us, length us, event | category | flops | bytes accessed | tf_op | source)
XLA Modules:
  0.0 160.0 jit_solution(15726849948839853403)
XLA Ops:
  0.7 0.8 copy.26
  1.8 0.9 reduce-window.6
  2.7 0.2 slice_reduce_fusion
  3.3 0.7 reduce_sum.58
  4.0 0.7 multiply_add_fusion
  4.7 4.0 %fusion.29 = f32[128,1280]{1,0:T(8,128)S(1)} fusion(bf16[2560,1280]{1,0:T(8,128)(2,1)} %param.12, bf16[64,2560]{1,0:T(8,128)(2,1)S(1)} %collective-permute-done, bf16[64,2560]{1,0:T(8,128)(2,1)} %param.10), kind=kOutput, calls=%fused_computation.42 | convolution fusion | flops 840171520 | bytes 7864320 | tf_op jit(solution)/shard_map/dot_general | solution.py:50
  8.8 0.6 collective-permute-start.1
  9.4 0.3 select_reduce_fusion
  9.7 0.7 collective-permute-done.1
  10.7 2.6 %convolution_convert_fusion = bf16[576,2560]{1,0:T(8,128)(2,1)} fusion(bf16[64,2560]{1,0:T(8,128)(2,1)S(1)} %get-tuple-element.7, f32[2560]{0:T(1024)S(1)} %copy-done.3, f32[64]{0:T(128)S(1)} %add_rsqrt_fusion.1, bf16[64,576]{1,0:T(8,128)(2,1)S(1)} %get-tuple-element.3), kind=kOutput, calls=%fused_computation | convolution fusion | flops 190873600 | bytes 3361024 | tf_op jit(solution)/shard_map/dot_general | solution.py:71
  13.3 5.1 %reshape.63 = bf16[64,180,128]{2,1,0:T(8,128)(2,1)S(1)} reshape(bf16[576,2560]{1,0:T(8,128)(2,1)} %convolution_convert_fusion) | data formatting | bytes 5898240 | tf_op jit(solution)/shard_map/reshape | solution.py:24
  18.3 51.9 %all_to_all.10 = bf16[64,180,128]{2,1,0:T(8,128)(2,1)} all-to-all(bf16[64,180,128]{2,1,0:T(8,128)(2,1)S(1)} %reshape.63), channel_id=1, replica_groups=mesh['ep'=64,'dp'=2] {'ep'}, dimensions={0} | all-to-all | bytes 5898240 | tf_op jit(solution)/shard_map/all_to_all | solution.py:25
  70.3 4.8 %reshape.64 = bf16[576,2560]{1,0:T(8,128)(2,1)S(1)} reshape(bf16[64,180,128]{2,1,0:T(8,128)(2,1)} %all_to_all.10) | data formatting | bytes 5898240 | tf_op jit(solution)/shard_map/reshape | solution.py:26
  75.2 4.7 %fusion.6 = f32[576,768]{1,0:T(8,128)S(1)} fusion(bf16[576,2560]{1,0:T(8,128)(2,1)S(1)} %reshape.64, bf16[1,2560,768]{2,1,0:T(8,128)(2,1)} %param.16), kind=kOutput, calls=%fused_computation.7 | convolution fusion | flops 2264924160 | bytes 8650752 | tf_op jit(solution)/shard_map/dot_general | solution.py:81
  79.9 2.6 %multiply_convert_fusion.1 = bf16[576,768]{1,0:T(8,128)(2,1)S(1)} fusion(f32[576,768]{1,0:T(8,128)S(1)} %fusion.6, bf16[576,2560]{1,0:T(8,128)(2,1)S(1)} %reshape.64, bf16[1,2560,768]{2,1,0:T(8,128)(2,1)S(1)} %copy-done.6), kind=kOutput, calls=%fused_computation.22 | convolution fusion | flops 2267578368 | bytes 9535488 | tf_op jit(solution)/shard_map/dot_general | solution.py:82
  82.5 0.7 collective-permute-start.4
  83.2 4.3 %fusion.4 = f32[576,768]{1,0:T(8,128)S(1)} fusion(bf16[576,2560]{1,0:T(8,128)(2,1)} %collective-permute-done.2, bf16[1,2560,768]{2,1,0:T(8,128)(2,1)S(1)} %copy-done.5), kind=kOutput, calls=%fused_computation.5 | convolution fusion | flops 2264924160 | bytes 8650752 | tf_op jit(solution)/shard_map/dot_general | solution.py:81
  87.5 4.6 %multiply_convert_fusion = bf16[576,768]{1,0:T(8,128)(2,1)S(1)} fusion(f32[576,768]{1,0:T(8,128)S(1)} %fusion.4, bf16[576,2560]{1,0:T(8,128)(2,1)} %collective-permute-done.2, bf16[1,2560,768]{2,1,0:T(8,128)(2,1)S(1)} %copy-done.6), kind=kOutput, calls=%fused_computation.21 | convolution fusion | flops 2267578368 | bytes 9535488 | tf_op jit(solution)/shard_map/dot_general | solution.py:82
  92.1 1.3 fusion.12
  93.5 1.3 fusion.9
  94.9 0.5 collective-permute-start.3
  95.4 1.3 fusion.14
  96.7 2.7 %collective-permute-done.3 = bf16[576,768]{1,0:T(8,128)(2,1)S(1)} collective-permute-done((bf16[576,768]{1,0:T(8,128)(2,1)S(1)}, bf16[576,768]{1,0:T(8,128)(2,1)S(1)}, u32[]{:S(2)}, u32[]{:S(2)}) %collective-permute-start.3) | collective-permute-done | bytes 884768 | tf_op jit(solution)/shard_map/ppermute | solution.py:88
  99.4 1.3 fusion.8
  100.7 1.8 %pad_maximum_fusion = bf16[576,2560]{1,0:T(8,128)(2,1)} fusion(bf16[576,1280]{1,0:T(8,128)(2,1)S(1)} %collective-permute-done.5, bf16[576,1280]{1,0:T(8,128)(2,1)S(1)} %fusion.8), kind=kLoop, calls=%fused_computation.14 | loop fusion | flops 5898240 | bytes 5898240 | tf_op jit(solution)/shard_map/concatenate | solution.py:103
  102.6 5.1 %reshape.65 = bf16[64,180,128]{2,1,0:T(8,128)(2,1)S(1)} reshape(bf16[576,2560]{1,0:T(8,128)(2,1)} %pad_maximum_fusion) | data formatting | bytes 5898240 | tf_op jit(solution)/shard_map/reshape | solution.py:24
  107.6 45.1 %all_to_all.11 = bf16[64,180,128]{2,1,0:T(8,128)(2,1)} all-to-all(bf16[64,180,128]{2,1,0:T(8,128)(2,1)S(1)} %reshape.65), channel_id=1, replica_groups=mesh['ep'=64,'dp'=2] {'ep'}, dimensions={0} | all-to-all | bytes 5898240 | tf_op jit(solution)/shard_map/all_to_all | solution.py:25
  152.7 4.8 %reshape.66 = bf16[576,2560]{1,0:T(8,128)(2,1)S(1)} reshape(bf16[64,180,128]{2,1,0:T(8,128)(2,1)} %all_to_all.11) | data formatting | bytes 5898240 | tf_op jit(solution)/shard_map/reshape | solution.py:26
  157.5 0.7 fusion.44
  158.2 0.7 convolution_add_fusion
  158.9 0.2 fusion.22
  159.2 0.9 fusion.24
  (38 shorter events, 1.3 us)
Async XLA Ops:
  0.6 4.1 %collective-permute-start = (bf16[64,2560]{1,0:T(8,128)(2,1)}, bf16[64,2560]{1,0:T(8,128)(2,1)S(1)}, u32[]{:S(2)}, u32[]{:S(2)}) collective-permute-start(bf16[64,2560]{1,0:T(8,128)(2,1)} %param.10), channel_id=1, source_target_pairs={{0,1},{1,0},{2,3},{3,2},{4,5},{5,4},{6,7},{7,6},{8,9},{9,8},{10,11... | collective-permute-start | bytes 983048 | tf_op jit(solution)/shard_map/ppermute | solution.py:49
  4.7 4.7 %copy-start.2 = (f32[64,6]{0,1:T(8,128)S(1)}, f32[64,6]{0,1:T(8,128)}, u32[]{:S(2)}) copy-start(f32[64,6]{0,1:T(8,128)} %param.15) | copy-start | bytes 4612
  4.7 5.7 %copy-start.1 = (bf16[64,2560]{1,0:T(8,128)(2,1)S(1)}, bf16[64,2560]{1,0:T(8,128)(2,1)}, u32[]{:S(2)}) copy-start(bf16[64,2560]{1,0:T(8,128)(2,1)} %param.11) | copy-start | bytes 983044
  8.8 1.9 %copy-start.3 = (f32[2560]{0:T(1024)S(1)}, f32[2560]{0:T(1024)}, u32[]{:S(2)}) copy-start(f32[2560]{0:T(1024)} %param.13) | copy-start | bytes 30724
  8.8 1.6 %collective-permute-start.1 = (bf16[64,1280]{1,0:T(8,128)(2,1)S(1)}, bf16[64,1280]{1,0:T(8,128)(2,1)S(1)}, u32[]{:S(2)}, u32[]{:S(2)}) collective-permute-start(bf16[64,1280]{1,0:T(8,128)(2,1)S(1)} %slice.34), channel_id=1, source_target_pairs={{0,1},{1,0},{2,3},{3,2},{4,5},{5,4},{6,7},{7,6},{8,9},{9,8},{10,11... | collective-permute-start | bytes 491528 | tf_op jit(solution)/shard_map/ppermute | solution.py:56
  75.0 8.2 %collective-permute-start.2 = (bf16[576,2560]{1,0:T(8,128)(2,1)S(1)}, bf16[576,2560]{1,0:T(8,128)(2,1)}, u32[]{:S(2)}, u32[]{:S(2)}) collective-permute-start(bf16[576,2560]{1,0:T(8,128)(2,1)S(1)} %reshape.64), channel_id=1, source_target_pairs={{0,1},{1,0},{2,3},{3,2},{4,5},{5,4},{6,7},{7,6},{8,9},{9,8},{10,11... | collective-permute-start | bytes 8847368 | tf_op jit(solution)/shard_map/ppermute | solution.py:78
  75.1 4.7 %copy-start.6 = (bf16[1,2560,768]{2,1,0:T(8,128)(2,1)S(1)}, bf16[1,2560,768]{2,1,0:T(8,128)(2,1)}, u32[]{:S(2)}) copy-start(bf16[1,2560,768]{2,1,0:T(8,128)(2,1)} %param.17) | copy-start | bytes 11796484
  79.9 3.4 %copy-start.5 = (bf16[1,2560,768]{2,1,0:T(8,128)(2,1)S(1)}, bf16[1,2560,768]{2,1,0:T(8,128)(2,1)}, u32[]{:S(2)}) copy-start(bf16[1,2560,768]{2,1,0:T(8,128)(2,1)} %param.16) | copy-start | bytes 11796484
  82.5 11.0 %collective-permute-start.4 = (bf16[576,768]{1,0:T(8,128)(2,1)S(1)}, bf16[576,768]{1,0:T(8,128)(2,1)S(1)}, u32[]{:S(2)}, u32[]{:S(2)}) collective-permute-start(bf16[576,768]{1,0:T(8,128)(2,1)S(1)} %multiply_convert_fusion.1), channel_id=1, source_target_pairs={{0,1},{1,0},{2,3},{3,2},{4,5},{5,4},{6,7},{7,6},{8,9},{9,8},{10,11... | collective-permute-start | bytes 2654216 | tf_op jit(solution)/shard_map/ppermute | solution.py:86
  87.5 4.6 %copy-start.7 = (bf16[1,1536,1280]{2,1,0:T(8,128)(2,1)S(1)}, bf16[1,1536,1280]{2,1,0:T(8,128)(2,1)}, u32[]{:S(2)}) copy-start(bf16[1,1536,1280]{2,1,0:T(8,128)(2,1)} %param.18) | copy-start | bytes 11796484
  94.8 5.9 %collective-permute-start.5 = (bf16[576,1280]{1,0:T(8,128)(2,1)S(1)}, bf16[576,1280]{1,0:T(8,128)(2,1)S(1)}, u32[]{:S(2)}, u32[]{:S(2)}) collective-permute-start(bf16[576,1280]{1,0:T(8,128)(2,1)S(1)} %fusion.9), channel_id=1, source_target_pairs={{0,1},{1,0},{2,3},{3,2},{4,5},{5,4},{6,7},{7,6},{8,9},{9,8},{10,11... | collective-permute-start | bytes 4423688 | tf_op jit(solution)/shard_map/ppermute | solution.py:101
  94.9 4.5 %collective-permute-start.3 = (bf16[576,768]{1,0:T(8,128)(2,1)S(1)}, bf16[576,768]{1,0:T(8,128)(2,1)S(1)}, u32[]{:S(2)}, u32[]{:S(2)}) collective-permute-start(bf16[576,768]{1,0:T(8,128)(2,1)S(1)} %multiply_convert_fusion), channel_id=1, source_target_pairs={{0,1},{1,0},{2,3},{3,2},{4,5},{5,4},{6,7},{7,6},{8,9},{9,8},{10,11... | collective-permute-start | bytes 2654216 | tf_op jit(solution)/shard_map/ppermute | solution.py:88
  158.2 1.0 copy-start.4
  159.1 0.9 copy-start

commit v7 on v6

--- a/solution.py
+++ b/solution.py
@@ -46,6 +46,12 @@
     capacity = max(2, 3 * tok_rows * top_picks // (2 * experts))
     swap = [(0, 1), (1, 0)]
     me = lax.axis_index("dp")
+    gate_local = gate_weight[0]
+    up_local = up_weight[0]
+    down_local = down_weight[0]
+    gate_partner = lax.ppermute(gate_local, "dp", swap)
+    up_partner = lax.ppermute(up_local, "dp", swap)
+    down_partner = lax.ppermute(down_local, "dp", swap)
     partner_att = lax.ppermute(attention_out, "dp", swap)
     cols = jnp.dot(
         jnp.concatenate([attention_out, partner_att], axis=0),
@@ -71,36 +77,27 @@
     outgoing = lax.dot_general(
         placing, normed_in, (((0,), (0,)), ((), ())), preferred_element_type=jnp.float32
     ).astype(jnp.bfloat16)
-    gate_local = gate_weight[0]
-    up_local = up_weight[0]
-    down_local = down_weight[0]
     own_rows = exchange_rows(outgoing, experts)
-    other_rows = lax.ppermute(own_rows, "dp", swap)
+    me = lax.axis_index("dp")
+    ff_half = gate_local.shape[1]
 
-    def hidden_of(rows):
-        gate_part = jnp.dot(rows, gate_local, preferred_element_type=jnp.float32)
-        up_part = jnp.dot(rows, up_local, preferred_element_type=jnp.float32)
+    def hidden_of(rows, gate_w, up_w):
+        gate_part = jnp.dot(rows, gate_w, preferred_element_type=jnp.float32)
+        up_part = jnp.dot(rows, up_w, preferred_element_type=jnp.float32)
         return (jax.nn.silu(gate_part) * up_part).astype(jnp.bfloat16)
 
-    hidden_own = hidden_of(own_rows)
-    hidden_own_in = lax.ppermute(hidden_own, "dp", swap)
-    hidden_other = hidden_of(other_rows)
-    hidden_other_in = lax.ppermute(hidden_other, "dp", swap)
-    me = lax.axis_index("dp")
-
-    ff_half = hidden_own.shape[1]
-    down_mine = lax.dynamic_slice_in_dim(down_local, me * ff_half, ff_half, axis=0)
-    down_theirs = lax.dynamic_slice_in_dim(down_local, (1 - me) * ff_half, ff_half, axis=0)
-
-    def project(mine, theirs):
-        total = jnp.dot(mine, down_mine, preferred_element_type=jnp.float32)
-        total = total + jnp.dot(theirs, down_theirs, preferred_element_type=jnp.float32)
+    def project(mine, theirs, down_w):
+        first = lax.dynamic_slice_in_dim(down_w, me * ff_half, ff_half, axis=0)
+        second = lax.dynamic_slice_in_dim(down_w, (1 - me) * ff_half, ff_half, axis=0)
+        total = jnp.dot(mine, first, preferred_element_type=jnp.float32)
+        total = total + jnp.dot(theirs, second, preferred_element_type=jnp.float32)
         return total.astype(jnp.bfloat16)
 
-    out_other = project(hidden_other, hidden_own_in)
-    out_other_in = lax.ppermute(out_other, "dp", swap)
-    out_own = project(hidden_own, hidden_other_in)
-    joined = jnp.concatenate([out_own, out_other_in], axis=1)
+    hidden_mine = hidden_of(own_rows, gate_local, up_local)
+    hidden_theirs = hidden_of(own_rows, gate_partner, up_partner)
+    out_own = project(hidden_mine, hidden_theirs, down_local)
+    out_other = project(hidden_mine, hidden_theirs, down_partner)
+    joined = jnp.concatenate([out_own, out_other], axis=1)
     returned = exchange_rows(joined, experts)
     mixing_hi = mixing.astype(jnp.bfloat16)
     mixing_lo = (mixing - mixing_hi.astype(jnp.float32)).astype(jnp.bfloat16)

time: 161 us -> 161 us (level)
  blocking collectives: 97 us -> 47.3 us
  waiting for transfers between devices: 3.44 us -> 41 us
  starting transfers between devices: 2.07 us -> 12.9 us
  matrix products: 29.4 us -> 32.2 us
    all_to_all x2 -> x1, blocking collectives: 97 us -> 47.3 us  [exchange_rows(): moved = lax.all_to_all(wire, 'ep', split_axis=0, concat_axis=0, tiled=True)]
    all_to_all x0 -> x1, waiting for transfers between devices: none -> 40.3 us  [exchange_rows(): moved = lax.all_to_all(wire, 'ep', split_axis=0, concat_axis=0, tiled=True)]
    all_to_all x0 -> x1, starting transfers between devices: none -> 11.5 us  [exchange_rows(): moved = lax.all_to_all(wire, 'ep', split_axis=0, concat_axis=0, tiled=True)]
    dot_general x8, matrix products: 21.4 us -> 25.9 us  [the longest x2 10.2 us: hidden_of(): gate_part = jnp.dot(rows, gate_w, preferred_element_type=jnp.float32)]
    ppermute x4 -> x3, waiting for transfers between devices: 2.71 us -> 0.01 us  [the longest x1 0.01 us: per_device(): gate_partner = lax.ppermute(gate_local, 'dp', swap)]
  transfers between devices with their start and end apart: 6 -> 6, of which waited for: 2 -> 2; matrix products, arithmetic and copies ran while one was open for 15% -> 18% of each run, Pallas kernels for 0% -> 0%
where the time goes in v7:
time: 161 us; the launch traced here: 160 us
  blocking collectives  47.3 us (29%)
  waiting for transfers between devices  41 us (25%)
  matrix products  32.2 us (20%)
  local copies, waits for them, and re-layouts  20.3 us (13%)
  starting transfers between devices  12.9 us (8%)
  other arithmetic  5.91 us (4%)
    all_to_all x1, blocking collectives, exchange_rows(): moved = lax.all_to_all(wire, 'ep', split_axis=0, concat_axis=0, tiled=True)  47.3 us
    all_to_all x1, waiting for transfers between devices, exchange_rows(): moved = lax.all_to_all(wire, 'ep', split_axis=0, concat_axis=0, tiled=True)  40.3 us
    all_to_all x1, starting transfers between devices, exchange_rows(): moved = lax.all_to_all(wire, 'ep', split_axis=0, concat_axis=0, tiled=True)  11.5 us
    dot_general x2, matrix products, hidden_of(): gate_part = jnp.dot(rows, gate_w, preferred_element_type=jnp.float32)  10.2 us
    reshape x2, local copies, waits for them, and re-layouts, exchange_rows(): wire = rows.reshape(experts, total * width // (experts * lanes), lanes)  9.66 us
    reshape x2, local copies, waits for them, and re-layouts, exchange_rows(): return moved.reshape(total, width)  8.99 us
    dot_general x2, matrix products, hidden_of(): up_part = jnp.dot(rows, up_w, preferred_element_type=jnp.float32)  7.26 us
    dot_general x2, matrix products, project(): total = jnp.dot(mine, first, preferred_element_type=jnp.float32)  4.24 us
  transfers between devices with their start and end apart: 6, of which 2 were waited for; matrix products, arithmetic and copies ran while one was open for 18% of the time, Pallas kernels for 0%

profile of v7, /device:TPU:0, one launch (start us, length us, event | category | flops | bytes accessed | tf_op | source)
XLA Modules:
  0.0 160.5 jit_solution(15573680770430693103)
XLA Ops:
  0.7 0.8 copy.26
  1.8 0.9 reduce-window.6
  2.7 0.2 slice_reduce_fusion
  3.3 0.7 reduce_sum.58
  4.0 0.7 multiply_add_fusion
  4.7 4.0 %fusion.17 = f32[128,1280]{1,0:T(8,128)S(1)} fusion(bf16[2560,1280]{1,0:T(8,128)(2,1)} %param.12, bf16[64,2560]{1,0:T(8,128)(2,1)S(1)} %collective-permute-done, bf16[64,2560]{1,0:T(8,128)(2,1)} %param.10), kind=kOutput, calls=%fused_computation.32 | convolution fusion | flops 840171520 | bytes 7864320 | tf_op jit(solution)/shard_map/dot_general | solution.py:56
  8.8 0.6 collective-permute-start.1
  9.4 0.3 select_reduce_fusion
  9.7 0.7 collective-permute-done.1
  10.5 0.2 fusion.13
  10.7 1.0 convolution_convert_fusion
  11.7 4.6 %reshape.63 = bf16[64,180,128]{2,1,0:T(8,128)(2,1)} reshape(bf16[576,2560]{1,0:T(8,128)(2,1)S(1)} %convolution_convert_fusion) | data formatting | bytes 5898240 | tf_op jit(solution)/shard_map/reshape | solution.py:24
  16.3 11.5 %all-to-all-start = ((bf16[64,180,128]{2,1,0:T(8,128)(2,1)}), bf16[64,180,128]{2,1,0:T(8,128)(2,1)S(1)}, u32[]{:S(2)}, u32[]{:S(2)}) async-start(bf16[64,180,128]{2,1,0:T(8,128)(2,1)} %reshape.63), calls=%async_computation | async-start | bytes 6029312 | tf_op jit(solution)/shard_map/all_to_all | solution.py:25
  28.0 0.4 collective-permute-start.3
  28.5 40.3 %all-to-all-done = bf16[64,180,128]{2,1,0:T(8,128)(2,1)S(1)} async-done(((bf16[64,180,128]{2,1,0:T(8,128)(2,1)}), bf16[64,180,128]{2,1,0:T(8,128)(2,1)S(1)}, u32[]{:S(2)}, u32[]{:S(2)}) %all-to-all-start) | async-done | bytes 2949152 | tf_op jit(solution)/shard_map/all_to_all | solution.py:25
  68.8 4.2 %reshape.64 = bf16[576,2560]{1,0:T(8,128)(2,1)} reshape(bf16[64,180,128]{2,1,0:T(8,128)(2,1)S(1)} %all-to-all-done) | data formatting | bytes 5898240 | tf_op jit(solution)/shard_map/reshape | solution.py:26
  73.0 5.6 %fusion.40 = f32[576,768]{1,0:T(8,128)S(1)} fusion(bf16[576,2560]{1,0:T(8,128)(2,1)} %reshape.64, bf16[1,2560,768]{2,1,0:T(8,128)(2,1)} %param.16), kind=kOutput, calls=%fused_computation.67 | convolution fusion | flops 2264924160 | bytes 8650752 | tf_op jit(solution)/shard_map/dot_general | solution.py:85
  78.6 2.6 %multiply_convert_fusion.1 = bf16[576,768]{1,0:T(8,128)(2,1)S(1)} fusion(f32[576,768]{1,0:T(8,128)S(1)} %fusion.40, bf16[576,2560]{1,0:T(8,128)(2,1)S(1)} %copy-done, bf16[1,2560,768]{2,1,0:T(8,128)(2,1)S(1)} %copy-done.6), kind=kOutput, calls=%fused_computation.16 | convolution fusion | flops 2267578368 | bytes 9535488 | tf_op jit(solution)/shard_map/dot_general | solution.py:86
  81.2 1.3 fusion.3
  82.6 4.6 %fusion.45 = f32[576,768]{1,0:T(8,128)S(1)} fusion(bf16[576,2560]{1,0:T(8,128)(2,1)S(1)} %copy-done, bf16[2560,768]{1,0:T(8,128)(2,1)} %collective-permute-done.2), kind=kOutput, calls=%fused_computation.70 | convolution fusion | flops 2264924160 | bytes 8650752 | tf_op jit(solution)/shard_map/dot_general | solution.py:85
  87.1 4.7 %multiply_convert_fusion = bf16[576,768]{1,0:T(8,128)(2,1)S(1)} fusion(f32[576,768]{1,0:T(8,128)S(1)} %fusion.45, bf16[576,2560]{1,0:T(8,128)(2,1)S(1)} %copy-done, bf16[2560,768]{1,0:T(8,128)(2,1)} %collective-permute-done.3), kind=kOutput, calls=%fused_computation.15 | convolution fusion | flops 2267578368 | bytes 9535488 | tf_op jit(solution)/shard_map/dot_general | solution.py:86
  91.8 1.4 fusion
  93.2 2.9 %fusion.5 = f32[576,1280]{1,0:T(8,128)S(1)} fusion(bf16[576,768]{1,0:T(8,128)(2,1)S(1)} %multiply_convert_fusion, bf16[1536,1280]{1,0:T(8,128)(2,1)} %collective-permute-done.4, s32[]{:T(128)S(6)} %select_n.23), kind=kOutput, calls=%fused_computation.10 | convolution fusion | flops 1132462080 | bytes 5799940 | tf_op jit(solution)/shard_map/dot_general | solution.py:93
  96.1 2.9 %fusion.1 = bf16[576,1280]{1,0:T(8,128)(2,1)S(1)} fusion(f32[576,1280]{1,0:T(8,128)S(1)} %fusion.5, bf16[576,768]{1,0:T(8,128)(2,1)S(1)} %multiply_convert_fusion.1, bf16[1536,1280]{1,0:T(8,128)(2,1)} %collective-permute-done.4, s32[]{:T(128)S(6)} %select_n.22), kind=kOutput, calls=%fused_computation.5 | convolution fusion | flops 1133936640 | bytes 7274500 | tf_op jit(solution)/shard_map/dot_general | solution.py:92
  99.0 1.8 %pad_maximum_fusion = bf16[576,2560]{1,0:T(8,128)(2,1)} fusion(bf16[576,1280]{1,0:T(8,128)(2,1)S(1)} %fusion.1, bf16[576,1280]{1,0:T(8,128)(2,1)S(1)} %fusion), kind=kLoop, calls=%fused_computation.6 | loop fusion | flops 5898240 | bytes 5898240 | tf_op jit(solution)/shard_map/concatenate | solution.py:100
  100.8 5.1 %reshape.65 = bf16[64,180,128]{2,1,0:T(8,128)(2,1)S(1)} reshape(bf16[576,2560]{1,0:T(8,128)(2,1)} %pad_maximum_fusion) | data formatting | bytes 5898240 | tf_op jit(solution)/shard_map/reshape | solution.py:24
  105.9 47.3 %all_to_all.10 = bf16[64,180,128]{2,1,0:T(8,128)(2,1)} all-to-all(bf16[64,180,128]{2,1,0:T(8,128)(2,1)S(1)} %reshape.65), channel_id=1, replica_groups=mesh['ep'=64,'dp'=2] {'ep'}, dimensions={0} | all-to-all | bytes 5898240 | tf_op jit(solution)/shard_map/all_to_all | solution.py:25
  153.2 4.8 %reshape.66 = bf16[576,2560]{1,0:T(8,128)(2,1)S(1)} reshape(bf16[64,180,128]{2,1,0:T(8,128)(2,1)} %all_to_all.10) | data formatting | bytes 5898240 | tf_op jit(solution)/shard_map/reshape | solution.py:26
  157.9 0.7 fusion.32
  158.6 0.7 convolution_add_fusion
  159.3 0.2 fusion.10
  159.6 0.9 fusion.12
  (37 shorter events, 1.2 us)
Async XLA Ops:
  0.6 4.1 %collective-permute-start = (bf16[64,2560]{1,0:T(8,128)(2,1)}, bf16[64,2560]{1,0:T(8,128)(2,1)S(1)}, u32[]{:S(2)}, u32[]{:S(2)}) collective-permute-start(bf16[64,2560]{1,0:T(8,128)(2,1)} %param.10), channel_id=1, source_target_pairs={{0,1},{1,0},{2,3},{3,2},{4,5},{5,4},{6,7},{7,6},{8,9},{9,8},{10,11... | collective-permute-start | bytes 983048 | tf_op jit(solution)/shard_map/ppermute | solution.py:55
  4.7 4.7 %copy-start.3 = (f32[64,6]{0,1:T(8,128)S(1)}, f32[64,6]{0,1:T(8,128)}, u32[]{:S(2)}) copy-start(f32[64,6]{0,1:T(8,128)} %param.15) | copy-start | bytes 4612
  4.7 5.7 %copy-start.2 = (bf16[64,2560]{1,0:T(8,128)(2,1)S(1)}, bf16[64,2560]{1,0:T(8,128)(2,1)}, u32[]{:S(2)}) copy-start(bf16[64,2560]{1,0:T(8,128)(2,1)} %param.11) | copy-start | bytes 983044
  8.8 1.9 %copy-start.4 = (f32[2560]{0:T(1024)S(1)}, f32[2560]{0:T(1024)}, u32[]{:S(2)}) copy-start(f32[2560]{0:T(1024)} %param.13) | copy-start | bytes 30724
  8.8 1.6 collective-permute-start.1
  16.3 52.5 %all-to-all-start = ((bf16[64,180,128]{2,1,0:T(8,128)(2,1)}), bf16[64,180,128]{2,1,0:T(8,128)(2,1)S(1)}, u32[]{:S(2)}, u32[]{:S(2)}) async-start(bf16[64,180,128]{2,1,0:T(8,128)(2,1)} %reshape.63), calls=%async_computation | async-start | bytes 6029312 | tf_op jit(solution)/shard_map/all_to_all | solution.py:25
  27.8 54.7 %collective-permute-start.2 = (bf16[2560,768]{1,0:T(8,128)(2,1)}, bf16[2560,768]{1,0:T(8,128)(2,1)}, u32[]{:S(2)}, u32[]{:S(2)}) collective-permute-start(bf16[2560,768]{1,0:T(8,128)(2,1)} %bitcast.48), channel_id=1, source_target_pairs={{0,1},{1,0},{2,3},{3,2},{4,5},{5,4},{6,7},{7,6},{8,9},{9,8},{10,11... | collective-permute-start | bytes 11796488 | tf_op jit(solution)/shard_map/ppermute | solution.py:52
  28.0 59.2 %collective-permute-start.3 = (bf16[2560,768]{1,0:T(8,128)(2,1)}, bf16[2560,768]{1,0:T(8,128)(2,1)}, u32[]{:S(2)}, u32[]{:S(2)}) collective-permute-start(bf16[2560,768]{1,0:T(8,128)(2,1)} %bitcast.49), channel_id=1, source_target_pairs={{0,1},{1,0},{2,3},{3,2},{4,5},{5,4},{6,7},{7,6},{8,9},{9,8},{10,11... | collective-permute-start | bytes 11796488 | tf_op jit(solution)/shard_map/ppermute | solution.py:53
  28.4 64.8 %collective-permute-start.4 = (bf16[1536,1280]{1,0:T(8,128)(2,1)}, bf16[1536,1280]{1,0:T(8,128)(2,1)}, u32[]{:S(2)}, u32[]{:S(2)}) collective-permute-start(bf16[1536,1280]{1,0:T(8,128)(2,1)} %bitcast.50), channel_id=1, source_target_pairs={{0,1},{1,0},{2,3},{3,2},{4,5},{5,4},{6,7},{7,6},{8,9},{9,8},{10,11... | collective-permute-start | bytes 11796488 | tf_op jit(solution)/shard_map/ppermute | solution.py:54
  73.0 5.6 %copy-start = (bf16[576,2560]{1,0:T(8,128)(2,1)S(1)}, bf16[576,2560]{1,0:T(8,128)(2,1)}, u32[]{:S(2)}) copy-start(bf16[576,2560]{1,0:T(8,128)(2,1)} %reshape.64) | copy-start | bytes 8847364
  73.0 5.6 %copy-start.6 = (bf16[1,2560,768]{2,1,0:T(8,128)(2,1)S(1)}, bf16[1,2560,768]{2,1,0:T(8,128)(2,1)}, u32[]{:S(2)}) copy-start(bf16[1,2560,768]{2,1,0:T(8,128)(2,1)} %param.17) | copy-start | bytes 11796484
  78.6 2.6 %copy-start.7 = (bf16[1,1536,1280]{2,1,0:T(8,128)(2,1)S(1)}, bf16[1,1536,1280]{2,1,0:T(8,128)(2,1)}, u32[]{:S(2)}) copy-start(bf16[1,1536,1280]{2,1,0:T(8,128)(2,1)} %param.18) | copy-start | bytes 11796484
  158.6 1.0 copy-start.5
  159.6 0.9 copy-start.1

commit v8 on v7

--- a/solution.py
+++ b/solution.py
@@ -86,17 +86,17 @@
         up_part = jnp.dot(rows, up_w, preferred_element_type=jnp.float32)
         return (jax.nn.silu(gate_part) * up_part).astype(jnp.bfloat16)
 
-    def project(mine, theirs, down_w):
-        first = lax.dynamic_slice_in_dim(down_w, me * ff_half, ff_half, axis=0)
-        second = lax.dynamic_slice_in_dim(down_w, (1 - me) * ff_half, ff_half, axis=0)
-        total = jnp.dot(mine, first, preferred_element_type=jnp.float32)
-        total = total + jnp.dot(theirs, second, preferred_element_type=jnp.float32)
-        return total.astype(jnp.bfloat16)
-
     hidden_mine = hidden_of(own_rows, gate_local, up_local)
     hidden_theirs = hidden_of(own_rows, gate_partner, up_partner)
-    out_own = project(hidden_mine, hidden_theirs, down_local)
-    out_other = project(hidden_mine, hidden_theirs, down_partner)
+    hidden_full = jnp.where(
+        me == 0,
+        jnp.concatenate([hidden_mine, hidden_theirs], axis=1),
+        jnp.concatenate([hidden_theirs, hidden_mine], axis=1),
+    )
+    out_own = jnp.dot(hidden_full, down_local, preferred_element_type=jnp.float32).astype(jnp.bfloat16)
+    out_other = jnp.dot(hidden_full, down_partner, preferred_element_type=jnp.float32).astype(
+        jnp.bfloat16
+    )
     joined = jnp.concatenate([out_own, out_other], axis=1)
     returned = exchange_rows(joined, experts)
     mixing_hi = mixing.astype(jnp.bfloat16)

time: 161 us -> 160 us (level)
    dot_general x4 -> x2, matrix products: 8.47 us -> 7.04 us  [the longest x1 4.57 us: per_device(): jnp.dot(hidden_full, down_partner, preferred_element_type=jnp.float32)]
where the time goes in v8:
time: 160 us; the launch traced here: 159 us
  blocking collectives  47.3 us (30%)
  waiting for transfers between devices  41 us (26%)
  matrix products  30.9 us (19%)
  local copies, waits for them, and re-layouts  20.3 us (13%)
  starting transfers between devices  12.9 us (8%)
  other arithmetic  5.91 us (4%)
    all_to_all x1, blocking collectives, exchange_rows(): moved = lax.all_to_all(wire, 'ep', split_axis=0, concat_axis=0, tiled=True)  47.3 us
    all_to_all x1, waiting for transfers between devices, exchange_rows(): moved = lax.all_to_all(wire, 'ep', split_axis=0, concat_axis=0, tiled=True)  40.3 us
    all_to_all x1, starting transfers between devices, exchange_rows(): moved = lax.all_to_all(wire, 'ep', split_axis=0, concat_axis=0, tiled=True)  11.5 us
    dot_general x2, matrix products, hidden_of(): gate_part = jnp.dot(rows, gate_w, preferred_element_type=jnp.float32)  10.2 us
    reshape x2, local copies, waits for them, and re-layouts, exchange_rows(): wire = rows.reshape(experts, total * width // (experts * lanes), lanes)  9.66 us
    reshape x2, local copies, waits for them, and re-layouts, exchange_rows(): return moved.reshape(total, width)  8.99 us
    dot_general x2, matrix products, hidden_of(): up_part = jnp.dot(rows, up_w, preferred_element_type=jnp.float32)  7.4 us
    dot_general x1, matrix products, per_device(): jnp.dot(hidden_full, down_partner, preferred_element_type=jnp.float32)  4.57 us
  transfers between devices with their start and end apart: 6, of which 2 were waited for; matrix products, arithmetic and copies ran while one was open for 18% of the time, Pallas kernels for 0%

profile of v8, /device:TPU:0, one launch (start us, length us, event | category | flops | bytes accessed | tf_op | source)
XLA Modules:
  0.0 159.2 jit_solution(8822392055086840110)
XLA Ops:
  0.7 0.8 copy.26
  1.6 0.1 eq.44
  1.8 0.9 reduce-window.6
  2.7 0.2 slice_reduce_fusion
  3.3 0.7 reduce_sum.58
  4.0 0.7 multiply_add_fusion
  4.7 4.0 %fusion.7 = f32[128,1280]{1,0:T(8,128)S(1)} fusion(bf16[2560,1280]{1,0:T(8,128)(2,1)} %param.12, bf16[64,2560]{1,0:T(8,128)(2,1)S(1)} %collective-permute-done, bf16[64,2560]{1,0:T(8,128)(2,1)} %param.10), kind=kOutput, calls=%fused_computation.23 | convolution fusion | flops 840171520 | bytes 7864320 | tf_op jit(solution)/shard_map/dot_general | solution.py:56
  8.8 0.6 collective-permute-start.1
  9.4 0.3 select_reduce_fusion
  9.7 0.7 collective-permute-done.1
  10.5 0.2 fusion.3
  10.7 1.0 convolution_convert_fusion
  11.7 4.6 %reshape.61 = bf16[64,180,128]{2,1,0:T(8,128)(2,1)} reshape(bf16[576,2560]{1,0:T(8,128)(2,1)S(1)} %convolution_convert_fusion) | data formatting | bytes 5898240 | tf_op jit(solution)/shard_map/reshape | solution.py:24
  16.3 11.5 %all-to-all-start = ((bf16[64,180,128]{2,1,0:T(8,128)(2,1)}), bf16[64,180,128]{2,1,0:T(8,128)(2,1)S(1)}, u32[]{:S(2)}, u32[]{:S(2)}) async-start(bf16[64,180,128]{2,1,0:T(8,128)(2,1)} %reshape.61), calls=%async_computation | async-start | bytes 6029312 | tf_op jit(solution)/shard_map/all_to_all | solution.py:25
  27.8 0.2 collective-permute-start.2
  28.0 0.4 collective-permute-start.3
  28.5 40.3 %all-to-all-done = bf16[64,180,128]{2,1,0:T(8,128)(2,1)S(1)} async-done(((bf16[64,180,128]{2,1,0:T(8,128)(2,1)}), bf16[64,180,128]{2,1,0:T(8,128)(2,1)S(1)}, u32[]{:S(2)}, u32[]{:S(2)}) %all-to-all-start) | async-done | bytes 2949152 | tf_op jit(solution)/shard_map/all_to_all | solution.py:25
  68.8 4.2 %reshape.62 = bf16[576,2560]{1,0:T(8,128)(2,1)} reshape(bf16[64,180,128]{2,1,0:T(8,128)(2,1)S(1)} %all-to-all-done) | data formatting | bytes 5898240 | tf_op jit(solution)/shard_map/reshape | solution.py:26
  73.0 5.6 %fusion.29 = f32[576,768]{1,0:T(8,128)S(1)} fusion(bf16[576,2560]{1,0:T(8,128)(2,1)} %reshape.62, bf16[1,2560,768]{2,1,0:T(8,128)(2,1)} %param.16), kind=kOutput, calls=%fused_computation.57 | convolution fusion | flops 2264924160 | bytes 8650752 | tf_op jit(solution)/shard_map/dot_general | solution.py:85
  78.6 2.6 %multiply_convert_fusion.1 = bf16[576,768]{1,0:T(8,128)(2,1)S(1)} fusion(f32[576,768]{1,0:T(8,128)S(1)} %fusion.29, bf16[576,2560]{1,0:T(8,128)(2,1)S(1)} %copy-done, bf16[1,2560,768]{2,1,0:T(8,128)(2,1)S(1)} %copy-done.6), kind=kOutput, calls=%fused_computation.7 | convolution fusion | flops 2267578368 | bytes 9535488 | tf_op jit(solution)/shard_map/dot_general | solution.py:86
  81.2 4.6 %fusion.34 = f32[576,768]{1,0:T(8,128)S(1)} fusion(bf16[576,2560]{1,0:T(8,128)(2,1)S(1)} %copy-done, bf16[2560,768]{1,0:T(8,128)(2,1)} %collective-permute-done.2), kind=kOutput, calls=%fused_computation.60 | convolution fusion | flops 2264924160 | bytes 8650752 | tf_op jit(solution)/shard_map/dot_general | solution.py:85
  85.8 4.8 %multiply_convert_fusion = bf16[576,768]{1,0:T(8,128)(2,1)S(1)} fusion(f32[576,768]{1,0:T(8,128)S(1)} %fusion.34, bf16[576,2560]{1,0:T(8,128)(2,1)S(1)} %copy-done, bf16[2560,768]{1,0:T(8,128)(2,1)} %collective-permute-done.3), kind=kOutput, calls=%fused_computation.6 | convolution fusion | flops 2267578368 | bytes 9535488 | tf_op jit(solution)/shard_map/dot_general | solution.py:86
  90.6 2.5 %convolution_convert_fusion.2 = bf16[576,1280]{1,0:T(8,128)(2,1)S(1)} fusion(bf16[576,768]{1,0:T(8,128)(2,1)S(1)} %multiply_convert_fusion, bf16[576,768]{1,0:T(8,128)(2,1)S(1)} %multiply_convert_fusion.1, pred[]{:T(512)S(6)} %eq.43, bf16[1,1536,1280]{2,1,0:T(8,128)(2,1)S(1)} %copy-done.7), kind=kOutput, calls=%fused_computation.3 | convolution fusion | flops 2273624064 | bytes 7176193 | tf_op jit(solution)/shard_map/dot_general | solution.py:96
  93.1 4.6 %convolution_convert_fusion.1 = bf16[576,1280]{1,0:T(8,128)(2,1)S(1)} fusion(bf16[1536,1280]{1,0:T(8,128)(2,1)} %collective-permute-done.4, bf16[576,768]{1,0:T(8,128)(2,1)S(1)} %multiply_convert_fusion, bf16[576,768]{1,0:T(8,128)(2,1)S(1)} %multiply_convert_fusion.1, pred[]{:T(512)S(6)} %eq.43), kind=kOutput, calls=%fused_computation.2 | convolution fusion | flops 2273624064 | bytes 7176193 | tf_op jit(solution)/shard_map/dot_general | solution.py:97
  97.7 1.8 %pad_maximum_fusion = bf16[576,2560]{1,0:T(8,128)(2,1)} fusion(bf16[576,1280]{1,0:T(8,128)(2,1)S(1)} %convolution_convert_fusion.1, bf16[576,1280]{1,0:T(8,128)(2,1)S(1)} %convolution_convert_fusion.2), kind=kLoop, calls=%fused_computation.4 | loop fusion | flops 5898240 | bytes 5898240 | tf_op jit(solution)/shard_map/concatenate | solution.py:100
  99.5 5.1 %reshape.63 = bf16[64,180,128]{2,1,0:T(8,128)(2,1)S(1)} reshape(bf16[576,2560]{1,0:T(8,128)(2,1)} %pad_maximum_fusion) | data formatting | bytes 5898240 | tf_op jit(solution)/shard_map/reshape | solution.py:24
  104.6 47.3 %all_to_all.10 = bf16[64,180,128]{2,1,0:T(8,128)(2,1)} all-to-all(bf16[64,180,128]{2,1,0:T(8,128)(2,1)S(1)} %reshape.63), channel_id=1, replica_groups=mesh['ep'=64,'dp'=2] {'ep'}, dimensions={0} | all-to-all | bytes 5898240 | tf_op jit(solution)/shard_map/all_to_all | solution.py:25
  151.9 4.8 %reshape.64 = bf16[576,2560]{1,0:T(8,128)(2,1)S(1)} reshape(bf16[64,180,128]{2,1,0:T(8,128)(2,1)} %all_to_all.10) | data formatting | bytes 5898240 | tf_op jit(solution)/shard_map/reshape | solution.py:26
  156.6 0.7 fusion.22
  157.3 0.7 convolution_add_fusion
  158.0 0.2 fusion
  158.3 0.9 fusion.2
  (35 shorter events, 0.9 us)
Async XLA Ops:
  0.6 4.1 %collective-permute-start = (bf16[64,2560]{1,0:T(8,128)(2,1)}, bf16[64,2560]{1,0:T(8,128)(2,1)S(1)}, u32[]{:S(2)}, u32[]{:S(2)}) collective-permute-start(bf16[64,2560]{1,0:T(8,128)(2,1)} %param.10), channel_id=1, source_target_pairs={{0,1},{1,0},{2,3},{3,2},{4,5},{5,4},{6,7},{7,6},{8,9},{9,8},{10,11... | collective-permute-start | bytes 983048 | tf_op jit(solution)/shard_map/ppermute | solution.py:55
  4.7 4.7 %copy-start.3 = (f32[64,6]{0,1:T(8,128)S(1)}, f32[64,6]{0,1:T(8,128)}, u32[]{:S(2)}) copy-start(f32[64,6]{0,1:T(8,128)} %param.15) | copy-start | bytes 4612
  4.7 5.7 %copy-start.2 = (bf16[64,2560]{1,0:T(8,128)(2,1)S(1)}, bf16[64,2560]{1,0:T(8,128)(2,1)}, u32[]{:S(2)}) copy-start(bf16[64,2560]{1,0:T(8,128)(2,1)} %param.11) | copy-start | bytes 983044
  8.8 1.9 %copy-start.4 = (f32[2560]{0:T(1024)S(1)}, f32[2560]{0:T(1024)}, u32[]{:S(2)}) copy-start(f32[2560]{0:T(1024)} %param.13) | copy-start | bytes 30724
  8.8 1.6 %collective-permute-start.1 = (bf16[64,1280]{1,0:T(8,128)(2,1)S(1)}, bf16[64,1280]{1,0:T(8,128)(2,1)S(1)}, u32[]{:S(2)}, u32[]{:S(2)}) collective-permute-start(bf16[64,1280]{1,0:T(8,128)(2,1)S(1)} %slice.34), channel_id=1, source_target_pairs={{0,1},{1,0},{2,3},{3,2},{4,5},{5,4},{6,7},{7,6},{8,9},{9,8},{10,11... | collective-permute-start | bytes 491528 | tf_op jit(solution)/shard_map/ppermute | solution.py:62
  16.3 52.5 %all-to-all-start = ((bf16[64,180,128]{2,1,0:T(8,128)(2,1)}), bf16[64,180,128]{2,1,0:T(8,128)(2,1)S(1)}, u32[]{:S(2)}, u32[]{:S(2)}) async-start(bf16[64,180,128]{2,1,0:T(8,128)(2,1)} %reshape.61), calls=%async_computation | async-start | bytes 6029312 | tf_op jit(solution)/shard_map/all_to_all | solution.py:25
  27.8 53.4 %collective-permute-start.2 = (bf16[2560,768]{1,0:T(8,128)(2,1)}, bf16[2560,768]{1,0:T(8,128)(2,1)}, u32[]{:S(2)}, u32[]{:S(2)}) collective-permute-start(bf16[2560,768]{1,0:T(8,128)(2,1)} %bitcast.41), channel_id=1, source_target_pairs={{0,1},{1,0},{2,3},{3,2},{4,5},{5,4},{6,7},{7,6},{8,9},{9,8},{10,11... | collective-permute-start | bytes 11796488 | tf_op jit(solution)/shard_map/ppermute | solution.py:52
  28.0 57.8 %collective-permute-start.3 = (bf16[2560,768]{1,0:T(8,128)(2,1)}, bf16[2560,768]{1,0:T(8,128)(2,1)}, u32[]{:S(2)}, u32[]{:S(2)}) collective-permute-start(bf16[2560,768]{1,0:T(8,128)(2,1)} %bitcast.42), channel_id=1, source_target_pairs={{0,1},{1,0},{2,3},{3,2},{4,5},{5,4},{6,7},{7,6},{8,9},{9,8},{10,11... | collective-permute-start | bytes 11796488 | tf_op jit(solution)/shard_map/ppermute | solution.py:53
  28.4 64.7 %collective-permute-start.4 = (bf16[1536,1280]{1,0:T(8,128)(2,1)}, bf16[1536,1280]{1,0:T(8,128)(2,1)}, u32[]{:S(2)}, u32[]{:S(2)}) collective-permute-start(bf16[1536,1280]{1,0:T(8,128)(2,1)} %bitcast.43), channel_id=1, source_target_pairs={{0,1},{1,0},{2,3},{3,2},{4,5},{5,4},{6,7},{7,6},{8,9},{9,8},{10,11... | collective-permute-start | bytes 11796488 | tf_op jit(solution)/shard_map/ppermute | solution.py:54
  73.0 5.6 %copy-start = (bf16[576,2560]{1,0:T(8,128)(2,1)S(1)}, bf16[576,2560]{1,0:T(8,128)(2,1)}, u32[]{:S(2)}) copy-start(bf16[576,2560]{1,0:T(8,128)(2,1)} %reshape.62) | copy-start | bytes 8847364
  73.0 5.6 %copy-start.6 = (bf16[1,2560,768]{2,1,0:T(8,128)(2,1)S(1)}, bf16[1,2560,768]{2,1,0:T(8,128)(2,1)}, u32[]{:S(2)}) copy-start(bf16[1,2560,768]{2,1,0:T(8,128)(2,1)} %param.17) | copy-start | bytes 11796484
  85.8 4.9 %copy-start.7 = (bf16[1,1536,1280]{2,1,0:T(8,128)(2,1)S(1)}, bf16[1,1536,1280]{2,1,0:T(8,128)(2,1)}, u32[]{:S(2)}) copy-start(bf16[1,1536,1280]{2,1,0:T(8,128)(2,1)} %param.18) | copy-start | bytes 11796484
  157.3 1.0 copy-start.5
  158.3 0.9 copy-start.1

commit v9 on v8

--- a/solution.py
+++ b/solution.py
@@ -93,11 +93,11 @@
         jnp.concatenate([hidden_mine, hidden_theirs], axis=1),
         jnp.concatenate([hidden_theirs, hidden_mine], axis=1),
     )
-    out_own = jnp.dot(hidden_full, down_local, preferred_element_type=jnp.float32).astype(jnp.bfloat16)
-    out_other = jnp.dot(hidden_full, down_partner, preferred_element_type=jnp.float32).astype(
-        jnp.bfloat16
-    )
-    joined = jnp.concatenate([out_own, out_other], axis=1)
+    joined = jnp.dot(
+        hidden_full,
+        jnp.concatenate([down_local, down_partner], axis=1),
+        preferred_element_type=jnp.float32,
+    ).astype(jnp.bfloat16)
     returned = exchange_rows(joined, experts)
     mixing_hi = mixing.astype(jnp.bfloat16)
     mixing_lo = (mixing - mixing_hi.astype(jnp.float32)).astype(jnp.bfloat16)

time: 160 us -> 159 us (level)
  other arithmetic: 5.91 us -> 4.09 us
    concatenate x1 -> x0, other arithmetic: 1.82 us -> none  [per_device(): joined = jnp.concatenate([out_own, out_other], axis=1)]
    dot_general x2 -> x1, matrix products: 7.04 us -> 8.48 us  [per_device(): jnp.dot(hidden_full, jnp.concatenate([down_local, down_partner], axis=1),...]
  transfers between devices with their start and end apart: 6 -> 6, of which waited for: 2 -> 2; matrix products, arithmetic and copies ran while one was open for 18% -> 16% of each run, Pallas kernels for 0% -> 0%
where the time goes in v9:
time: 159 us
  blocking collectives  47.3 us (30%)
  waiting for transfers between devices  41 us (26%)
  matrix products  32.4 us (20%)
  local copies, waits for them, and re-layouts  20.3 us (13%)
  starting transfers between devices  12.9 us (8%)
  other arithmetic  4.09 us (3%)
    all_to_all x1, blocking collectives, exchange_rows(): moved = lax.all_to_all(wire, 'ep', split_axis=0, concat_axis=0, tiled=True)  47.3 us
    all_to_all x1, waiting for transfers between devices, exchange_rows(): moved = lax.all_to_all(wire, 'ep', split_axis=0, concat_axis=0, tiled=True)  40.3 us
    all_to_all x1, starting transfers between devices, exchange_rows(): moved = lax.all_to_all(wire, 'ep', split_axis=0, concat_axis=0, tiled=True)  11.5 us
    dot_general x2, matrix products, hidden_of(): gate_part = jnp.dot(rows, gate_w, preferred_element_type=jnp.float32)  10.2 us
    reshape x2, local copies, waits for them, and re-layouts, exchange_rows(): wire = rows.reshape(experts, total * width // (experts * lanes), lanes)  9.66 us
    reshape x2, local copies, waits for them, and re-layouts, exchange_rows(): return moved.reshape(total, width)  8.99 us
    dot_general x1, matrix products, per_device(): jnp.dot(hidden_full, jnp.concatenate([down_local, down_partner], axis=1),...  8.48 us
    dot_general x2, matrix products, hidden_of(): up_part = jnp.dot(rows, up_w, preferred_element_type=jnp.float32)  7.43 us
  transfers between devices with their start and end apart: 6, of which 2 were waited for; matrix products, arithmetic and copies ran while one was open for 16% of the time, Pallas kernels for 0%

profile of v9, /device:TPU:0, one launch (start us, length us, event | category | flops | bytes accessed | tf_op | source)
XLA Modules:
  0.0 158.8 jit_solution(1872606165801108245)
XLA Ops:
  0.7 0.8 copy.26
  1.5 0.1 eq.48
  1.6 0.1 eq.44
  1.8 0.9 reduce-window.6
  2.7 0.2 slice_reduce_fusion
  3.1 0.1 reduce_sum.57
  3.3 0.7 reduce_sum.58
  4.0 0.7 multiply_add_fusion
  4.7 4.0 %fusion.20 = f32[128,1280]{1,0:T(8,128)S(1)} fusion(bf16[2560,1280]{1,0:T(8,128)(2,1)} %param.12, bf16[64,2560]{1,0:T(8,128)(2,1)S(1)} %collective-permute-done, bf16[64,2560]{1,0:T(8,128)(2,1)} %param.10), kind=kOutput, calls=%fused_computation.31 | convolution fusion | flops 840171520 | bytes 7864320 | tf_op jit(solution)/shard_map/dot_general | solution.py:56
  8.8 0.6 collective-permute-start.1
  9.4 0.3 select_reduce_fusion
  9.7 0.7 collective-permute-done.1
  10.5 0.2 fusion.16
  10.7 1.0 convolution_convert_fusion
  11.7 4.6 %reshape.61 = bf16[64,180,128]{2,1,0:T(8,128)(2,1)} reshape(bf16[576,2560]{1,0:T(8,128)(2,1)S(1)} %convolution_convert_fusion) | data formatting | bytes 5898240 | tf_op jit(solution)/shard_map/reshape | solution.py:24
  16.3 11.5 %all-to-all-start = ((bf16[64,180,128]{2,1,0:T(8,128)(2,1)}), bf16[64,180,128]{2,1,0:T(8,128)(2,1)S(1)}, u32[]{:S(2)}, u32[]{:S(2)}) async-start(bf16[64,180,128]{2,1,0:T(8,128)(2,1)} %reshape.61), calls=%async_computation | async-start | bytes 6029312 | tf_op jit(solution)/shard_map/all_to_all | solution.py:25
  27.8 0.2 collective-permute-start.2
  28.0 0.4 collective-permute-start.3
  28.5 40.3 %all-to-all-done = bf16[64,180,128]{2,1,0:T(8,128)(2,1)S(1)} async-done(((bf16[64,180,128]{2,1,0:T(8,128)(2,1)}), bf16[64,180,128]{2,1,0:T(8,128)(2,1)S(1)}, u32[]{:S(2)}, u32[]{:S(2)}) %all-to-all-start) | async-done | bytes 2949152 | tf_op jit(solution)/shard_map/all_to_all | solution.py:25
  68.8 4.2 %reshape.62 = bf16[576,2560]{1,0:T(8,128)(2,1)} reshape(bf16[64,180,128]{2,1,0:T(8,128)(2,1)S(1)} %all-to-all-done) | data formatting | bytes 5898240 | tf_op jit(solution)/shard_map/reshape | solution.py:26
  73.0 5.6 %fusion.40 = f32[576,768]{1,0:T(8,128)S(1)} fusion(bf16[576,2560]{1,0:T(8,128)(2,1)} %reshape.62, bf16[1,2560,768]{2,1,0:T(8,128)(2,1)} %param.16), kind=kOutput, calls=%fused_computation.63 | convolution fusion | flops 2264924160 | bytes 8650752 | tf_op jit(solution)/shard_map/dot_general | solution.py:85
  78.6 2.6 %multiply_convert_fusion.1 = bf16[576,768]{1,0:T(8,128)(2,1)S(1)} fusion(f32[576,768]{1,0:T(8,128)S(1)} %fusion.40, bf16[576,2560]{1,0:T(8,128)(2,1)S(1)} %copy-done, bf16[1,2560,768]{2,1,0:T(8,128)(2,1)S(1)} %copy-done.6), kind=kOutput, calls=%fused_computation.14 | convolution fusion | flops 2267578368 | bytes 9535488 | tf_op jit(solution)/shard_map/dot_general | solution.py:86
  81.2 4.6 %fusion.45 = f32[576,768]{1,0:T(8,128)S(1)} fusion(bf16[576,2560]{1,0:T(8,128)(2,1)S(1)} %copy-done, bf16[2560,768]{1,0:T(8,128)(2,1)} %collective-permute-done.2), kind=kOutput, calls=%fused_computation.66 | convolution fusion | flops 2264924160 | bytes 8650752 | tf_op jit(solution)/shard_map/dot_general | solution.py:85
  85.8 4.9 %multiply_convert_fusion = bf16[576,768]{1,0:T(8,128)(2,1)S(1)} fusion(f32[576,768]{1,0:T(8,128)S(1)} %fusion.45, bf16[576,2560]{1,0:T(8,128)(2,1)S(1)} %copy-done, bf16[2560,768]{1,0:T(8,128)(2,1)} %collective-permute-done.3), kind=kOutput, calls=%fused_computation.13 | convolution fusion | flops 2267578368 | bytes 9535488 | tf_op jit(solution)/shard_map/dot_general | solution.py:86
  90.7 8.5 %fusion.4 = bf16[576,2560]{1,0:T(8,128)(2,1)} fusion(bf16[1536,1280]{1,0:T(8,128)(2,1)} %collective-permute-done.4, bf16[1536,1280]{1,0:T(8,128)(2,1)S(1)} %bitcast.41, bf16[576,768]{1,0:T(8,128)(2,1)S(1)} %multiply_convert_fusion, bf16[576,768]{1,0:T(8,128)(2,1)S(1)} %multiply_convert_fusion.1, pred[]{:T(512)S(6)} %eq.43), kind=kOutput, calls=%fused_computation.4 | convolution fusion | flops 4555014144 | bytes 12582913 | tf_op jit(solution)/shard_map/dot_general | solution.py:96
  99.2 5.1 %reshape.63 = bf16[64,180,128]{2,1,0:T(8,128)(2,1)S(1)} reshape(bf16[576,2560]{1,0:T(8,128)(2,1)} %fusion.4) | data formatting | bytes 5898240 | tf_op jit(solution)/shard_map/reshape | solution.py:24
  104.2 47.3 %all_to_all.10 = bf16[64,180,128]{2,1,0:T(8,128)(2,1)} all-to-all(bf16[64,180,128]{2,1,0:T(8,128)(2,1)S(1)} %reshape.63), channel_id=1, replica_groups=mesh['ep'=64,'dp'=2] {'ep'}, dimensions={0} | all-to-all | bytes 5898240 | tf_op jit(solution)/shard_map/all_to_all | solution.py:25
  151.5 4.8 %reshape.64 = bf16[576,2560]{1,0:T(8,128)(2,1)S(1)} reshape(bf16[64,180,128]{2,1,0:T(8,128)(2,1)} %all_to_all.10) | data formatting | bytes 5898240 | tf_op jit(solution)/shard_map/reshape | solution.py:26
  156.3 0.7 fusion.35
  157.0 0.7 convolution_add_fusion
  157.7 0.2 fusion.13
  157.9 0.9 fusion.15
  (33 shorter events, 0.6 us)
Async XLA Ops:
  0.6 4.1 %collective-permute-start = (bf16[64,2560]{1,0:T(8,128)(2,1)}, bf16[64,2560]{1,0:T(8,128)(2,1)S(1)}, u32[]{:S(2)}, u32[]{:S(2)}) collective-permute-start(bf16[64,2560]{1,0:T(8,128)(2,1)} %param.10), channel_id=1, source_target_pairs={{0,1},{1,0},{2,3},{3,2},{4,5},{5,4},{6,7},{7,6},{8,9},{9,8},{10,11... | collective-permute-start | bytes 983048 | tf_op jit(solution)/shard_map/ppermute | solution.py:55
  4.7 4.7 %copy-start.3 = (f32[64,6]{0,1:T(8,128)S(1)}, f32[64,6]{0,1:T(8,128)}, u32[]{:S(2)}) copy-start(f32[64,6]{0,1:T(8,128)} %param.15) | copy-start | bytes 4612
  4.7 5.7 %copy-start.2 = (bf16[64,2560]{1,0:T(8,128)(2,1)S(1)}, bf16[64,2560]{1,0:T(8,128)(2,1)}, u32[]{:S(2)}) copy-start(bf16[64,2560]{1,0:T(8,128)(2,1)} %param.11) | copy-start | bytes 983044
  8.8 1.9 %copy-start.4 = (f32[2560]{0:T(1024)S(1)}, f32[2560]{0:T(1024)}, u32[]{:S(2)}) copy-start(f32[2560]{0:T(1024)} %param.13) | copy-start | bytes 30724
  8.8 1.6 %collective-permute-start.1 = (bf16[64,1280]{1,0:T(8,128)(2,1)S(1)}, bf16[64,1280]{1,0:T(8,128)(2,1)S(1)}, u32[]{:S(2)}, u32[]{:S(2)}) collective-permute-start(bf16[64,1280]{1,0:T(8,128)(2,1)S(1)} %slice.34), channel_id=1, source_target_pairs={{0,1},{1,0},{2,3},{3,2},{4,5},{5,4},{6,7},{7,6},{8,9},{9,8},{10,11... | collective-permute-start | bytes 491528 | tf_op jit(solution)/shard_map/ppermute | solution.py:62
  16.3 52.5 %all-to-all-start = ((bf16[64,180,128]{2,1,0:T(8,128)(2,1)}), bf16[64,180,128]{2,1,0:T(8,128)(2,1)S(1)}, u32[]{:S(2)}, u32[]{:S(2)}) async-start(bf16[64,180,128]{2,1,0:T(8,128)(2,1)} %reshape.61), calls=%async_computation | async-start | bytes 6029312 | tf_op jit(solution)/shard_map/all_to_all | solution.py:25
  27.8 53.4 %collective-permute-start.2 = (bf16[2560,768]{1,0:T(8,128)(2,1)}, bf16[2560,768]{1,0:T(8,128)(2,1)}, u32[]{:S(2)}, u32[]{:S(2)}) collective-permute-start(bf16[2560,768]{1,0:T(8,128)(2,1)} %bitcast.38), channel_id=1, source_target_pairs={{0,1},{1,0},{2,3},{3,2},{4,5},{5,4},{6,7},{7,6},{8,9},{9,8},{10,11... | collective-permute-start | bytes 11796488 | tf_op jit(solution)/shard_map/ppermute | solution.py:52
  28.0 57.8 %collective-permute-start.3 = (bf16[2560,768]{1,0:T(8,128)(2,1)}, bf16[2560,768]{1,0:T(8,128)(2,1)}, u32[]{:S(2)}, u32[]{:S(2)}) collective-permute-start(bf16[2560,768]{1,0:T(8,128)(2,1)} %bitcast.39), channel_id=1, source_target_pairs={{0,1},{1,0},{2,3},{3,2},{4,5},{5,4},{6,7},{7,6},{8,9},{9,8},{10,11... | collective-permute-start | bytes 11796488 | tf_op jit(solution)/shard_map/ppermute | solution.py:53
  28.4 62.3 %collective-permute-start.4 = (bf16[1536,1280]{1,0:T(8,128)(2,1)}, bf16[1536,1280]{1,0:T(8,128)(2,1)}, u32[]{:S(2)}, u32[]{:S(2)}) collective-permute-start(bf16[1536,1280]{1,0:T(8,128)(2,1)} %bitcast.40), channel_id=1, source_target_pairs={{0,1},{1,0},{2,3},{3,2},{4,5},{5,4},{6,7},{7,6},{8,9},{9,8},{10,11... | collective-permute-start | bytes 11796488 | tf_op jit(solution)/shard_map/ppermute | solution.py:54
  73.0 5.6 %copy-start = (bf16[576,2560]{1,0:T(8,128)(2,1)S(1)}, bf16[576,2560]{1,0:T(8,128)(2,1)}, u32[]{:S(2)}) copy-start(bf16[576,2560]{1,0:T(8,128)(2,1)} %reshape.62) | copy-start | bytes 8847364
  73.0 5.6 %copy-start.6 = (bf16[1,2560,768]{2,1,0:T(8,128)(2,1)S(1)}, bf16[1,2560,768]{2,1,0:T(8,128)(2,1)}, u32[]{:S(2)}) copy-start(bf16[1,2560,768]{2,1,0:T(8,128)(2,1)} %param.17) | copy-start | bytes 11796484
  85.8 4.9 %copy-start.7 = (bf16[1,1536,1280]{2,1,0:T(8,128)(2,1)S(1)}, bf16[1,1536,1280]{2,1,0:T(8,128)(2,1)}, u32[]{:S(2)}) copy-start(bf16[1,1536,1280]{2,1,0:T(8,128)(2,1)} %param.18) | copy-start | bytes 11796484
  156.9 1.0 copy-start.5
  157.9 0.9 copy-start.1

commit v10 on v9

--- a/solution.py
+++ b/solution.py
@@ -86,13 +86,13 @@
         up_part = jnp.dot(rows, up_w, preferred_element_type=jnp.float32)
         return (jax.nn.silu(gate_part) * up_part).astype(jnp.bfloat16)
 
-    hidden_mine = hidden_of(own_rows, gate_local, up_local)
-    hidden_theirs = hidden_of(own_rows, gate_partner, up_partner)
-    hidden_full = jnp.where(
-        me == 0,
-        jnp.concatenate([hidden_mine, hidden_theirs], axis=1),
-        jnp.concatenate([hidden_theirs, hidden_mine], axis=1),
+    hidden_pair = hidden_of(
+        own_rows,
+        jnp.concatenate([gate_local, gate_partner], axis=1),
+        jnp.concatenate([up_local, up_partner], axis=1),
     )
+    swapped = jnp.concatenate([hidden_pair[:, ff_half:], hidden_pair[:, :ff_half]], axis=1)
+    hidden_full = jnp.where(me == 0, hidden_pair, swapped)
     joined = jnp.dot(
         hidden_full,
         jnp.concatenate([down_local, down_partner], axis=1),

time: 159 us -> 159 us (level)
  waiting for transfers between devices: 41 us -> 44 us
  matrix products: 32.4 us -> 30.4 us
    ppermute x1, waiting for transfers between devices: 0.73 us -> 3.63 us  [per_device(): lax.ppermute(cols_partner.astype(jnp.bfloat16), 'dp', swap)]
    dot_general x2 -> x1, matrix products: 10.2 us -> 8.3 us  [hidden_of(): gate_part = jnp.dot(rows, gate_w, preferred_element_type=jnp.float32)]
    dot_general x2 -> x1, matrix products: 7.43 us -> 7.24 us  [hidden_of(): up_part = jnp.dot(rows, up_w, preferred_element_type=jnp.float32)]
  transfers between devices with their start and end apart: 6 -> 6, of which waited for: 2 -> 2; matrix products, arithmetic and copies ran while one was open for 16% -> 21% of each run, Pallas kernels for 0% -> 0%
where the time goes in v10:
time: 159 us
  blocking collectives  45.9 us (29%)
  waiting for transfers between devices  44 us (28%)
  matrix products  30.4 us (19%)
  local copies, waits for them, and re-layouts  20.4 us (13%)
  starting transfers between devices  12.9 us (8%)
  other arithmetic  4.09 us (3%)
    all_to_all x1, blocking collectives, exchange_rows(): moved = lax.all_to_all(wire, 'ep', split_axis=0, concat_axis=0, tiled=True)  45.9 us
    all_to_all x1, waiting for transfers between devices, exchange_rows(): moved = lax.all_to_all(wire, 'ep', split_axis=0, concat_axis=0, tiled=True)  40.3 us
    all_to_all x1, starting transfers between devices, exchange_rows(): moved = lax.all_to_all(wire, 'ep', split_axis=0, concat_axis=0, tiled=True)  11.5 us
    reshape x2, local copies, waits for them, and re-layouts, exchange_rows(): wire = rows.reshape(experts, total * width // (experts * lanes), lanes)  9.66 us
    reshape x2, local copies, waits for them, and re-layouts, exchange_rows(): return moved.reshape(total, width)  8.99 us
    dot_general x1, matrix products, per_device(): jnp.dot(hidden_full, jnp.concatenate([down_local, down_partner], axis=1),...  8.48 us
    dot_general x1, matrix products, hidden_of(): gate_part = jnp.dot(rows, gate_w, preferred_element_type=jnp.float32)  8.3 us
    dot_general x1, matrix products, hidden_of(): up_part = jnp.dot(rows, up_w, preferred_element_type=jnp.float32)  7.24 us
  transfers between devices with their start and end apart: 6, of which 2 were waited for; matrix products, arithmetic and copies ran while one was open for 21% of the time, Pallas kernels for 0%

profile of v10, /device:TPU:0, one launch (start us, length us, event | category | flops | bytes accessed | tf_op | source)
XLA Modules:
  0.0 158.6 jit_solution(12175618180881087354)
XLA Ops:
  0.7 0.5 collective-permute-start.2
  1.3 0.8 copy.26
  2.1 0.1 eq.48
  2.2 0.1 eq.44
  2.4 0.9 reduce-window.6
  3.3 0.2 slice_reduce_fusion
  3.6 0.1 fusion.36
  3.7 0.1 reduce_sum.57
  3.9 0.7 reduce_sum.58
  4.6 0.7 multiply_add_fusion
  5.3 4.0 %fusion.25 = f32[128,1280]{1,0:T(8,128)S(1)} fusion(bf16[2560,1280]{1,0:T(8,128)(2,1)} %param.12, bf16[64,2560]{1,0:T(8,128)(2,1)S(1)} %collective-permute-done, bf16[64,2560]{1,0:T(8,128)(2,1)} %param.10), kind=kOutput, calls=%fused_computation.35 | convolution fusion | flops 840171520 | bytes 7864320 | tf_op jit(solution)/shard_map/dot_general | solution.py:56
  9.4 0.5 collective-permute-start.1
  9.9 0.3 select_reduce_fusion
  10.2 3.6 %collective-permute-done.1 = bf16[64,1280]{1,0:T(8,128)(2,1)S(1)} collective-permute-done((bf16[64,1280]{1,0:T(8,128)(2,1)S(1)}, bf16[64,1280]{1,0:T(8,128)(2,1)S(1)}, u32[]{:S(2)}, u32[]{:S(2)}) %collective-permute-start.1) | collective-permute-done | bytes 163872 | tf_op jit(solution)/shard_map/ppermute | solution.py:62
  13.9 0.2 fusion.21
  14.1 1.0 convolution_convert_fusion
  15.1 4.6 %reshape.61 = bf16[64,180,128]{2,1,0:T(8,128)(2,1)} reshape(bf16[576,2560]{1,0:T(8,128)(2,1)S(1)} %convolution_convert_fusion) | data formatting | bytes 5898240 | tf_op jit(solution)/shard_map/reshape | solution.py:24
  19.7 11.5 %all-to-all-start = ((bf16[64,180,128]{2,1,0:T(8,128)(2,1)}), bf16[64,180,128]{2,1,0:T(8,128)(2,1)S(1)}, u32[]{:S(2)}, u32[]{:S(2)}) async-start(bf16[64,180,128]{2,1,0:T(8,128)(2,1)} %reshape.61), calls=%async_computation | async-start | bytes 6029312 | tf_op jit(solution)/shard_map/all_to_all | solution.py:25
  31.2 0.3 collective-permute-start.4
  31.5 40.3 %all-to-all-done = bf16[64,180,128]{2,1,0:T(8,128)(2,1)S(1)} async-done(((bf16[64,180,128]{2,1,0:T(8,128)(2,1)}), bf16[64,180,128]{2,1,0:T(8,128)(2,1)S(1)}, u32[]{:S(2)}, u32[]{:S(2)}) %all-to-all-start) | async-done | bytes 2949152 | tf_op jit(solution)/shard_map/all_to_all | solution.py:25
  71.8 4.2 %reshape.62 = bf16[576,2560]{1,0:T(8,128)(2,1)} reshape(bf16[64,180,128]{2,1,0:T(8,128)(2,1)S(1)} %all-to-all-done) | data formatting | bytes 5898240 | tf_op jit(solution)/shard_map/reshape | solution.py:26
  76.0 8.3 %fusion = f32[576,1536]{1,0:T(8,128)S(1)} fusion(bf16[576,2560]{1,0:T(8,128)(2,1)} %reshape.62, bf16[2560,768]{1,0:T(8,128)(2,1)} %collective-permute-done.2, bf16[2560,768]{1,0:T(8,128)(2,1)} %bitcast.31), kind=kOutput, calls=%fused_computation | convolution fusion | flops 4545576960 | bytes 14352384 | tf_op jit(solution)/shard_map/dot_general | solution.py:85
  84.4 7.2 %multiply_convert_fusion = bf16[576,1536]{1,0:T(8,128)(2,1)S(1)} fusion(f32[576,1536]{1,0:T(8,128)S(1)} %fusion, bf16[576,2560]{1,0:T(8,128)(2,1)S(1)} %copy-done, bf16[2560,768]{1,0:T(8,128)(2,1)} %collective-permute-done.3, bf16[2560,768]{1,0:T(8,128)(2,1)S(1)} %bitcast.33), kind=kOutput, calls=%fused_computation.14 | convolution fusion | flops 4550885376 | bytes 16121856 | tf_op jit(solution)/shard_map/dot_general | solution.py:86
  91.6 0.1 fusion.50
  91.8 8.5 %fusion.12 = bf16[576,2560]{1,0:T(8,128)(2,1)} fusion(bf16[1536,1280]{1,0:T(8,128)(2,1)} %collective-permute-done.4, bf16[1536,1280]{1,0:T(8,128)(2,1)S(1)} %bitcast.35, bf16[576,1536]{1,0:T(8,128)(2,1)S(1)} %multiply_convert_fusion, bf16[576,768]{1,0:T(8,128)(2,1)S(1)} %get-tuple-element.9, bf16[576,768]{1,0:T(8,128)(2,1)S(1)} %get-tuple-element.8, ...), kind=kOutput, calls=%fused_computation.12 | convolution fusion | flops 4551475200 | bytes 14352385 | tf_op jit(solution)/shard_map/dot_general | solution.py:96
  100.2 5.1 %reshape.63 = bf16[64,180,128]{2,1,0:T(8,128)(2,1)S(1)} reshape(bf16[576,2560]{1,0:T(8,128)(2,1)} %fusion.12) | data formatting | bytes 5898240 | tf_op jit(solution)/shard_map/reshape | solution.py:24
  105.3 45.9 %all_to_all.10 = bf16[64,180,128]{2,1,0:T(8,128)(2,1)} all-to-all(bf16[64,180,128]{2,1,0:T(8,128)(2,1)S(1)} %reshape.63), channel_id=1, replica_groups=mesh['ep'=64,'dp'=2] {'ep'}, dimensions={0} | all-to-all | bytes 5898240 | tf_op jit(solution)/shard_map/all_to_all | solution.py:25
  151.3 4.8 %reshape.64 = bf16[576,2560]{1,0:T(8,128)(2,1)S(1)} reshape(bf16[64,180,128]{2,1,0:T(8,128)(2,1)} %all_to_all.10) | data formatting | bytes 5898240 | tf_op jit(solution)/shard_map/reshape | solution.py:26
  156.0 0.7 fusion.40
  156.7 0.7 convolution_add_fusion
  157.4 0.2 fusion.18
  157.7 0.9 fusion.20
  (32 shorter events, 0.5 us)
Async XLA Ops:
  0.6 4.7 %collective-permute-start = (bf16[64,2560]{1,0:T(8,128)(2,1)}, bf16[64,2560]{1,0:T(8,128)(2,1)S(1)}, u32[]{:S(2)}, u32[]{:S(2)}) collective-permute-start(bf16[64,2560]{1,0:T(8,128)(2,1)} %param.10), channel_id=1, source_target_pairs={{0,1},{1,0},{2,3},{3,2},{4,5},{5,4},{6,7},{7,6},{8,9},{9,8},{10,11... | collective-permute-start | bytes 983048 | tf_op jit(solution)/shard_map/ppermute | solution.py:55
  0.7 75.3 %collective-permute-start.2 = (bf16[2560,768]{1,0:T(8,128)(2,1)}, bf16[2560,768]{1,0:T(8,128)(2,1)}, u32[]{:S(2)}, u32[]{:S(2)}) collective-permute-start(bf16[2560,768]{1,0:T(8,128)(2,1)} %bitcast.30), channel_id=1, source_target_pairs={{0,1},{1,0},{2,3},{3,2},{4,5},{5,4},{6,7},{7,6},{8,9},{9,8},{10,11... | collective-permute-start | bytes 11796488 | tf_op jit(solution)/shard_map/ppermute | solution.py:52
  1.2 83.1 %collective-permute-start.3 = (bf16[2560,768]{1,0:T(8,128)(2,1)}, bf16[2560,768]{1,0:T(8,128)(2,1)}, u32[]{:S(2)}, u32[]{:S(2)}) collective-permute-start(bf16[2560,768]{1,0:T(8,128)(2,1)} %bitcast.32), channel_id=1, source_target_pairs={{0,1},{1,0},{2,3},{3,2},{4,5},{5,4},{6,7},{7,6},{8,9},{9,8},{10,11... | collective-permute-start | bytes 11796488 | tf_op jit(solution)/shard_map/ppermute | solution.py:53
  5.3 4.6 %copy-start.3 = (f32[64,6]{0,1:T(8,128)S(1)}, f32[64,6]{0,1:T(8,128)}, u32[]{:S(2)}) copy-start(f32[64,6]{0,1:T(8,128)} %param.15) | copy-start | bytes 4612
  5.3 8.5 %copy-start.2 = (bf16[64,2560]{1,0:T(8,128)(2,1)S(1)}, bf16[64,2560]{1,0:T(8,128)(2,1)}, u32[]{:S(2)}) copy-start(bf16[64,2560]{1,0:T(8,128)(2,1)} %param.11) | copy-start | bytes 983044
  5.3 8.8 %copy-start.4 = (f32[2560]{0:T(1024)S(1)}, f32[2560]{0:T(1024)}, u32[]{:S(2)}) copy-start(f32[2560]{0:T(1024)} %param.13) | copy-start | bytes 30724
  9.4 4.4 %collective-permute-start.1 = (bf16[64,1280]{1,0:T(8,128)(2,1)S(1)}, bf16[64,1280]{1,0:T(8,128)(2,1)S(1)}, u32[]{:S(2)}, u32[]{:S(2)}) collective-permute-start(bf16[64,1280]{1,0:T(8,128)(2,1)S(1)} %slice.44), channel_id=1, source_target_pairs={{0,1},{1,0},{2,3},{3,2},{4,5},{5,4},{6,7},{7,6},{8,9},{9,8},{10,11... | collective-permute-start | bytes 491528 | tf_op jit(solution)/shard_map/ppermute | solution.py:62
  19.7 52.1 %all-to-all-start = ((bf16[64,180,128]{2,1,0:T(8,128)(2,1)}), bf16[64,180,128]{2,1,0:T(8,128)(2,1)S(1)}, u32[]{:S(2)}, u32[]{:S(2)}) async-start(bf16[64,180,128]{2,1,0:T(8,128)(2,1)} %reshape.61), calls=%async_computation | async-start | bytes 6029312 | tf_op jit(solution)/shard_map/all_to_all | solution.py:25
  31.2 60.5 %collective-permute-start.4 = (bf16[1536,1280]{1,0:T(8,128)(2,1)}, bf16[1536,1280]{1,0:T(8,128)(2,1)}, u32[]{:S(2)}, u32[]{:S(2)}) collective-permute-start(bf16[1536,1280]{1,0:T(8,128)(2,1)} %bitcast.34), channel_id=1, source_target_pairs={{0,1},{1,0},{2,3},{3,2},{4,5},{5,4},{6,7},{7,6},{8,9},{9,8},{10,11... | collective-permute-start | bytes 11796488 | tf_op jit(solution)/shard_map/ppermute | solution.py:54
  76.0 8.3 %copy-start = (bf16[576,2560]{1,0:T(8,128)(2,1)S(1)}, bf16[576,2560]{1,0:T(8,128)(2,1)}, u32[]{:S(2)}) copy-start(bf16[576,2560]{1,0:T(8,128)(2,1)} %reshape.62) | copy-start | bytes 8847364
  76.0 8.3 %copy-start.6 = (bf16[1,2560,768]{2,1,0:T(8,128)(2,1)S(1)}, bf16[1,2560,768]{2,1,0:T(8,128)(2,1)}, u32[]{:S(2)}) copy-start(bf16[1,2560,768]{2,1,0:T(8,128)(2,1)} %param.17) | copy-start | bytes 11796484
  84.4 7.4 %copy-start.7 = (bf16[1,1536,1280]{2,1,0:T(8,128)(2,1)S(1)}, bf16[1,1536,1280]{2,1,0:T(8,128)(2,1)}, u32[]{:S(2)}) copy-start(bf16[1,1536,1280]{2,1,0:T(8,128)(2,1)} %param.18) | copy-start | bytes 11796484
  156.7 1.0 copy-start.5
  157.7 0.9 copy-start.1

commit v11 on v10

--- a/solution.py
+++ b/solution.py
@@ -49,9 +49,6 @@
     gate_local = gate_weight[0]
     up_local = up_weight[0]
     down_local = down_weight[0]
-    gate_partner = lax.ppermute(gate_local, "dp", swap)
-    up_partner = lax.ppermute(up_local, "dp", swap)
-    down_partner = lax.ppermute(down_local, "dp", swap)
     partner_att = lax.ppermute(attention_out, "dp", swap)
     cols = jnp.dot(
         jnp.concatenate([attention_out, partner_att], axis=0),
@@ -60,6 +57,12 @@
     )
     cols_own, cols_partner = cols[:tok_rows], cols[tok_rows:]
     cols_in = lax.ppermute(cols_partner.astype(jnp.bfloat16), "dp", swap).astype(jnp.float32)
+    gate_send, up_send, down_send, cols_in = lax.optimization_barrier(
+        (gate_local, up_local, down_local, cols_in)
+    )
+    gate_partner = lax.ppermute(gate_send, "dp", swap)
+    up_partner = lax.ppermute(up_send, "dp", swap)
+    down_partner = lax.ppermute(down_send, "dp", swap)
     home_cols = jnp.where(
         me == 0,
         jnp.concatenate([cols_own, cols_in], axis=1),

time: 159 us -> 158 us (level)
  waiting for transfers between devices: 44 us -> 41.7 us
    ppermute x1, waiting for transfers between devices: 3.63 us -> 1.02 us  [per_device(): lax.ppermute(cols_partner.astype(jnp.bfloat16), 'dp', swap)]
  transfers between devices with their start and end apart: 6 -> 6, of which waited for: 2 -> 2; matrix products, arithmetic and copies ran while one was open for 21% -> 19% of each run, Pallas kernels for 0% -> 0%
where the time goes in v11:
time: 158 us; the launch traced here: 157 us
  blocking collectives  47.3 us (30%)
  waiting for transfers between devices  41.7 us (26%)
  matrix products  30.4 us (19%)
  local copies, waits for them, and re-layouts  20.4 us (13%)
  starting transfers between devices  13.2 us (8%)
  other arithmetic  3.41 us (2%)
    all_to_all x1, blocking collectives, exchange_rows(): moved = lax.all_to_all(wire, 'ep', split_axis=0, concat_axis=0, tiled=True)  47.3 us
    all_to_all x1, waiting for transfers between devices, exchange_rows(): moved = lax.all_to_all(wire, 'ep', split_axis=0, concat_axis=0, tiled=True)  40.6 us
    all_to_all x1, starting transfers between devices, exchange_rows(): moved = lax.all_to_all(wire, 'ep', split_axis=0, concat_axis=0, tiled=True)  11.5 us
    reshape x2, local copies, waits for them, and re-layouts, exchange_rows(): wire = rows.reshape(experts, total * width // (experts * lanes), lanes)  9.66 us
    reshape x2, local copies, waits for them, and re-layouts, exchange_rows(): return moved.reshape(total, width)  8.99 us
    dot_general x1, matrix products, per_device(): jnp.dot(hidden_full, jnp.concatenate([down_local, down_partner], axis=1),...  8.48 us
    dot_general x1, matrix products, hidden_of(): gate_part = jnp.dot(rows, gate_w, preferred_element_type=jnp.float32)  8.3 us
    dot_general x1, matrix products, hidden_of(): up_part = jnp.dot(rows, up_w, preferred_element_type=jnp.float32)  7.23 us
  transfers between devices with their start and end apart: 6, of which 2 were waited for; matrix products, arithmetic and copies ran while one was open for 19% of the time, Pallas kernels for 0%

profile of v11, /device:TPU:0, one launch (start us, length us, event | category | flops | bytes accessed | tf_op | source)
XLA Modules:
  0.0 157.2 jit_solution(1762106763995664538)
XLA Ops:
  0.7 0.8 copy.26
  1.5 0.1 eq.48
  1.7 0.1 eq.44
  1.8 0.9 reduce-window.6
  2.7 0.2 slice_reduce_fusion
  3.0 0.1 fusion.36
  3.1 0.1 reduce_sum.57
  3.3 0.7 reduce_sum.58
  4.1 4.0 %fusion.25 = f32[128,1280]{1,0:T(8,128)S(1)} fusion(bf16[2560,1280]{1,0:T(8,128)(2,1)} %param.12, bf16[64,2560]{1,0:T(8,128)(2,1)S(1)} %collective-permute-done, bf16[64,2560]{1,0:T(8,128)(2,1)} %param.10), kind=kOutput, calls=%fused_computation.35 | convolution fusion | flops 840171520 | bytes 7864320 | tf_op jit(solution)/shard_map/dot_general | solution.py:53
  8.1 0.6 collective-permute-start.1
  8.7 1.0 collective-permute-done.1
  9.8 0.4 collective-permute-start.2
  10.2 0.3 select_reduce_fusion
  10.5 0.2 collective-permute-start.3
  10.7 0.2 fusion.21
  11.0 1.0 convolution_convert_fusion
  12.0 4.6 %reshape.61 = bf16[64,180,128]{2,1,0:T(8,128)(2,1)} reshape(bf16[576,2560]{1,0:T(8,128)(2,1)S(1)} %convolution_convert_fusion) | data formatting | bytes 5898240 | tf_op jit(solution)/shard_map/reshape | solution.py:24
  16.6 11.5 %all-to-all-start = ((bf16[64,180,128]{2,1,0:T(8,128)(2,1)}), bf16[64,180,128]{2,1,0:T(8,128)(2,1)S(1)}, u32[]{:S(2)}, u32[]{:S(2)}) async-start(bf16[64,180,128]{2,1,0:T(8,128)(2,1)} %reshape.61), calls=%async_computation | async-start | bytes 6029312 | tf_op jit(solution)/shard_map/all_to_all | solution.py:25
  28.1 0.3 collective-permute-start.4
  28.4 40.6 %all-to-all-done = bf16[64,180,128]{2,1,0:T(8,128)(2,1)S(1)} async-done(((bf16[64,180,128]{2,1,0:T(8,128)(2,1)}), bf16[64,180,128]{2,1,0:T(8,128)(2,1)S(1)}, u32[]{:S(2)}, u32[]{:S(2)}) %all-to-all-start) | async-done | bytes 2949152 | tf_op jit(solution)/shard_map/all_to_all | solution.py:25
  69.1 4.2 %reshape.62 = bf16[576,2560]{1,0:T(8,128)(2,1)} reshape(bf16[64,180,128]{2,1,0:T(8,128)(2,1)S(1)} %all-to-all-done) | data formatting | bytes 5898240 | tf_op jit(solution)/shard_map/reshape | solution.py:26
  73.3 8.3 %fusion = f32[576,1536]{1,0:T(8,128)S(1)} fusion(bf16[576,2560]{1,0:T(8,128)(2,1)} %reshape.62, bf16[2560,768]{1,0:T(8,128)(2,1)} %collective-permute-done.2, bf16[2560,768]{1,0:T(8,128)(2,1)} %bitcast), kind=kOutput, calls=%fused_computation | convolution fusion | flops 4545576960 | bytes 14352384 | tf_op jit(solution)/shard_map/dot_general | solution.py:88
  81.6 7.2 %multiply_convert_fusion = bf16[576,1536]{1,0:T(8,128)(2,1)S(1)} fusion(f32[576,1536]{1,0:T(8,128)S(1)} %fusion, bf16[576,2560]{1,0:T(8,128)(2,1)S(1)} %copy-done, bf16[2560,768]{1,0:T(8,128)(2,1)} %collective-permute-done.3, bf16[2560,768]{1,0:T(8,128)(2,1)S(1)} %bitcast.31), kind=kOutput, calls=%fused_computation.14 | convolution fusion | flops 4550885376 | bytes 16121856 | tf_op jit(solution)/shard_map/dot_general | solution.py:89
  88.9 0.1 fusion.50
  89.0 8.5 %fusion.12 = bf16[576,2560]{1,0:T(8,128)(2,1)} fusion(bf16[1536,1280]{1,0:T(8,128)(2,1)} %collective-permute-done.4, bf16[1536,1280]{1,0:T(8,128)(2,1)S(1)} %bitcast.33, bf16[576,1536]{1,0:T(8,128)(2,1)S(1)} %multiply_convert_fusion, bf16[576,768]{1,0:T(8,128)(2,1)S(1)} %get-tuple-element.17, bf16[576,768]{1,0:T(8,128)(2,1)S(1)} %get-tuple-element.16, ...), kind=kOutput, calls=%fused_computation.12 | convolution fusion | flops 4551475200 | bytes 14352385 | tf_op jit(solution)/shard_map/dot_general | solution.py:99
  97.5 5.1 %reshape.63 = bf16[64,180,128]{2,1,0:T(8,128)(2,1)S(1)} reshape(bf16[576,2560]{1,0:T(8,128)(2,1)} %fusion.12) | data formatting | bytes 5898240 | tf_op jit(solution)/shard_map/reshape | solution.py:24
  102.6 47.3 %all_to_all.10 = bf16[64,180,128]{2,1,0:T(8,128)(2,1)} all-to-all(bf16[64,180,128]{2,1,0:T(8,128)(2,1)S(1)} %reshape.63), channel_id=1, replica_groups=mesh['ep'=64,'dp'=2] {'ep'}, dimensions={0} | all-to-all | bytes 5898240 | tf_op jit(solution)/shard_map/all_to_all | solution.py:25
  149.8 4.8 %reshape.64 = bf16[576,2560]{1,0:T(8,128)(2,1)S(1)} reshape(bf16[64,180,128]{2,1,0:T(8,128)(2,1)} %all_to_all.10) | data formatting | bytes 5898240 | tf_op jit(solution)/shard_map/reshape | solution.py:26
  154.6 0.7 fusion.40
  155.3 0.7 convolution_add_fusion
  156.0 0.2 fusion.18
  156.3 0.9 fusion.20
  (34 shorter events, 0.4 us)
Async XLA Ops:
  0.6 3.4 %collective-permute-start = (bf16[64,2560]{1,0:T(8,128)(2,1)}, bf16[64,2560]{1,0:T(8,128)(2,1)S(1)}, u32[]{:S(2)}, u32[]{:S(2)}) collective-permute-start(bf16[64,2560]{1,0:T(8,128)(2,1)} %param.10), channel_id=1, source_target_pairs={{0,1},{1,0},{2,3},{3,2},{4,5},{5,4},{6,7},{7,6},{8,9},{9,8},{10,11... | collective-permute-start | bytes 983048 | tf_op jit(solution)/shard_map/ppermute | solution.py:52
  4.0 4.7 %copy-start.3 = (s32[64,6]{0,1:T(8,128)S(1)}, s32[64,6]{0,1:T(8,128)}, u32[]{:S(2)}) copy-start(s32[64,6]{0,1:T(8,128)} %param.14) | copy-start | bytes 4612
  4.0 6.2 %copy-start.4 = (f32[64,6]{0,1:T(8,128)S(1)}, f32[64,6]{0,1:T(8,128)}, u32[]{:S(2)}) copy-start(f32[64,6]{0,1:T(8,128)} %param.15) | copy-start | bytes 4612
  4.0 6.7 %copy-start.2 = (bf16[64,2560]{1,0:T(8,128)(2,1)S(1)}, bf16[64,2560]{1,0:T(8,128)(2,1)}, u32[]{:S(2)}) copy-start(bf16[64,2560]{1,0:T(8,128)(2,1)} %param.11) | copy-start | bytes 983044
  4.0 6.9 %copy-start.5 = (f32[2560]{0:T(1024)S(1)}, f32[2560]{0:T(1024)}, u32[]{:S(2)}) copy-start(f32[2560]{0:T(1024)} %param.13) | copy-start | bytes 30724
  8.1 1.6 %collective-permute-start.1 = (bf16[64,1280]{1,0:T(8,128)(2,1)S(1)}, bf16[64,1280]{1,0:T(8,128)(2,1)S(1)}, u32[]{:S(2)}, u32[]{:S(2)}) collective-permute-start(bf16[64,1280]{1,0:T(8,128)(2,1)S(1)} %slice.44), channel_id=1, source_target_pairs={{0,1},{1,0},{2,3},{3,2},{4,5},{5,4},{6,7},{7,6},{8,9},{9,8},{10,11... | collective-permute-start | bytes 491528 | tf_op jit(solution)/shard_map/ppermute | solution.py:59
  9.8 63.5 %collective-permute-start.2 = (bf16[2560,768]{1,0:T(8,128)(2,1)}, bf16[2560,768]{1,0:T(8,128)(2,1)}, u32[]{:S(2)}, u32[]{:S(2)}) collective-permute-start(bf16[2560,768]{1,0:T(8,128)(2,1)} %bitcast), channel_id=1, source_target_pairs={{0,1},{1,0},{2,3},{3,2},{4,5},{5,4},{6,7},{7,6},{8,9},{9,8},{10,11... | collective-permute-start | bytes 11796488 | tf_op jit(solution)/shard_map/ppermute | solution.py:63
  10.5 71.1 %collective-permute-start.3 = (bf16[2560,768]{1,0:T(8,128)(2,1)}, bf16[2560,768]{1,0:T(8,128)(2,1)}, u32[]{:S(2)}, u32[]{:S(2)}) collective-permute-start(bf16[2560,768]{1,0:T(8,128)(2,1)} %bitcast.30), channel_id=1, source_target_pairs={{0,1},{1,0},{2,3},{3,2},{4,5},{5,4},{6,7},{7,6},{8,9},{9,8},{10,11... | collective-permute-start | bytes 11796488 | tf_op jit(solution)/shard_map/ppermute | solution.py:64
  16.6 52.5 %all-to-all-start = ((bf16[64,180,128]{2,1,0:T(8,128)(2,1)}), bf16[64,180,128]{2,1,0:T(8,128)(2,1)S(1)}, u32[]{:S(2)}, u32[]{:S(2)}) async-start(bf16[64,180,128]{2,1,0:T(8,128)(2,1)} %reshape.61), calls=%async_computation | async-start | bytes 6029312 | tf_op jit(solution)/shard_map/all_to_all | solution.py:25
  28.1 60.9 %collective-permute-start.4 = (bf16[1536,1280]{1,0:T(8,128)(2,1)}, bf16[1536,1280]{1,0:T(8,128)(2,1)}, u32[]{:S(2)}, u32[]{:S(2)}) collective-permute-start(bf16[1536,1280]{1,0:T(8,128)(2,1)} %bitcast.32), channel_id=1, source_target_pairs={{0,1},{1,0},{2,3},{3,2},{4,5},{5,4},{6,7},{7,6},{8,9},{9,8},{10,11... | collective-permute-start | bytes 11796488 | tf_op jit(solution)/shard_map/ppermute | solution.py:65
  73.3 8.3 %copy-start = (bf16[576,2560]{1,0:T(8,128)(2,1)S(1)}, bf16[576,2560]{1,0:T(8,128)(2,1)}, u32[]{:S(2)}) copy-start(bf16[576,2560]{1,0:T(8,128)(2,1)} %reshape.62) | copy-start | bytes 8847364
  73.3 8.3 %copy-start.7 = (bf16[1,2560,768]{2,1,0:T(8,128)(2,1)S(1)}, bf16[1,2560,768]{2,1,0:T(8,128)(2,1)}, u32[]{:S(2)}) copy-start(bf16[1,2560,768]{2,1,0:T(8,128)(2,1)} %param.17) | copy-start | bytes 11796484
  81.6 7.4 %copy-start.8 = (bf16[1,1536,1280]{2,1,0:T(8,128)(2,1)S(1)}, bf16[1,1536,1280]{2,1,0:T(8,128)(2,1)}, u32[]{:S(2)}) copy-start(bf16[1,1536,1280]{2,1,0:T(8,128)(2,1)} %param.18) | copy-start | bytes 11796484
  155.3 1.0 copy-start.6
  156.3 0.9 copy-start.1

commit v12 on v11

--- a/solution.py
+++ b/solution.py
@@ -104,8 +104,11 @@
     returned = exchange_rows(joined, experts)
     mixing_hi = mixing.astype(jnp.bfloat16)
     mixing_lo = (mixing - mixing_hi.astype(jnp.float32)).astype(jnp.bfloat16)
-    expert_sum = jnp.dot(mixing_hi, returned, preferred_element_type=jnp.float32)
-    expert_sum = expert_sum + jnp.dot(mixing_lo, returned, preferred_element_type=jnp.float32)
+    expert_sum = jnp.dot(
+        jnp.concatenate([mixing_hi, mixing_lo], axis=1),
+        jnp.concatenate([returned, returned], axis=0),
+        preferred_element_type=jnp.float32,
+    )
     expert_sum = jnp.where(me == 0, expert_sum, jnp.roll(expert_sum, part_cols, axis=1))
     new_state = (summed.astype(jnp.float32) + expert_sum).astype(jnp.bfloat16)
     normed_state = rms_scale(new_state, post_gain).astype(jnp.bfloat16)

time: 158 us -> 157 us (level)
  blocking collectives: 47.3 us -> 0 us
  waiting for transfers between devices: 41.7 us -> 81.3 us
  starting transfers between devices: 13.2 us -> 20.4 us
    all_to_all x1 -> x0, blocking collectives: 47.3 us -> none  [exchange_rows(): moved = lax.all_to_all(wire, 'ep', split_axis=0, concat_axis=0, tiled=True)]
    all_to_all x1 -> x2, waiting for transfers between devices: 40.6 us -> 80.3 us  [exchange_rows(): moved = lax.all_to_all(wire, 'ep', split_axis=0, concat_axis=0, tiled=True)]
    all_to_all x1 -> x2, starting transfers between devices: 11.5 us -> 18.7 us  [exchange_rows(): moved = lax.all_to_all(wire, 'ep', split_axis=0, concat_axis=0, tiled=True)]
    dot_general x2 -> x1, matrix products: 1.33 us -> 3.46 us  [per_device(): jnp.dot(jnp.concatenate([mixing_hi, mixing_lo], axis=1), jnp.concatenate(...]
    dot_general x1, matrix products: 8.48 us -> 6.85 us  [per_device(): jnp.dot(hidden_full, jnp.concatenate([down_local, down_partner], axis=1),...]
  transfers between devices with their start and end apart: 6 -> 7, of which waited for: 2 -> 3; matrix products, arithmetic and copies ran while one was open for 19% -> 19% of each run, Pallas kernels for 0% -> 0%
where the time goes in v12:
time: 157 us
  waiting for transfers between devices  81.3 us (52%)
  matrix products  30.9 us (20%)
  starting transfers between devices  20.4 us (13%)
  local copies, waits for them, and re-layouts  19.3 us (12%)
  other arithmetic  4.11 us (3%)
    all_to_all x2, waiting for transfers between devices, exchange_rows(): moved = lax.all_to_all(wire, 'ep', split_axis=0, concat_axis=0, tiled=True)  80.3 us
    all_to_all x2, starting transfers between devices, exchange_rows(): moved = lax.all_to_all(wire, 'ep', split_axis=0, concat_axis=0, tiled=True)  18.7 us
    reshape x2, local copies, waits for them, and re-layouts, exchange_rows(): wire = rows.reshape(experts, total * width // (experts * lanes), lanes)  9.18 us
    reshape x2, local copies, waits for them, and re-layouts, exchange_rows(): return moved.reshape(total, width)  8.42 us
    dot_general x1, matrix products, hidden_of(): gate_part = jnp.dot(rows, gate_w, preferred_element_type=jnp.float32)  8.3 us
    dot_general x1, matrix products, hidden_of(): up_part = jnp.dot(rows, up_w, preferred_element_type=jnp.float32)  7.23 us
    dot_general x1, matrix products, per_device(): jnp.dot(hidden_full, jnp.concatenate([down_local, down_partner], axis=1),...  6.85 us
    dot_general x1, matrix products, per_device(): jnp.dot(jnp.concatenate([attention_out, partner_att], axis=0), out_weight...  4.04 us
  transfers between devices with their start and end apart: 7, of which 3 were waited for; matrix products, arithmetic and copies ran while one was open for 19% of the time, Pallas kernels for 0%

profile of v12, /device:TPU:0, one launch (start us, length us, event | category | flops | bytes accessed | tf_op | source)
XLA Modules:
  0.0 156.9 jit_solution(16235143118877698347)
XLA Ops:
  0.7 0.8 copy.26
  1.5 0.1 eq.48
  1.7 0.1 eq.44
  1.8 0.9 reduce-window.6
  2.7 0.2 slice_reduce_fusion
  3.0 0.1 fusion.43
  3.1 0.1 reduce_sum.57
  3.3 0.7 reduce_sum.58
  4.1 4.0 %fusion.29 = f32[128,1280]{1,0:T(8,128)S(1)} fusion(bf16[2560,1280]{1,0:T(8,128)(2,1)} %param.12, bf16[64,2560]{1,0:T(8,128)(2,1)S(1)} %collective-permute-done, bf16[64,2560]{1,0:T(8,128)(2,1)} %param.10), kind=kOutput, calls=%fused_computation.38 | convolution fusion | flops 840171520 | bytes 7864320 | tf_op jit(solution)/shard_map/dot_general | solution.py:53
  8.1 0.6 collective-permute-start.1
  8.7 1.0 collective-permute-done.1
  9.8 0.4 collective-permute-start.2
  10.2 0.3 select_reduce_fusion
  10.5 0.2 collective-permute-start.3
  10.7 0.2 fusion.25
  11.0 1.0 convolution_convert_fusion
  12.0 4.6 %reshape.61 = bf16[64,180,128]{2,1,0:T(8,128)(2,1)} reshape(bf16[576,2560]{1,0:T(8,128)(2,1)S(1)} %convolution_convert_fusion) | data formatting | bytes 5898240 | tf_op jit(solution)/shard_map/reshape | solution.py:24
  16.6 11.5 %all-to-all-start = ((bf16[64,180,128]{2,1,0:T(8,128)(2,1)}), bf16[64,180,128]{2,1,0:T(8,128)(2,1)S(1)}, u32[]{:S(2)}, u32[]{:S(2)}) async-start(bf16[64,180,128]{2,1,0:T(8,128)(2,1)} %reshape.61), calls=%async_computation | async-start | bytes 6029312 | tf_op jit(solution)/shard_map/all_to_all | solution.py:25
  28.1 0.3 collective-permute-start.4
  28.4 40.6 %all-to-all-done = bf16[64,180,128]{2,1,0:T(8,128)(2,1)S(1)} async-done(((bf16[64,180,128]{2,1,0:T(8,128)(2,1)}), bf16[64,180,128]{2,1,0:T(8,128)(2,1)S(1)}, u32[]{:S(2)}, u32[]{:S(2)}) %all-to-all-start) | async-done | bytes 2949152 | tf_op jit(solution)/shard_map/all_to_all | solution.py:25
  69.1 4.2 %reshape.62 = bf16[576,2560]{1,0:T(8,128)(2,1)} reshape(bf16[64,180,128]{2,1,0:T(8,128)(2,1)S(1)} %all-to-all-done) | data formatting | bytes 5898240 | tf_op jit(solution)/shard_map/reshape | solution.py:26
  73.3 8.3 %fusion = f32[576,1536]{1,0:T(8,128)S(1)} fusion(bf16[576,2560]{1,0:T(8,128)(2,1)} %reshape.62, bf16[2560,768]{1,0:T(8,128)(2,1)} %collective-permute-done.2, bf16[2560,768]{1,0:T(8,128)(2,1)} %bitcast), kind=kOutput, calls=%fused_computation | convolution fusion | flops 4545576960 | bytes 14352384 | tf_op jit(solution)/shard_map/dot_general | solution.py:88
  81.6 7.2 %multiply_convert_fusion = bf16[576,1536]{1,0:T(8,128)(2,1)S(1)} fusion(f32[576,1536]{1,0:T(8,128)S(1)} %fusion, bf16[576,2560]{1,0:T(8,128)(2,1)S(1)} %copy-done, bf16[2560,768]{1,0:T(8,128)(2,1)} %collective-permute-done.3, bf16[2560,768]{1,0:T(8,128)(2,1)S(1)} %bitcast.29), kind=kOutput, calls=%fused_computation.18 | convolution fusion | flops 4550885376 | bytes 16121856 | tf_op jit(solution)/shard_map/dot_general | solution.py:89
  89.0 6.8 %fusion.16 = bf16[576,2560]{1,0:T(8,128)(2,1)S(1)} fusion(bf16[1536,1280]{1,0:T(8,128)(2,1)} %collective-permute-done.4, bf16[1536,1280]{1,0:T(8,128)(2,1)S(1)} %bitcast.31, bf16[576,1536]{1,0:T(8,128)(2,1)S(1)} %multiply_convert_fusion, bf16[576,768]{1,0:T(8,128)(2,1)S(1)} %get-tuple-element.19, bf16[576,768]{1,0:T(8,128)(2,1)S(1)} %get-tuple-element.18, ...), kind=kOutput, calls=%fused_computation.16 | convolution fusion | flops 4551475200 | bytes 14352385 | tf_op jit(solution)/shard_map/dot_general | solution.py:99
  95.9 4.6 %reshape.63 = bf16[64,180,128]{2,1,0:T(8,128)(2,1)} reshape(bf16[576,2560]{1,0:T(8,128)(2,1)S(1)} %fusion.16) | data formatting | bytes 5898240 | tf_op jit(solution)/shard_map/reshape | solution.py:24
  100.4 7.2 %all-to-all-start.1 = ((bf16[64,180,128]{2,1,0:T(8,128)(2,1)}), bf16[64,180,128]{2,1,0:T(8,128)(2,1)S(1)}, u32[]{:S(2)}, u32[]{:S(2)}) async-start(bf16[64,180,128]{2,1,0:T(8,128)(2,1)} %reshape.63), calls=%async_computation.1 | async-start | bytes 6029312 | tf_op jit(solution)/shard_map/all_to_all | solution.py:25
  107.7 0.7 subtract_convert_fusion
  108.4 39.7 %all-to-all-done.1 = bf16[64,180,128]{2,1,0:T(8,128)(2,1)S(1)} async-done(((bf16[64,180,128]{2,1,0:T(8,128)(2,1)}), bf16[64,180,128]{2,1,0:T(8,128)(2,1)S(1)}, u32[]{:S(2)}, u32[]{:S(2)}) %all-to-all-start.1) | async-done | bytes 2949152 | tf_op jit(solution)/shard_map/all_to_all | solution.py:25
  148.0 4.2 %reshape.64 = bf16[576,2560]{1,0:T(8,128)(2,1)} reshape(bf16[64,180,128]{2,1,0:T(8,128)(2,1)S(1)} %all-to-all-done.1) | data formatting | bytes 5898240 | tf_op jit(solution)/shard_map/reshape | solution.py:26
  152.3 3.5 %fusion.12 = f32[64,2560]{1,0:T(8,128)S(1)} fusion(bf16[576,2560]{1,0:T(8,128)(2,1)} %reshape.64, bf16[64,576]{1,0:T(8,128)(2,1)S(1)} %copy-done.3, bf16[64,576]{1,0:T(8,128)(2,1)S(1)} %copy-done.4), kind=kOutput, calls=%fused_computation.12 | convolution fusion | flops 389578752 | bytes 3751936 | tf_op jit(solution)/shard_map/dot_general | solution.py:107
  155.8 0.2 fusion.22
  156.1 0.9 fusion.24
  (39 shorter events, 0.5 us)
Async XLA Ops:
  0.6 3.4 %collective-permute-start = (bf16[64,2560]{1,0:T(8,128)(2,1)}, bf16[64,2560]{1,0:T(8,128)(2,1)S(1)}, u32[]{:S(2)}, u32[]{:S(2)}) collective-permute-start(bf16[64,2560]{1,0:T(8,128)(2,1)} %param.10), channel_id=1, source_target_pairs={{0,1},{1,0},{2,3},{3,2},{4,5},{5,4},{6,7},{7,6},{8,9},{9,8},{10,11... | collective-permute-start | bytes 983048 | tf_op jit(solution)/shard_map/ppermute | solution.py:52
  4.0 4.7 %copy-start.5 = (s32[64,6]{0,1:T(8,128)S(1)}, s32[64,6]{0,1:T(8,128)}, u32[]{:S(2)}) copy-start(s32[64,6]{0,1:T(8,128)} %param.14) | copy-start | bytes 4612
  4.0 6.2 %copy-start.6 = (f32[64,6]{0,1:T(8,128)S(1)}, f32[64,6]{0,1:T(8,128)}, u32[]{:S(2)}) copy-start(f32[64,6]{0,1:T(8,128)} %param.15) | copy-start | bytes 4612
  4.0 6.7 %copy-start.2 = (bf16[64,2560]{1,0:T(8,128)(2,1)S(1)}, bf16[64,2560]{1,0:T(8,128)(2,1)}, u32[]{:S(2)}) copy-start(bf16[64,2560]{1,0:T(8,128)(2,1)} %param.11) | copy-start | bytes 983044
  4.0 6.9 %copy-start.7 = (f32[2560]{0:T(1024)S(1)}, f32[2560]{0:T(1024)}, u32[]{:S(2)}) copy-start(f32[2560]{0:T(1024)} %param.13) | copy-start | bytes 30724
  8.1 1.6 %collective-permute-start.1 = (bf16[64,1280]{1,0:T(8,128)(2,1)S(1)}, bf16[64,1280]{1,0:T(8,128)(2,1)S(1)}, u32[]{:S(2)}, u32[]{:S(2)}) collective-permute-start(bf16[64,1280]{1,0:T(8,128)(2,1)S(1)} %slice.44), channel_id=1, source_target_pairs={{0,1},{1,0},{2,3},{3,2},{4,5},{5,4},{6,7},{7,6},{8,9},{9,8},{10,11... | collective-permute-start | bytes 491528 | tf_op jit(solution)/shard_map/ppermute | solution.py:59
  9.8 63.5 %collective-permute-start.2 = (bf16[2560,768]{1,0:T(8,128)(2,1)}, bf16[2560,768]{1,0:T(8,128)(2,1)}, u32[]{:S(2)}, u32[]{:S(2)}) collective-permute-start(bf16[2560,768]{1,0:T(8,128)(2,1)} %bitcast), channel_id=1, source_target_pairs={{0,1},{1,0},{2,3},{3,2},{4,5},{5,4},{6,7},{7,6},{8,9},{9,8},{10,11... | collective-permute-start | bytes 11796488 | tf_op jit(solution)/shard_map/ppermute | solution.py:63
  10.5 71.1 %collective-permute-start.3 = (bf16[2560,768]{1,0:T(8,128)(2,1)}, bf16[2560,768]{1,0:T(8,128)(2,1)}, u32[]{:S(2)}, u32[]{:S(2)}) collective-permute-start(bf16[2560,768]{1,0:T(8,128)(2,1)} %bitcast.28), channel_id=1, source_target_pairs={{0,1},{1,0},{2,3},{3,2},{4,5},{5,4},{6,7},{7,6},{8,9},{9,8},{10,11... | collective-permute-start | bytes 11796488 | tf_op jit(solution)/shard_map/ppermute | solution.py:64
  16.6 52.5 %all-to-all-start = ((bf16[64,180,128]{2,1,0:T(8,128)(2,1)}), bf16[64,180,128]{2,1,0:T(8,128)(2,1)S(1)}, u32[]{:S(2)}, u32[]{:S(2)}) async-start(bf16[64,180,128]{2,1,0:T(8,128)(2,1)} %reshape.61), calls=%async_computation | async-start | bytes 6029312 | tf_op jit(solution)/shard_map/all_to_all | solution.py:25
  28.1 60.9 %collective-permute-start.4 = (bf16[1536,1280]{1,0:T(8,128)(2,1)}, bf16[1536,1280]{1,0:T(8,128)(2,1)}, u32[]{:S(2)}, u32[]{:S(2)}) collective-permute-start(bf16[1536,1280]{1,0:T(8,128)(2,1)} %bitcast.30), channel_id=1, source_target_pairs={{0,1},{1,0},{2,3},{3,2},{4,5},{5,4},{6,7},{7,6},{8,9},{9,8},{10,11... | collective-permute-start | bytes 11796488 | tf_op jit(solution)/shard_map/ppermute | solution.py:65
  73.3 8.3 %copy-start = (bf16[576,2560]{1,0:T(8,128)(2,1)S(1)}, bf16[576,2560]{1,0:T(8,128)(2,1)}, u32[]{:S(2)}) copy-start(bf16[576,2560]{1,0:T(8,128)(2,1)} %reshape.62) | copy-start | bytes 8847364
  73.3 8.3 %copy-start.9 = (bf16[1,2560,768]{2,1,0:T(8,128)(2,1)S(1)}, bf16[1,2560,768]{2,1,0:T(8,128)(2,1)}, u32[]{:S(2)}) copy-start(bf16[1,2560,768]{2,1,0:T(8,128)(2,1)} %param.17) | copy-start | bytes 11796484
  81.6 7.4 %copy-start.10 = (bf16[1,1536,1280]{2,1,0:T(8,128)(2,1)S(1)}, bf16[1,1536,1280]{2,1,0:T(8,128)(2,1)}, u32[]{:S(2)}) copy-start(bf16[1,1536,1280]{2,1,0:T(8,128)(2,1)} %param.18) | copy-start | bytes 11796484
  100.4 47.6 %all-to-all-start.1 = ((bf16[64,180,128]{2,1,0:T(8,128)(2,1)}), bf16[64,180,128]{2,1,0:T(8,128)(2,1)S(1)}, u32[]{:S(2)}, u32[]{:S(2)}) async-start(bf16[64,180,128]{2,1,0:T(8,128)(2,1)} %reshape.63), calls=%async_computation.1 | async-start | bytes 6029312 | tf_op jit(solution)/shard_map/all_to_all | solution.py:25
  108.4 43.9 %copy-start.3 = (bf16[64,576]{1,0:T(8,128)(2,1)S(1)}, bf16[64,576]{1,0:T(8,128)(2,1)}, u32[]{:S(2)}) copy-start(bf16[64,576]{1,0:T(8,128)(2,1)} %get-tuple-element.14) | copy-start | bytes 221188
  108.4 43.9 %copy-start.4 = (bf16[64,576]{1,0:T(8,128)(2,1)S(1)}, bf16[64,576]{1,0:T(8,128)(2,1)}, u32[]{:S(2)}) copy-start(bf16[64,576]{1,0:T(8,128)(2,1)} %get-tuple-element.15) | copy-start | bytes 221188
  152.3 3.8 %copy-start.8 = (f32[2560]{0:T(1024)S(1)}, f32[2560]{0:T(1024)}, u32[]{:S(2)}) copy-start(f32[2560]{0:T(1024)} %param.19) | copy-start | bytes 30724
  156.0 0.9 copy-start.1

commit v13 on v12

--- a/solution.py
+++ b/solution.py
@@ -57,12 +57,6 @@
     )
     cols_own, cols_partner = cols[:tok_rows], cols[tok_rows:]
     cols_in = lax.ppermute(cols_partner.astype(jnp.bfloat16), "dp", swap).astype(jnp.float32)
-    gate_send, up_send, down_send, cols_in = lax.optimization_barrier(
-        (gate_local, up_local, down_local, cols_in)
-    )
-    gate_partner = lax.ppermute(gate_send, "dp", swap)
-    up_partner = lax.ppermute(up_send, "dp", swap)
-    down_partner = lax.ppermute(down_send, "dp", swap)
     home_cols = jnp.where(
         me == 0,
         jnp.concatenate([cols_own, cols_in], axis=1),
@@ -80,6 +74,12 @@
     outgoing = lax.dot_general(
         placing, normed_in, (((0,), (0,)), ((), ())), preferred_element_type=jnp.float32
     ).astype(jnp.bfloat16)
+    gate_send, up_send, down_send, outgoing = lax.optimization_barrier(
+        (gate_local, up_local, down_local, outgoing)
+    )
+    gate_partner = lax.ppermute(gate_send, "dp", swap)
+    up_partner = lax.ppermute(up_send, "dp", swap)
+    down_partner = lax.ppermute(down_send, "dp", swap)
     own_rows = exchange_rows(outgoing, experts)
     me = lax.axis_index("dp")
     ff_half = gate_local.shape[1]

time: 157 us -> 159 us (1.013)
  no operation moved by 1% of the time
where the time goes in v13:
time: 159 us; the launch traced here: 158 us
  waiting for transfers between devices  81.1 us (51%)
  matrix products  32 us (20%)
  starting transfers between devices  20.3 us (13%)
  local copies, waits for them, and re-layouts  19.3 us (12%)
  other arithmetic  4.8 us (3%)
    all_to_all x2, waiting for transfers between devices, exchange_rows(): moved = lax.all_to_all(wire, 'ep', split_axis=0, concat_axis=0, tiled=True)  80.3 us
    all_to_all x2, starting transfers between devices, exchange_rows(): moved = lax.all_to_all(wire, 'ep', split_axis=0, concat_axis=0, tiled=True)  18.7 us
    reshape x2, local copies, waits for them, and re-layouts, exchange_rows(): wire = rows.reshape(experts, total * width // (experts * lanes), lanes)  9.16 us
    reshape x2, local copies, waits for them, and re-layouts, exchange_rows(): return moved.reshape(total, width)  8.42 us
    dot_general x1, matrix products, hidden_of(): up_part = jnp.dot(rows, up_w, preferred_element_type=jnp.float32)  8.41 us
    dot_general x1, matrix products, hidden_of(): gate_part = jnp.dot(rows, gate_w, preferred_element_type=jnp.float32)  8.3 us
    dot_general x1, matrix products, per_device(): jnp.dot(hidden_full, jnp.concatenate([down_local, down_partner], axis=1),...  6.85 us
    dot_general x1, matrix products, per_device(): jnp.dot(jnp.concatenate([attention_out, partner_att], axis=0), out_weight...  4.04 us
  transfers between devices with their start and end apart: 7, of which 3 were waited for; matrix products, arithmetic and copies ran while one was open for 19% of the time, Pallas kernels for 0%

profile of v13, /device:TPU:0, one launch (start us, length us, event | category | flops | bytes accessed | tf_op | source)
XLA Modules:
  0.0 158.4 jit_solution(7163317244891532446)
XLA Ops:
  0.7 0.8 copy.26
  1.5 0.1 eq.48
  1.6 0.1 eq.44
  1.8 0.9 reduce-window.6
  2.7 0.2 slice_reduce_fusion
  3.1 0.1 reduce_sum.57
  3.3 0.7 reduce_sum.58
  4.0 0.7 multiply_add_fusion
  4.7 4.0 %fusion.29 = f32[128,1280]{1,0:T(8,128)S(1)} fusion(bf16[2560,1280]{1,0:T(8,128)(2,1)} %param.12, bf16[64,2560]{1,0:T(8,128)(2,1)S(1)} %collective-permute-done, bf16[64,2560]{1,0:T(8,128)(2,1)} %param.10), kind=kOutput, calls=%fused_computation.38 | convolution fusion | flops 840171520 | bytes 7864320 | tf_op jit(solution)/shard_map/dot_general | solution.py:53
  8.8 0.6 collective-permute-start.1
  9.4 0.3 select_reduce_fusion
  9.7 0.7 collective-permute-done.1
  10.4 0.2 fusion.25
  10.7 1.0 convolution_convert_fusion
  11.7 0.4 collective-permute-start.2
  12.1 0.1 collective-permute-start.3
  12.3 4.6 %reshape.61 = bf16[64,180,128]{2,1,0:T(8,128)(2,1)} reshape(bf16[576,2560]{1,0:T(8,128)(2,1)S(1)} %convolution_convert_fusion) | data formatting | bytes 5898240 | tf_op jit(solution)/shard_map/reshape | solution.py:24
  16.9 11.5 %all-to-all-start = ((bf16[64,180,128]{2,1,0:T(8,128)(2,1)}), bf16[64,180,128]{2,1,0:T(8,128)(2,1)S(1)}, u32[]{:S(2)}, u32[]{:S(2)}) async-start(bf16[64,180,128]{2,1,0:T(8,128)(2,1)} %reshape.61), calls=%async_computation | async-start | bytes 6029312 | tf_op jit(solution)/shard_map/all_to_all | solution.py:25
  28.4 0.3 collective-permute-start.4
  28.7 40.6 %all-to-all-done = bf16[64,180,128]{2,1,0:T(8,128)(2,1)S(1)} async-done(((bf16[64,180,128]{2,1,0:T(8,128)(2,1)}), bf16[64,180,128]{2,1,0:T(8,128)(2,1)S(1)}, u32[]{:S(2)}, u32[]{:S(2)}) %all-to-all-start) | async-done | bytes 2949152 | tf_op jit(solution)/shard_map/all_to_all | solution.py:25
  69.3 4.2 %reshape.62 = bf16[576,2560]{1,0:T(8,128)(2,1)} reshape(bf16[64,180,128]{2,1,0:T(8,128)(2,1)S(1)} %all-to-all-done) | data formatting | bytes 5898240 | tf_op jit(solution)/shard_map/reshape | solution.py:26
  73.6 8.3 %fusion = f32[576,1536]{1,0:T(8,128)S(1)} fusion(bf16[576,2560]{1,0:T(8,128)(2,1)} %reshape.62, bf16[2560,768]{1,0:T(8,128)(2,1)} %collective-permute-done.2, bf16[2560,768]{1,0:T(8,128)(2,1)} %bitcast.1), kind=kOutput, calls=%fused_computation | convolution fusion | flops 4545576960 | bytes 14352384 | tf_op jit(solution)/shard_map/dot_general | solution.py:88
  81.9 8.4 %multiply_convert_fusion = bf16[576,1536]{1,0:T(8,128)(2,1)S(1)} fusion(f32[576,1536]{1,0:T(8,128)S(1)} %fusion, bf16[576,2560]{1,0:T(8,128)(2,1)S(1)} %copy-done, bf16[2560,768]{1,0:T(8,128)(2,1)} %collective-permute-done.3, bf16[2560,768]{1,0:T(8,128)(2,1)} %bitcast.2), kind=kOutput, calls=%fused_computation.18 | convolution fusion | flops 4550885376 | bytes 16121856 | tf_op jit(solution)/shard_map/dot_general | solution.py:89
  90.5 6.8 %fusion.16 = bf16[576,2560]{1,0:T(8,128)(2,1)S(1)} fusion(bf16[1536,1280]{1,0:T(8,128)(2,1)} %collective-permute-done.4, bf16[1536,1280]{1,0:T(8,128)(2,1)S(1)} %bitcast.29, bf16[576,1536]{1,0:T(8,128)(2,1)S(1)} %multiply_convert_fusion, bf16[576,768]{1,0:T(8,128)(2,1)S(1)} %get-tuple-element.19, bf16[576,768]{1,0:T(8,128)(2,1)S(1)} %get-tuple-element.18, ...), kind=kOutput, calls=%fused_computation.16 | convolution fusion | flops 4551475200 | bytes 14352385 | tf_op jit(solution)/shard_map/dot_general | solution.py:99
  97.3 4.6 %reshape.63 = bf16[64,180,128]{2,1,0:T(8,128)(2,1)} reshape(bf16[576,2560]{1,0:T(8,128)(2,1)S(1)} %fusion.16) | data formatting | bytes 5898240 | tf_op jit(solution)/shard_map/reshape | solution.py:24
  101.9 7.2 %all-to-all-start.1 = ((bf16[64,180,128]{2,1,0:T(8,128)(2,1)}), bf16[64,180,128]{2,1,0:T(8,128)(2,1)S(1)}, u32[]{:S(2)}, u32[]{:S(2)}) async-start(bf16[64,180,128]{2,1,0:T(8,128)(2,1)} %reshape.63), calls=%async_computation.1 | async-start | bytes 6029312 | tf_op jit(solution)/shard_map/all_to_all | solution.py:25
  109.1 0.7 subtract_convert_fusion
  109.8 39.7 %all-to-all-done.1 = bf16[64,180,128]{2,1,0:T(8,128)(2,1)S(1)} async-done(((bf16[64,180,128]{2,1,0:T(8,128)(2,1)}), bf16[64,180,128]{2,1,0:T(8,128)(2,1)S(1)}, u32[]{:S(2)}, u32[]{:S(2)}) %all-to-all-start.1) | async-done | bytes 2949152 | tf_op jit(solution)/shard_map/all_to_all | solution.py:25
  149.5 4.2 %reshape.64 = bf16[576,2560]{1,0:T(8,128)(2,1)} reshape(bf16[64,180,128]{2,1,0:T(8,128)(2,1)S(1)} %all-to-all-done.1) | data formatting | bytes 5898240 | tf_op jit(solution)/shard_map/reshape | solution.py:26
  153.7 3.5 %fusion.12 = f32[64,2560]{1,0:T(8,128)S(1)} fusion(bf16[576,2560]{1,0:T(8,128)(2,1)} %reshape.64, bf16[64,576]{1,0:T(8,128)(2,1)S(1)} %copy-done.3, bf16[64,576]{1,0:T(8,128)(2,1)S(1)} %copy-done.4), kind=kOutput, calls=%fused_computation.12 | convolution fusion | flops 389578752 | bytes 3751936 | tf_op jit(solution)/shard_map/dot_general | solution.py:107
  157.2 0.2 fusion.22
  157.5 0.9 fusion.24
  (35 shorter events, 0.6 us)
Async XLA Ops:
  0.6 4.1 %collective-permute-start = (bf16[64,2560]{1,0:T(8,128)(2,1)}, bf16[64,2560]{1,0:T(8,128)(2,1)S(1)}, u32[]{:S(2)}, u32[]{:S(2)}) collective-permute-start(bf16[64,2560]{1,0:T(8,128)(2,1)} %param.10), channel_id=1, source_target_pairs={{0,1},{1,0},{2,3},{3,2},{4,5},{5,4},{6,7},{7,6},{8,9},{9,8},{10,11... | collective-permute-start | bytes 983048 | tf_op jit(solution)/shard_map/ppermute | solution.py:52
  4.7 4.7 %copy-start.5 = (f32[64,6]{0,1:T(8,128)S(1)}, f32[64,6]{0,1:T(8,128)}, u32[]{:S(2)}) copy-start(f32[64,6]{0,1:T(8,128)} %param.15) | copy-start | bytes 4612
  4.7 5.7 %copy-start.2 = (bf16[64,2560]{1,0:T(8,128)(2,1)S(1)}, bf16[64,2560]{1,0:T(8,128)(2,1)}, u32[]{:S(2)}) copy-start(bf16[64,2560]{1,0:T(8,128)(2,1)} %param.11) | copy-start | bytes 983044
  4.7 6.0 %copy-start.6 = (f32[2560]{0:T(1024)S(1)}, f32[2560]{0:T(1024)}, u32[]{:S(2)}) copy-start(f32[2560]{0:T(1024)} %param.13) | copy-start | bytes 30724
  8.8 1.6 %collective-permute-start.1 = (bf16[64,1280]{1,0:T(8,128)(2,1)S(1)}, bf16[64,1280]{1,0:T(8,128)(2,1)S(1)}, u32[]{:S(2)}, u32[]{:S(2)}) collective-permute-start(bf16[64,1280]{1,0:T(8,128)(2,1)S(1)} %slice.44), channel_id=1, source_target_pairs={{0,1},{1,0},{2,3},{3,2},{4,5},{5,4},{6,7},{7,6},{8,9},{9,8},{10,11... | collective-permute-start | bytes 491528 | tf_op jit(solution)/shard_map/ppermute | solution.py:59
  11.7 61.9 %collective-permute-start.2 = (bf16[2560,768]{1,0:T(8,128)(2,1)}, bf16[2560,768]{1,0:T(8,128)(2,1)}, u32[]{:S(2)}, u32[]{:S(2)}) collective-permute-start(bf16[2560,768]{1,0:T(8,128)(2,1)} %bitcast.1), channel_id=1, source_target_pairs={{0,1},{1,0},{2,3},{3,2},{4,5},{5,4},{6,7},{7,6},{8,9},{9,8},{10,11... | collective-permute-start | bytes 11796488 | tf_op jit(solution)/shard_map/ppermute | solution.py:80
  12.1 69.7 %collective-permute-start.3 = (bf16[2560,768]{1,0:T(8,128)(2,1)}, bf16[2560,768]{1,0:T(8,128)(2,1)}, u32[]{:S(2)}, u32[]{:S(2)}) collective-permute-start(bf16[2560,768]{1,0:T(8,128)(2,1)} %bitcast.2), channel_id=1, source_target_pairs={{0,1},{1,0},{2,3},{3,2},{4,5},{5,4},{6,7},{7,6},{8,9},{9,8},{10,11... | collective-permute-start | bytes 11796488 | tf_op jit(solution)/shard_map/ppermute | solution.py:81
  16.9 52.5 %all-to-all-start = ((bf16[64,180,128]{2,1,0:T(8,128)(2,1)}), bf16[64,180,128]{2,1,0:T(8,128)(2,1)S(1)}, u32[]{:S(2)}, u32[]{:S(2)}) async-start(bf16[64,180,128]{2,1,0:T(8,128)(2,1)} %reshape.61), calls=%async_computation | async-start | bytes 6029312 | tf_op jit(solution)/shard_map/all_to_all | solution.py:25
  28.4 62.1 %collective-permute-start.4 = (bf16[1536,1280]{1,0:T(8,128)(2,1)}, bf16[1536,1280]{1,0:T(8,128)(2,1)}, u32[]{:S(2)}, u32[]{:S(2)}) collective-permute-start(bf16[1536,1280]{1,0:T(8,128)(2,1)} %bitcast.28), channel_id=1, source_target_pairs={{0,1},{1,0},{2,3},{3,2},{4,5},{5,4},{6,7},{7,6},{8,9},{9,8},{10,11... | collective-permute-start | bytes 11796488 | tf_op jit(solution)/shard_map/ppermute | solution.py:82
  73.6 8.3 %copy-start = (bf16[576,2560]{1,0:T(8,128)(2,1)S(1)}, bf16[576,2560]{1,0:T(8,128)(2,1)}, u32[]{:S(2)}) copy-start(bf16[576,2560]{1,0:T(8,128)(2,1)} %reshape.62) | copy-start | bytes 8847364
  81.9 8.6 %copy-start.8 = (bf16[1,1536,1280]{2,1,0:T(8,128)(2,1)S(1)}, bf16[1,1536,1280]{2,1,0:T(8,128)(2,1)}, u32[]{:S(2)}) copy-start(bf16[1,1536,1280]{2,1,0:T(8,128)(2,1)} %param.18) | copy-start | bytes 11796484
  101.9 47.6 %all-to-all-start.1 = ((bf16[64,180,128]{2,1,0:T(8,128)(2,1)}), bf16[64,180,128]{2,1,0:T(8,128)(2,1)S(1)}, u32[]{:S(2)}, u32[]{:S(2)}) async-start(bf16[64,180,128]{2,1,0:T(8,128)(2,1)} %reshape.63), calls=%async_computation.1 | async-start | bytes 6029312 | tf_op jit(solution)/shard_map/all_to_all | solution.py:25
  109.8 43.9 %copy-start.3 = (bf16[64,576]{1,0:T(8,128)(2,1)S(1)}, bf16[64,576]{1,0:T(8,128)(2,1)}, u32[]{:S(2)}) copy-start(bf16[64,576]{1,0:T(8,128)(2,1)} %get-tuple-element.14) | copy-start | bytes 221188
  109.8 43.9 %copy-start.4 = (bf16[64,576]{1,0:T(8,128)(2,1)S(1)}, bf16[64,576]{1,0:T(8,128)(2,1)}, u32[]{:S(2)}) copy-start(bf16[64,576]{1,0:T(8,128)(2,1)} %get-tuple-element.15) | copy-start | bytes 221188
  153.7 3.8 %copy-start.7 = (f32[2560]{0:T(1024)S(1)}, f32[2560]{0:T(1024)}, u32[]{:S(2)}) copy-start(f32[2560]{0:T(1024)} %param.19) | copy-start | bytes 30724
  157.5 0.9 copy-start.1
